TPU v7x, 32 devices: a whole 2x2x4 slice. The times are simulated.
32 devices in a mesh: section: 2 (over x), dp: 4 (over z), mp: 4 (over y, core).
Axes of the slice: x: 2, y: 2, z: 4, core: 2. Of those that a mesh axis runs over, the one named last changes fastest.
Arguments:
- queries: bfloat16 [2, 4, 640, 4096], P('section', 'dp', None, 'mp')
- keys: bfloat16 [2, 4, 640, 4096], P('section', 'dp', None, 'mp')
- values: bfloat16 [2, 4, 640, 4096], P('section', 'dp', None, 'mp'), may hold values from -6 to 6
- grad_out: bfloat16 [2, 4, 640, 4096], P('section', 'dp', None, 'mp'), may hold values from -6 to 6
- positions: int32 [2, 4, 640], P('section', 'dp'), may hold values from 0 to 319, as said below
Outputs:
- received: bfloat16 [2, 4, 3, 640, 4096], P('section', 'dp', None, 'mp')
- bias_grad: float32 [2, 3, 4096], P('section')
Inputs may be any that keep to these rules, and one draw needn't show every extreme that they name: `positions`: along each sequence a position is 0 or one more than the position before it; the first is 0; a document starts at token 320, and none is longer than 320 tokens.
All inputs are finite; a program needn't handle non-finite values.
Results may differ from a plain program's by a relative error of at most 0.0065.
Values may be sent and summed in bfloat16 or wider, within the bound.
No kernel may reach another device: no remote copies, remote signals or barrier semaphores. Data moves between devices by JAX's collectives and lax.ppermute only.
A program may use at most 64 MiB of HBM per device.

v0:
```python
import math

import jax
import jax.numpy as jnp
from jax import lax
from jax.sharding import PartitionSpec as P

HEAD_DIM = 128


def from_behind(value, axis, steps):
    count = lax.axis_size(axis)
    initial, last = (max(0, -steps), min(count, count - steps))
    return lax.ppermute(value, axis, [(source, source + steps) for source in range(initial, last)])


def per_device(queries, keys, values, grad_out, positions):
    query_rows = queries[0, 0]
    key_rows = keys[0, 0]
    value_rows = values[0, 0]
    grad_rows = grad_out[0, 0]
    token_positions = positions[0, 0]
    length = query_rows.shape[0]
    columns = query_rows.shape[1]
    head_count = columns // HEAD_DIM
    scaling = 1.0 / math.sqrt(HEAD_DIM)
    indices = jnp.arange(length, dtype=jnp.int32)
    allowed = (indices[None, :] <= indices[:, None]) & (
        indices[None, :] >= (indices - token_positions)[:, None]
    )

    def one_head(head, results):
        offset = head * HEAD_DIM
        query_part = lax.dynamic_slice_in_dim(query_rows, offset, HEAD_DIM, 1)
        key_part = lax.dynamic_slice_in_dim(key_rows, offset, HEAD_DIM, 1)
        value_part = lax.dynamic_slice_in_dim(value_rows, offset, HEAD_DIM, 1)
        grad_part = lax.dynamic_slice_in_dim(grad_rows, offset, HEAD_DIM, 1)
        scores = (
            jnp.einsum("qd,kd->qk", query_part, key_part, preferred_element_type=jnp.float32)
            * scaling
        )
        scores = jnp.where(allowed, scores, jnp.float32(-1e30))
        highest = jnp.max(scores, axis=-1, keepdims=True)
        expont = jnp.exp(scores - highest)
        attn = expont / jnp.sum(expont, axis=-1, keepdims=True)
        attn_low = attn.astype(jnp.bfloat16)
        grad_v = jnp.einsum("qk,qd->kd", attn_low, grad_part, preferred_element_type=jnp.float32)
        grad_attn = jnp.einsum(
            "qd,kd->qk", grad_part, value_part, preferred_element_type=jnp.float32
        )
        delta = jnp.sum(attn * grad_attn, axis=-1, keepdims=True)
        grad_scores = (attn * (grad_attn - delta) * scaling).astype(jnp.bfloat16)
        grad_q = jnp.einsum("qk,kd->qd", grad_scores, key_part, preferred_element_type=jnp.float32)
        grad_k = jnp.einsum(
            "qk,qd->kd", grad_scores, query_part, preferred_element_type=jnp.float32
        )
        blocks = jnp.stack([grad_q, grad_k, grad_v]).astype(jnp.bfloat16)
        return lax.dynamic_update_slice_in_dim(results, blocks, offset, 2)

    stacked = lax.fori_loop(0, head_count, one_head, jnp.zeros((3, length, columns), jnp.bfloat16))
    arrived = from_behind(stacked, "section", -1)
    received = lax.all_to_all(arrived, "mp", split_axis=1, concat_axis=2, tiled=True)
    partial_sums = jnp.sum(received.astype(jnp.float32), axis=1)
    totals = lax.psum(partial_sums, ("dp", "mp"))
    bias_grad = totals / math.sqrt(lax.axis_size("dp") * length)
    return (received[None, None], bias_grad[None])


def solution(mesh):
    return jax.shard_map(
        per_device,
        mesh=mesh,
        in_specs=(
            P("section", "dp", None, "mp"),
            P("section", "dp", None, "mp"),
            P("section", "dp", None, "mp"),
            P("section", "dp", None, "mp"),
            P("section", "dp", None),
        ),
        out_specs=(P("section", "dp", None, "mp", None), P("section", None, None)),
        check_vma=False,
    )
```

profile of v0, /device:TPU:0, one launch (start us, length us, event | category | flops | bytes accessed | tf_op | source)
XLA Modules:
  0.0 304.0 jit_solution(6090517974584673321)
XLA Ops:
  1.3 2.4 broadcast_in_dim.30
  3.8 67.3 %while.14 = (s32[]{:T(128)}, bf16[3,640,1024]{2,1,0:T(8,128)(2,1)}, bf16[640,1024]{1,0:T(8,128)(2,1)}, bf16[640,1024]{1,0:T(8,128)(2,1)}, bf16[640,1024]{1,0:T(8...) while((s32[]{:T(128)}, bf16[3,640,1024]{2,1,0:T(8,128)(2,1)}, ...), condition=%wide.region_4.5_spmd.clone, body=%wide.region_0.4_spmd.clone.sunk | while | flops 534608000 | bytes 16580779 | solution.py:60
  3.8 1.4 fusion.43
  6.8 1.5 multiply_reduce_fusion.2
  8.7 1.3 fusion.47
  12.2 1.4 fusion.43
  15.2 1.5 multiply_reduce_fusion.2
  17.1 1.3 fusion.47
  20.6 1.4 fusion.43
  23.6 1.5 multiply_reduce_fusion.2
  25.5 1.3 fusion.47
  29.0 1.4 fusion.43
  32.0 1.5 multiply_reduce_fusion.2
  34.0 1.3 fusion.47
  37.4 1.4 fusion.43
  40.5 1.5 multiply_reduce_fusion.2
  42.4 1.3 fusion.47
  45.8 1.4 fusion.43
  48.9 1.5 multiply_reduce_fusion.2
  50.8 1.3 fusion.47
  54.2 1.4 fusion.43
  57.3 1.5 multiply_reduce_fusion.2
  59.2 1.3 fusion.47
  62.7 1.4 fusion.43
  65.7 1.5 multiply_reduce_fusion.2
  72.4 88.1 %collective-permute-done = bf16[3,640,1024]{2,1,0:T(8,128)(2,1)S(1)} collective-permute-done((bf16[3,640,1024]{2,1,0:T(8,128)(2,1)}, bf16[3,640,1024]{2,1,0:T(8,128)(2,1)S(1)}, u32[]{:S(2)}, u32[]{:S(2)}) %collective-permute-start) | collective-permute-done | bytes 3932192 | tf_op jit(solution)/shard_map/ppermute | solution.py:14
  160.5 3.4 %copy.10 = bf16[3,640,1024]{2,0,1:T(4,128)(2,1)S(1)} copy(bf16[3,640,1024]{2,1,0:T(8,128)(2,1)S(1)} %collective-permute-done) | data formatting | bytes 7864320 | tf_op jit(solution)/shard_map/ppermute | solution.py:14
  163.9 62.8 %all_to_all.15 = bf16[3,640,1024]{2,0,1:T(4,128)(2,1)S(1)} all-to-all(bf16[3,640,1024]{2,0,1:T(4,128)(2,1)S(1)} %copy.10), channel_id=1, replica_groups=mesh['section'=2,'dp'=4,'mp'=4] {'mp'}, dimensions={1} | all-to-all | bytes 7864320 | tf_op jit(solution)/shard_map/all_to_all | solution.py:62
  226.7 2.0 convert_reduce_fusion
  228.7 5.6 %copy.11 = bf16[3,160,4,1024]{3,2,1,0:T(4,128)(2,1)} copy(bf16[3,160,4,1024]{3,0,1,2:T(4,128)(2,1)S(1)} %bitcast.27) | data formatting | bytes 7864320 | tf_op jit(solution)/shard_map/all_to_all | solution.py:62
  234.3 8.6 %broadcast_in_dim.31 = bf16[1,1,3,160,4096]{4,3,2,1,0:T(8,128)(2,1)} reshape(bf16[3,160,4,1024]{3,2,1,0:T(4,128)(2,1)} %copy.11) | data formatting | bytes 7864320 | tf_op jit(solution)/shard_map/broadcast_in_dim | solution.py:66
  242.9 60.4 %psum.7 = f32[3,4096]{1,0:T(4,128)S(1)} all-reduce(f32[3,4096]{1,0:T(4,128)S(1)} %bitcast.30), channel_id=1, replica_groups=mesh['section'=2,'dp'=4,'mp'=4] {'dp','mp'}, use_global_device_ids=true, to_apply=%region_6.7 | all-reduce | flops 12288 | bytes 98304 | tf_op jit(solution)/shard_map/psum | solution.py:64
  (46 shorter events, 37.1 us)
Async XLA Ops:
  71.1 89.4 %collective-permute-start = (bf16[3,640,1024]{2,1,0:T(8,128)(2,1)}, bf16[3,640,1024]{2,1,0:T(8,128)(2,1)S(1)}, u32[]{:S(2)}, u32[]{:S(2)}) collective-permute-start(bf16[3,640,1024]{2,1,0:T(8,128)(2,1)} %get-tuple-element.126), channel_id=1, source_target_pairs={{16,0},{17,1},{18,2},{19,3},{20,4},{21,5},{22,6},{23,7},{24,8},{25... | collective-permute-start | bytes 11796488 | tf_op jit(solution)/shard_map/ppermute | solution.py:14
where the time goes:
time: 305 us; the launch traced here: 304 us
  blocking collectives  123 us (40%)
  waiting for transfers between devices  88.1 us (29%)
  matrix products  54.9 us (18%)
  local copies, waits for them, and re-layouts  20.6 us (7%)
  other arithmetic  14.9 us (5%)
    ppermute x1, waiting for transfers between devices, from_behind(): lax.ppermute(value, axis, [(source, source + steps) for source in range(i...  88.1 us
    all_to_all x1, blocking collectives, per_device(): lax.all_to_all(arrived, 'mp', split_axis=1, concat_axis=2, tiled=True)  62.8 us
    psum x1, blocking collectives, per_device(): totals = lax.psum(partial_sums, ('dp', 'mp'))  60.4 us
    dot_general x8, matrix products, one_head(): jnp.einsum('qd,kd->qk', grad_part, value_part, preferred_element_type=jnp...  11.8 us
    dot_general x8, matrix products, one_head(): jnp.einsum('qd,kd->qk', query_part, key_part, preferred_element_type=jnp....  11.5 us
    dot_general x8, matrix products, one_head(): jnp.einsum('qk,kd->qd', grad_scores, key_part, preferred_element_type=jnp...  10.6 us
    dot_general x8, matrix products, one_head(): jnp.einsum('qk,qd->kd', attn_low, grad_part, preferred_element_type=jnp.f...  10.5 us
    dot_general x8, matrix products, one_head(): jnp.einsum('qk,qd->kd', grad_scores, query_part, preferred_element_type=j...  10.4 us
  transfers between devices with their start and end apart: 1, of which 1 were waited for; matrix products, arithmetic and copies ran while one was open for 0% of the time, Pallas kernels for 0%

commit v1 on v0

v1 whole, which is shorter than its diff:
```python
import math

import jax
import jax.numpy as jnp
from jax import lax
from jax.sharding import PartitionSpec as P

HEAD_DIM = 128
CHUNK_HEADS = 2


def chunk_grads(query_rows, key_rows, value_rows, grad_rows, allowed, halves):
    length, width = query_rows.shape
    heads = width // HEAD_DIM
    block = length // halves
    scaling = 1.0 / math.sqrt(HEAD_DIM)

    def split(rows):
        return rows.reshape(halves, block, heads, HEAD_DIM)

    q, k, v, g = split(query_rows), split(key_rows), split(value_rows), split(grad_rows)
    scores = jnp.einsum("bqhd,bkhd->bhqk", q, k, preferred_element_type=jnp.float32) * scaling
    scores = jnp.where(allowed[:, None], scores, jnp.float32(-1e30))
    highest = jnp.max(scores, axis=-1, keepdims=True)
    expont = jnp.exp(scores - highest)
    attn = expont / jnp.sum(expont, axis=-1, keepdims=True)
    attn_low = attn.astype(jnp.bfloat16)
    grad_v = jnp.einsum("bhqk,bqhd->bkhd", attn_low, g, preferred_element_type=jnp.float32)
    grad_attn = jnp.einsum("bqhd,bkhd->bhqk", g, v, preferred_element_type=jnp.float32)
    delta = jnp.sum(attn * grad_attn, axis=-1, keepdims=True)
    grad_scores = (attn * (grad_attn - delta) * scaling).astype(jnp.bfloat16)
    grad_q = jnp.einsum("bhqk,bkhd->bqhd", grad_scores, k, preferred_element_type=jnp.float32)
    grad_k = jnp.einsum("bhqk,bqhd->bkhd", grad_scores, q, preferred_element_type=jnp.float32)
    blocks = jnp.stack([grad_q, grad_k, grad_v]).astype(jnp.bfloat16)
    return blocks.reshape(3, length, width)


def per_device(queries, keys, values, grad_out, positions):
    query_rows = queries[0, 0]
    key_rows = keys[0, 0]
    value_rows = values[0, 0]
    grad_rows = grad_out[0, 0]
    token_positions = positions[0, 0]
    length, columns = query_rows.shape
    sections = lax.axis_size("section")
    parts = lax.axis_size("mp")
    replicas = lax.axis_size("dp")
    part = lax.axis_index("mp")
    rows = length // parts
    halves = 2
    block = length // halves

    local = jnp.arange(block, dtype=jnp.int32)
    pos = token_positions.reshape(halves, block)
    allowed = (local[None, None, :] <= local[None, :, None]) & (
        local[None, None, :] >= (local[None, :] - pos)[:, :, None]
    )

    def pairs(shift):
        return [
            ((s + 1) * parts + m, s * parts + (m + shift) % parts)
            for s in range(sections - 1)
            for m in range(parts)
        ]

    width = CHUNK_HEADS * HEAD_DIM
    chunk_count = columns // width
    arrived = [[None] * chunk_count for _ in range(parts)]
    sums = []
    for c in range(chunk_count):
        cols = slice(c * width, (c + 1) * width)
        grads = chunk_grads(
            query_rows[:, cols], key_rows[:, cols], value_rows[:, cols], grad_rows[:, cols], allowed, halves
        )
        sums.append(jnp.sum(grads.astype(jnp.float32), axis=1))
        for shift in range(parts):
            target = (part + shift) % parts
            piece = lax.dynamic_slice_in_dim(grads, target * rows, rows, 1)
            arrived[shift][c] = lax.ppermute(piece, ("section", "mp"), pairs(shift))

    own = jnp.concatenate(sums, axis=1)
    slots = lax.dynamic_update_slice_in_dim(
        jnp.zeros((3, columns * parts), jnp.float32), own, part * columns, 1
    )
    totals = lax.psum(slots, ("dp", "mp"))
    totals = lax.ppermute(totals, "section", [(s + 1, s) for s in range(sections - 1)])
    bias_grad = totals / math.sqrt(replicas * length)

    received = jnp.zeros((3, rows, columns * parts), jnp.bfloat16)
    for shift in range(parts):
        source = (part - shift) % parts
        piece = jnp.concatenate(arrived[shift], axis=2)
        received = lax.dynamic_update_slice_in_dim(received, piece, source * columns, 2)
    return (received[None, None], bias_grad[None])


def solution(mesh):
    return jax.shard_map(
        per_device,
        mesh=mesh,
        in_specs=(
            P("section", "dp", None, "mp"),
            P("section", "dp", None, "mp"),
            P("section", "dp", None, "mp"),
            P("section", "dp", None, "mp"),
            P("section", "dp", None),
        ),
        out_specs=(P("section", "dp", None, "mp", None), P("section", None, None)),
        check_vma=False,
    )
```

time: 305 us -> 253 us (0.83); the launches traced: 304 us -> 249 us
  blocking collectives: 123 us -> 63.6 us
  waiting for transfers between devices: 88.1 us -> 55 us
  local copies, waits for them, and re-layouts: 20.6 us -> 47.7 us
  starting transfers between devices: 1.28 us -> 22.2 us
  other arithmetic: 14.9 us -> 3.64 us
    all_to_all x1 -> x0, blocking collectives: 62.8 us -> none  [per_device(): lax.all_to_all(arrived, 'mp', split_axis=1, concat_axis=2, tiled=True)]
    ppermute x1 -> x17, waiting for transfers between devices: 88.1 us -> 55 us  [the longest x16 55 us: per_device(): arrived[shift][c] = lax.ppermute(piece, ('section', 'mp'), pairs(shift))]
    ppermute x1 -> x17, starting transfers between devices: 1.28 us -> 22.2 us  [the longest x16 20.9 us: per_device(): arrived[shift][c] = lax.ppermute(piece, ('section', 'mp'), pairs(shift))]
    another operation x0 -> x17, local copies, waits for them, and re-layouts: none -> 12.4 us  [the longest x16 12.4 us: chunk_grads(): blocks = jnp.stack([grad_q, grad_k, grad_v]).astype(jnp.bfloat16)]
    transpose x0 -> x12, local copies, waits for them, and re-layouts: none -> 11.6 us  [the longest x4 4.73 us: chunk_grads(): jnp.einsum('bhqk,bqhd->bkhd', attn_low, g, preferred_element_type=jnp.flo...]
    sub x0 -> x4, matrix products: none -> 9.71 us  [chunk_grads(): expont = jnp.exp(scores - highest)]
    dot_general x40 -> x16, matrix products: 54.9 us -> 45.4 us  [the longest x4 15.1 us: chunk_grads(): jnp.einsum('bhqk,bkhd->bqhd', grad_scores, k, preferred_element_type=jnp....]
    broadcast_in_dim x2, local copies, waits for them, and re-layouts: 9.26 us -> 1.12 us  [per_device(): return (received[None, None], bias_grad[None])]
  transfers between devices with their start and end apart: 1 -> 17, of which waited for: 1 -> 13; matrix products, arithmetic and copies ran while one was open for 0% -> 2% of each run, Pallas kernels for 0% -> 0%
where the time goes in v1:
time: 253 us; the launch traced here: 249 us
  blocking collectives  63.6 us (25%)
  matrix products  55.1 us (22%)
  waiting for transfers between devices  55 us (22%)
  local copies, waits for them, and re-layouts  47.7 us (19%)
  starting transfers between devices  22.2 us (9%)
  other arithmetic  3.64 us (1%)
    psum x1, blocking collectives, per_device(): totals = lax.psum(slots, ('dp', 'mp'))  63.6 us
    ppermute x16, waiting for transfers between devices, per_device(): arrived[shift][c] = lax.ppermute(piece, ('section', 'mp'), pairs(shift))  55 us
    ppermute x16, starting transfers between devices, per_device(): arrived[shift][c] = lax.ppermute(piece, ('section', 'mp'), pairs(shift))  20.9 us
    dot_general x4, matrix products, chunk_grads(): jnp.einsum('bhqk,bkhd->bqhd', grad_scores, k, preferred_element_type=jnp....  15.1 us
    dot_general x4, matrix products, chunk_grads(): jnp.einsum('bhqk,bqhd->bkhd', grad_scores, q, preferred_element_type=jnp....  14.5 us
    another operation x16, local copies, waits for them, and re-layouts, chunk_grads(): blocks = jnp.stack([grad_q, grad_k, grad_v]).astype(jnp.bfloat16)  12.4 us
    dot_general x4, matrix products, chunk_grads(): jnp.einsum('bhqk,bqhd->bkhd', attn_low, g, preferred_element_type=jnp.flo...  11 us
    sub x4, matrix products, chunk_grads(): expont = jnp.exp(scores - highest)  9.71 us
  transfers between devices with their start and end apart: 17, of which 13 were waited for; matrix products, arithmetic and copies ran while one was open for 2% of the time, Pallas kernels for 0%

profile of v1, /device:TPU:0, one launch (start us, length us, event | category | flops | bytes accessed | tf_op | source)
XLA Modules:
  0.0 248.7 jit_solution(15631880437137905530)
XLA Ops:
  0.7 2.3 fusion.237
  5.7 2.2 fusion.239
  12.1 3.2 %fusion.256 = (f32[2,2,320]{2,1,0:T(2,128)S(1)}, f32[2,2,320,320]{2,3,1,0:T(8,128)}) fusion(pred[2,320,320]{1,2,0:T(8,128)(4,1)S(1)} %fusion.124, bf16[2,320,2,128]{3,2,1,0:T(2,128)(2,1)} %reshape.143, bf16[2,320,2,128]{3,2,1,0:T(2,128)(2,1)} %reshape.142), kind=kOutput, calls=%fused_computation.205 | convolution fusion | flops 106496320 | bytes 2503680 | tf_op jit(solution)/shard_map/sub | solution.py:25
  15.3 3.8 %fusion.75 = bf16[2,320,2,128]{3,1,2,0:T(8,128)(2,1)} fusion(f32[2,2,320,320]{2,3,1,0:T(8,128)S(1)} %fusion.135, bf16[2,320,2,128]{3,2,1,0:T(2,128)(2,1)} %reshape.143, f32[2,2,320,320]{2,3,1,0:T(8,128)} %get-tuple-element.41, f32[2,2,320]{2,1,0:T(2,128)S(1)} %get-tuple-element.40), kind=kOutput, calls=%fused_computation.57 | convolution fusion | flops 107890240 | bytes 3937280 | tf_op jit(solution)/shard_map/bhqk,bkhd->bqhd/dot_general | solution.py:32
  19.0 3.6 %fusion.72 = bf16[2,320,2,128]{3,1,2,0:T(8,128)(2,1)} fusion(f32[2,2,320,320]{2,3,1,0:T(8,128)S(1)} %fusion.135, bf16[2,320,2,128]{3,2,1,0:T(2,128)(2,1)} %reshape.142, f32[2,2,320,320]{2,3,1,0:T(8,128)} %get-tuple-element.41, f32[2,2,320]{2,1,0:T(2,128)S(1)} %get-tuple-element.40), kind=kOutput, calls=%fused_computation.56 | convolution fusion | flops 107890240 | bytes 3937280 | tf_op jit(solution)/shard_map/bhqk,bqhd->bkhd/dot_general | solution.py:33
  22.7 2.8 %fusion.96 = bf16[2,320,2,128]{3,1,2,0:T(8,128)(2,1)} fusion(bf16[2,320,2,128]{3,2,1,0:T(2,128)(2,1)} %reshape.144, f32[2,2,320,320]{2,3,1,0:T(8,128)} %get-tuple-element.41, f32[2,2,320]{2,1,0:T(2,128)S(1)} %get-tuple-element.40), kind=kOutput, calls=%fused_computation.64 | convolution fusion | flops 105840640 | bytes 2298880 | tf_op jit(solution)/shard_map/bhqk,bqhd->bkhd/dot_general | solution.py:28
  27.3 2.1 fusion.251
  30.9 3.8 %fusion.81 = bf16[2,320,2,128]{3,1,2,0:T(8,128)(2,1)} fusion(f32[2,2,320,320]{2,3,1,0:T(8,128)S(1)} %fusion.133, bf16[2,320,2,128]{3,2,1,0:T(2,128)(2,1)} %copy-done.22, f32[2,2,320,320]{2,3,1,0:T(8,128)} %get-tuple-element.39, f32[2,2,320]{2,1,0:T(2,128)S(1)} %get-tuple-element.38), kind=kOutput, calls=%fused_computation.59 | convolution fusion | flops 107890240 | bytes 3937280 | tf_op jit(solution)/shard_map/bhqk,bkhd->bqhd/dot_general | solution.py:32
  34.7 3.6 %fusion.78 = bf16[2,320,2,128]{3,1,2,0:T(8,128)(2,1)} fusion(f32[2,2,320,320]{2,3,1,0:T(8,128)S(1)} %fusion.133, bf16[2,320,2,128]{3,2,1,0:T(2,128)(2,1)} %copy-done.20, f32[2,2,320,320]{2,3,1,0:T(8,128)} %get-tuple-element.39, f32[2,2,320]{2,1,0:T(2,128)S(1)} %get-tuple-element.38), kind=kOutput, calls=%fused_computation.58 | convolution fusion | flops 107890240 | bytes 3937280 | tf_op jit(solution)/shard_map/bhqk,bqhd->bkhd/dot_general | solution.py:33
  38.3 2.8 %fusion.97 = bf16[2,320,2,128]{3,1,2,0:T(8,128)(2,1)} fusion(bf16[2,320,2,128]{3,2,1,0:T(2,128)(2,1)} %reshape.148, f32[2,2,320,320]{2,3,1,0:T(8,128)} %get-tuple-element.39, f32[2,2,320]{2,1,0:T(2,128)S(1)} %get-tuple-element.38), kind=kOutput, calls=%fused_computation.65 | convolution fusion | flops 105840640 | bytes 2298880 | tf_op jit(solution)/shard_map/bhqk,bqhd->bkhd/dot_general | solution.py:28
  43.0 2.1 fusion.246
  46.6 3.8 %fusion.87 = bf16[2,320,2,128]{3,1,2,0:T(8,128)(2,1)} fusion(f32[2,2,320,320]{2,3,1,0:T(8,128)S(1)} %fusion.131, bf16[2,320,2,128]{3,2,1,0:T(2,128)(2,1)} %copy-done.23, f32[2,2,320,320]{2,3,1,0:T(8,128)} %get-tuple-element.37, f32[2,2,320]{2,1,0:T(2,128)S(1)} %get-tuple-element.36), kind=kOutput, calls=%fused_computation.61 | convolution fusion | flops 107890240 | bytes 3937280 | tf_op jit(solution)/shard_map/bhqk,bkhd->bqhd/dot_general | solution.py:32
  50.4 3.6 %fusion.84 = bf16[2,320,2,128]{3,1,2,0:T(8,128)(2,1)} fusion(f32[2,2,320,320]{2,3,1,0:T(8,128)S(1)} %fusion.131, bf16[2,320,2,128]{3,2,1,0:T(2,128)(2,1)} %copy-done.21, f32[2,2,320,320]{2,3,1,0:T(8,128)} %get-tuple-element.37, f32[2,2,320]{2,1,0:T(2,128)S(1)} %get-tuple-element.36), kind=kOutput, calls=%fused_computation.60 | convolution fusion | flops 107890240 | bytes 3937280 | tf_op jit(solution)/shard_map/bhqk,bqhd->bkhd/dot_general | solution.py:33
  54.0 2.7 %fusion.98 = bf16[2,320,2,128]{3,1,2,0:T(8,128)(2,1)} fusion(bf16[2,320,2,128]{3,2,1,0:T(2,128)(2,1)} %reshape.152, f32[2,2,320,320]{2,3,1,0:T(8,128)} %get-tuple-element.37, f32[2,2,320]{2,1,0:T(2,128)S(1)} %get-tuple-element.36), kind=kOutput, calls=%fused_computation.66 | convolution fusion | flops 105840640 | bytes 2298880 | tf_op jit(solution)/shard_map/bhqk,bqhd->bkhd/dot_general | solution.py:28
  57.0 2.3 fusion.241
  59.7 3.6 %fusion.90 = bf16[2,320,2,128]{3,1,2,0:T(8,128)(2,1)} fusion(f32[2,2,320,320]{2,3,1,0:T(8,128)S(1)} %fusion.129, bf16[2,320,2,128]{3,2,1,0:T(2,128)(2,1)S(1)} %reshape.154, f32[2,2,320,320]{2,3,1,0:T(8,128)} %get-tuple-element.35, f32[2,2,320]{2,1,0:T(2,128)S(1)} %get-tuple-element.34), kind=kOutput, calls=%fused_computation.62 | convolution fusion | flops 107890240 | bytes 3937280 | tf_op jit(solution)/shard_map/bhqk,bqhd->bkhd/dot_general | solution.py:33
  63.4 3.7 %fusion.93 = bf16[2,320,2,128]{3,1,2,0:T(8,128)(2,1)} fusion(f32[2,2,320,320]{2,3,1,0:T(8,128)S(1)} %fusion.129, bf16[2,320,2,128]{3,2,1,0:T(2,128)(2,1)S(1)} %reshape.155, f32[2,2,320,320]{2,3,1,0:T(8,128)} %get-tuple-element.35, f32[2,2,320]{2,1,0:T(2,128)S(1)} %get-tuple-element.34), kind=kOutput, calls=%fused_computation.63 | convolution fusion | flops 107890240 | bytes 3937280 | tf_op jit(solution)/shard_map/bhqk,bkhd->bqhd/dot_general | solution.py:32
  67.1 2.7 %fusion.99 = bf16[2,320,2,128]{3,1,2,0:T(8,128)(2,1)} fusion(bf16[2,320,2,128]{3,2,1,0:T(2,128)(2,1)S(1)} %reshape.156, f32[2,2,320,320]{2,3,1,0:T(8,128)} %get-tuple-element.35, f32[2,2,320]{2,1,0:T(2,128)S(1)} %get-tuple-element.34), kind=kOutput, calls=%fused_computation.67 | convolution fusion | flops 105840640 | bytes 2298880 | tf_op jit(solution)/shard_map/bhqk,bqhd->bkhd/dot_general | solution.py:28
  75.5 2.0 copy.41
  78.7 2.0 copy.43
  86.1 2.0 copy.50
  99.6 63.6 %psum.7 = f32[3,4096]{1,0:T(4,128)} all-reduce(f32[3,4096]{1,0:T(4,128)S(1)} %maximum_dynamic-update-slice_fusion), channel_id=1, replica_groups=mesh['section'=2,'dp'=4,'mp'=4] {'dp','mp'}, use_global_device_ids=true, to_apply=%region_16.17 | all-reduce | flops 12288 | bytes 98304 | tf_op jit(solution)/shard_map/psum | solution.py:85
  177.7 3.9 %collective-permute-done.1 = bf16[3,160,256]{2,1,0:T(8,128)(2,1)} collective-permute-done((bf16[3,160,256]{2,1,0:T(8,128)(2,1)}, bf16[3,160,256]{2,1,0:T(8,128)(2,1)}, u32[]{:S(2)}, u32[]{:S(2)}) %collective-permute-start.1) | collective-permute-done | bytes 245792 | tf_op jit(solution)/shard_map/ppermute | solution.py:79
  182.9 3.9 %collective-permute-done.2 = bf16[3,160,256]{2,1,0:T(8,128)(2,1)S(1)} collective-permute-done((bf16[3,160,256]{2,1,0:T(8,128)(2,1)}, bf16[3,160,256]{2,1,0:T(8,128)(2,1)S(1)}, u32[]{:S(2)}, u32[]{:S(2)}) %collective-permute-start.2) | collective-permute-done | bytes 245792 | tf_op jit(solution)/shard_map/ppermute | solution.py:79
  188.1 4.0 %collective-permute-done.3 = bf16[3,160,256]{2,1,0:T(8,128)(2,1)S(1)} collective-permute-done((bf16[3,160,256]{2,1,0:T(8,128)(2,1)}, bf16[3,160,256]{2,1,0:T(8,128)(2,1)S(1)}, u32[]{:S(2)}, u32[]{:S(2)}) %collective-permute-start.3) | collective-permute-done | bytes 245792 | tf_op jit(solution)/shard_map/ppermute | solution.py:79
  202.3 12.5 %collective-permute-done.8 = bf16[3,160,256]{2,1,0:T(8,128)(2,1)S(1)} collective-permute-done((bf16[3,160,256]{2,1,0:T(8,128)(2,1)S(1)}, bf16[3,160,256]{2,1,0:T(8,128)(2,1)S(1)}, u32[]{:S(2)}, u32[]{:S(2)}) %collective-permute-start.8) | collective-permute-done | bytes 245792 | tf_op jit(solution)/shard_map/ppermute | solution.py:79
  216.1 4.0 %collective-permute-done.9 = bf16[3,160,256]{2,1,0:T(8,128)(2,1)S(1)} collective-permute-done((bf16[3,160,256]{2,1,0:T(8,128)(2,1)S(1)}, bf16[3,160,256]{2,1,0:T(8,128)(2,1)S(1)}, u32[]{:S(2)}, u32[]{:S(2)}) %collective-permute-start.9) | collective-permute-done | bytes 245792 | tf_op jit(solution)/shard_map/ppermute | solution.py:79
  221.4 4.0 %collective-permute-done.10 = bf16[3,160,256]{2,1,0:T(8,128)(2,1)S(1)} collective-permute-done((bf16[3,160,256]{2,1,0:T(8,128)(2,1)S(1)}, bf16[3,160,256]{2,1,0:T(8,128)(2,1)S(1)}, u32[]{:S(2)}, u32[]{:S(2)}) %collective-permute-start.10) | collective-permute-done | bytes 245792 | tf_op jit(solution)/shard_map/ppermute | solution.py:79
  226.8 3.9 %collective-permute-done.11 = bf16[3,160,256]{2,1,0:T(8,128)(2,1)S(1)} collective-permute-done((bf16[3,160,256]{2,1,0:T(8,128)(2,1)S(1)}, bf16[3,160,256]{2,1,0:T(8,128)(2,1)S(1)}, u32[]{:S(2)}, u32[]{:S(2)}) %collective-permute-start.11) | collective-permute-done | bytes 245792 | tf_op jit(solution)/shard_map/ppermute | solution.py:79
  230.8 5.3 %collective-permute-done.13 = bf16[3,160,256]{2,1,0:T(8,128)(2,1)S(1)} collective-permute-done((bf16[3,160,256]{2,1,0:T(8,128)(2,1)S(1)}, bf16[3,160,256]{2,1,0:T(8,128)(2,1)S(1)}, u32[]{:S(2)}, u32[]{:S(2)}) %collective-permute-start.13) | collective-permute-done | bytes 245792 | tf_op jit(solution)/shard_map/ppermute | solution.py:79
  236.1 5.3 %collective-permute-done.14 = bf16[3,160,256]{2,1,0:T(8,128)(2,1)S(1)} collective-permute-done((bf16[3,160,256]{2,1,0:T(8,128)(2,1)S(1)}, bf16[3,160,256]{2,1,0:T(8,128)(2,1)S(1)}, u32[]{:S(2)}, u32[]{:S(2)}) %collective-permute-start.14) | collective-permute-done | bytes 245792 | tf_op jit(solution)/shard_map/ppermute | solution.py:79
  241.4 5.3 %collective-permute-done.15 = bf16[3,160,256]{2,1,0:T(8,128)(2,1)S(1)} collective-permute-done((bf16[3,160,256]{2,1,0:T(8,128)(2,1)S(1)}, bf16[3,160,256]{2,1,0:T(8,128)(2,1)S(1)}, u32[]{:S(2)}, u32[]{:S(2)}) %collective-permute-start.15) | collective-permute-done | bytes 245792 | tf_op jit(solution)/shard_map/ppermute | solution.py:79
  (155 shorter events, 70.8 us)
Async XLA Ops:
  0.6 3.2 %copy-start.10 = (bf16[1,1,640,1024]{3,2,1,0:T(8,128)(2,1)S(1)}, bf16[1,1,640,1024]{3,2,1,0:T(8,128)(2,1)}, u32[]{:S(2)}) copy-start(bf16[1,1,640,1024]{3,2,1,0:T(8,128)(2,1)} %param.6) | copy-start | bytes 3932164
  3.0 2.5 %copy-start.26 = (s32[1,1,640]{2,1,0:T(1,128)S(1)}, s32[1,1,640]{2,1,0:T(1,128)}, u32[]{:S(2)}) copy-start(s32[1,1,640]{2,1,0:T(1,128)} %param.9) | copy-start | bytes 7684
  4.8 3.9 %copy-start.11 = (bf16[1,1,640,1024]{3,2,1,0:T(8,128)(2,1)S(1)}, bf16[1,1,640,1024]{3,2,1,0:T(8,128)(2,1)}, u32[]{:S(2)}) copy-start(bf16[1,1,640,1024]{3,2,1,0:T(8,128)(2,1)} %param.7) | copy-start | bytes 3932164
  22.7 2.8 %copy-start.6 = (bf16[640,256]{1,0:T(8,128)(2,1)S(1)}, bf16[640,256]{1,0:T(8,128)(2,1)}, u32[]{:S(2)}) copy-start(bf16[640,256]{1,0:T(8,128)(2,1)} %get-tuple-element.5) | copy-start | bytes 983044
  22.7 2.9 %copy-start.7 = (bf16[640,256]{1,0:T(8,128)(2,1)S(1)}, bf16[640,256]{1,0:T(8,128)(2,1)}, u32[]{:S(2)}) copy-start(bf16[640,256]{1,0:T(8,128)(2,1)} %get-tuple-element.9) | copy-start | bytes 983044
  22.7 3.0 %copy-start.8 = (bf16[640,256]{1,0:T(8,128)(2,1)S(1)}, bf16[640,256]{1,0:T(8,128)(2,1)}, u32[]{:S(2)}) copy-start(bf16[640,256]{1,0:T(8,128)(2,1)} %get-tuple-element.13) | copy-start | bytes 983044
  38.3 2.8 %copy-start.2 = (bf16[640,256]{1,0:T(8,128)(2,1)S(1)}, bf16[640,256]{1,0:T(8,128)(2,1)}, u32[]{:S(2)}) copy-start(bf16[640,256]{1,0:T(8,128)(2,1)} %get-tuple-element.4) | copy-start | bytes 983044
  38.3 2.9 %copy-start.3 = (bf16[640,256]{1,0:T(8,128)(2,1)S(1)}, bf16[640,256]{1,0:T(8,128)(2,1)}, u32[]{:S(2)}) copy-start(bf16[640,256]{1,0:T(8,128)(2,1)} %get-tuple-element.8) | copy-start | bytes 983044
  38.3 3.0 %copy-start.4 = (bf16[640,256]{1,0:T(8,128)(2,1)S(1)}, bf16[640,256]{1,0:T(8,128)(2,1)}, u32[]{:S(2)}) copy-start(bf16[640,256]{1,0:T(8,128)(2,1)} %get-tuple-element.12) | copy-start | bytes 983044
  41.2 1.8 copy-start.21
  67.1 2.7 %copy-start.16 = (bf16[2,320,2,128]{3,1,2,0:T(8,128)(2,1)S(1)}, bf16[2,320,2,128]{3,1,2,0:T(8,128)(2,1)}, u32[]{:S(2)}) copy-start(bf16[2,320,2,128]{3,1,2,0:T(8,128)(2,1)} %fusion.75) | copy-start | bytes 983044
  163.2 10.2 %collective-permute-start.16 = (f32[3,4096]{1,0:T(4,128)}, f32[3,4096]{1,0:T(4,128)S(1)}, u32[]{:S(2)}, u32[]{:S(2)}) collective-permute-start(f32[3,4096]{1,0:T(4,128)} %psum.7), channel_id=1, source_target_pairs={{16,0},{17,1},{18,2},{19,3},{20,4},{21,5},{22,6},{23,7},{24,8},{25... | collective-permute-start | bytes 147464 | tf_op jit(solution)/shard_map/ppermute | solution.py:86
  165.3 6.0 %copy-start = (bf16[3,640,256]{2,1,0:T(8,128)(2,1)S(1)}, bf16[3,640,256]{2,1,0:T(8,128)(2,1)}, u32[]{:S(2)}) copy-start(bf16[3,640,256]{2,1,0:T(8,128)(2,1)} %constant_dynamic-update-slice_fusion.9) | copy-start | bytes 2949124
  165.3 11.0 %collective-permute-start = (bf16[3,160,256]{2,1,0:T(8,128)(2,1)S(1)}, bf16[3,160,256]{2,1,0:T(8,128)(2,1)}, u32[]{:S(2)}, u32[]{:S(2)}) collective-permute-start(bf16[3,160,256]{2,1,0:T(8,128)(2,1)S(1)} %get-tuple-element.21), channel_id=1, source_target_pairs={{16,0},{17,1},{18,2},{19,3},{20,4},{21,5},{22,6},{23,7},{24,8},{25... | collective-permute-start | bytes 737288 | tf_op jit(solution)/shard_map/ppermute | solution.py:79
  167.7 25.7 %copy-start.24 = (bf16[3,160,256]{2,1,0:T(8,128)(2,1)S(1)}, bf16[3,160,256]{2,1,0:T(8,128)(2,1)}, u32[]{:S(2)}) copy-start(bf16[3,160,256]{2,1,0:T(8,128)(2,1)} %get-tuple-element.23) | copy-start | bytes 737284
  167.7 14.0 %collective-permute-start.1 = (bf16[3,160,256]{2,1,0:T(8,128)(2,1)}, bf16[3,160,256]{2,1,0:T(8,128)(2,1)}, u32[]{:S(2)}, u32[]{:S(2)}) collective-permute-start(bf16[3,160,256]{2,1,0:T(8,128)(2,1)} %get-tuple-element.25), channel_id=1, source_target_pairs={{16,0},{17,1},{18,2},{19,3},{20,4},{21,5},{22,6},{23,7},{24,8},{25... | collective-permute-start | bytes 737288 | tf_op jit(solution)/shard_map/ppermute | solution.py:79
  169.9 11.7 %copy-start.25 = (bf16[3,160,256]{2,1,0:T(8,128)(2,1)S(1)}, bf16[3,160,256]{2,1,0:T(8,128)(2,1)}, u32[]{:S(2)}) copy-start(bf16[3,160,256]{2,1,0:T(8,128)(2,1)} %get-tuple-element.28) | copy-start | bytes 737284
  169.9 16.8 %collective-permute-start.2 = (bf16[3,160,256]{2,1,0:T(8,128)(2,1)}, bf16[3,160,256]{2,1,0:T(8,128)(2,1)S(1)}, u32[]{:S(2)}, u32[]{:S(2)}) collective-permute-start(bf16[3,160,256]{2,1,0:T(8,128)(2,1)} %get-tuple-element.29), channel_id=1, source_target_pairs={{16,0},{17,1},{18,2},{19,3},{20,4},{21,5},{22,6},{23,7},{24,8},{25... | collective-permute-start | bytes 737288 | tf_op jit(solution)/shard_map/ppermute | solution.py:79
  172.1 19.9 %collective-permute-start.3 = (bf16[3,160,256]{2,1,0:T(8,128)(2,1)}, bf16[3,160,256]{2,1,0:T(8,128)(2,1)S(1)}, u32[]{:S(2)}, u32[]{:S(2)}) collective-permute-start(bf16[3,160,256]{2,1,0:T(8,128)(2,1)} %get-tuple-element.33), channel_id=1, source_target_pairs={{16,0},{17,1},{18,2},{19,3},{20,4},{21,5},{22,6},{23,7},{24,8},{25... | collective-permute-start | bytes 737288 | tf_op jit(solution)/shard_map/ppermute | solution.py:79
  173.4 19.9 %collective-permute-start.4 = (bf16[3,160,256]{2,1,0:T(8,128)(2,1)}, bf16[3,160,256]{2,1,0:T(8,128)(2,1)S(1)}, u32[]{:S(2)}, u32[]{:S(2)}) collective-permute-start(bf16[3,160,256]{2,1,0:T(8,128)(2,1)} %get-tuple-element.20), channel_id=1, source_target_pairs={{16,1},{17,2},{18,3},{19,0},{20,5},{21,6},{22,7},{23,4},{24,9},{25... | collective-permute-start | bytes 737288 | tf_op jit(solution)/shard_map/ppermute | solution.py:79
  176.3 18.3 %collective-permute-start.5 = (bf16[3,160,256]{2,1,0:T(8,128)(2,1)}, bf16[3,160,256]{2,1,0:T(8,128)(2,1)S(1)}, u32[]{:S(2)}, u32[]{:S(2)}) collective-permute-start(bf16[3,160,256]{2,1,0:T(8,128)(2,1)} %get-tuple-element.24), channel_id=1, source_target_pairs={{16,1},{17,2},{18,3},{19,0},{20,5},{21,6},{22,7},{23,4},{24,9},{25... | collective-permute-start | bytes 737288 | tf_op jit(solution)/shard_map/ppermute | solution.py:79
  181.6 15.0 %collective-permute-start.6 = (bf16[3,160,256]{2,1,0:T(8,128)(2,1)S(1)}, bf16[3,160,256]{2,1,0:T(8,128)(2,1)S(1)}, u32[]{:S(2)}, u32[]{:S(2)}) collective-permute-start(bf16[3,160,256]{2,1,0:T(8,128)(2,1)S(1)} %copy-done.25), channel_id=1, source_target_pairs={{16,1},{17,2},{18,3},{19,0},{20,5},{21,6},{22,7},{23,4},{24,9},{25... | collective-permute-start | bytes 737288 | tf_op jit(solution)/shard_map/ppermute | solution.py:79
  186.8 14.3 %collective-permute-start.7 = (bf16[3,160,256]{2,1,0:T(8,128)(2,1)S(1)}, bf16[3,160,256]{2,1,0:T(8,128)(2,1)S(1)}, u32[]{:S(2)}, u32[]{:S(2)}) collective-permute-start(bf16[3,160,256]{2,1,0:T(8,128)(2,1)S(1)} %get-tuple-element.32), channel_id=1, source_target_pairs={{16,1},{17,2},{18,3},{19,0},{20,5},{21,6},{22,7},{23,4},{24,9},{25... | collective-permute-start | bytes 737288 | tf_op jit(solution)/shard_map/ppermute | solution.py:79
  192.0 22.8 %collective-permute-start.8 = (bf16[3,160,256]{2,1,0:T(8,128)(2,1)S(1)}, bf16[3,160,256]{2,1,0:T(8,128)(2,1)S(1)}, u32[]{:S(2)}, u32[]{:S(2)}) collective-permute-start(bf16[3,160,256]{2,1,0:T(8,128)(2,1)S(1)} %get-tuple-element.19), channel_id=1, source_target_pairs={{16,2},{17,3},{18,0},{19,1},{20,6},{21,7},{22,4},{23,5},{24,10},{2... | collective-permute-start | bytes 737288 | tf_op jit(solution)/shard_map/ppermute | solution.py:79
  193.3 26.8 %collective-permute-start.9 = (bf16[3,160,256]{2,1,0:T(8,128)(2,1)S(1)}, bf16[3,160,256]{2,1,0:T(8,128)(2,1)S(1)}, u32[]{:S(2)}, u32[]{:S(2)}) collective-permute-start(bf16[3,160,256]{2,1,0:T(8,128)(2,1)S(1)} %copy-done.24), channel_id=1, source_target_pairs={{16,2},{17,3},{18,0},{19,1},{20,6},{21,7},{22,4},{23,5},{24,10},{2... | collective-permute-start | bytes 737288 | tf_op jit(solution)/shard_map/ppermute | solution.py:79
  194.7 30.7 %collective-permute-start.10 = (bf16[3,160,256]{2,1,0:T(8,128)(2,1)S(1)}, bf16[3,160,256]{2,1,0:T(8,128)(2,1)S(1)}, u32[]{:S(2)}, u32[]{:S(2)}) collective-permute-start(bf16[3,160,256]{2,1,0:T(8,128)(2,1)S(1)} %get-tuple-element.27), channel_id=1, source_target_pairs={{16,2},{17,3},{18,0},{19,1},{20,6},{21,7},{22,4},{23,5},{24,10},{2... | collective-permute-start | bytes 737288 | tf_op jit(solution)/shard_map/ppermute | solution.py:79
  196.6 34.0 %collective-permute-start.11 = (bf16[3,160,256]{2,1,0:T(8,128)(2,1)S(1)}, bf16[3,160,256]{2,1,0:T(8,128)(2,1)S(1)}, u32[]{:S(2)}, u32[]{:S(2)}) collective-permute-start(bf16[3,160,256]{2,1,0:T(8,128)(2,1)S(1)} %get-tuple-element.31), channel_id=1, source_target_pairs={{16,2},{17,3},{18,0},{19,1},{20,6},{21,7},{22,4},{23,5},{24,10},{2... | collective-permute-start | bytes 737288 | tf_op jit(solution)/shard_map/ppermute | solution.py:79
  201.0 29.8 %collective-permute-start.12 = (bf16[3,160,256]{2,1,0:T(8,128)(2,1)S(1)}, bf16[3,160,256]{2,1,0:T(8,128)(2,1)S(1)}, u32[]{:S(2)}, u32[]{:S(2)}) collective-permute-start(bf16[3,160,256]{2,1,0:T(8,128)(2,1)S(1)} %get-tuple-element.18), channel_id=1, source_target_pairs={{16,3},{17,0},{18,1},{19,2},{20,7},{21,4},{22,5},{23,6},{24,11},{2... | collective-permute-start | bytes 737288 | tf_op jit(solution)/shard_map/ppermute | solution.py:79
  214.9 21.3 %collective-permute-start.13 = (bf16[3,160,256]{2,1,0:T(8,128)(2,1)S(1)}, bf16[3,160,256]{2,1,0:T(8,128)(2,1)S(1)}, u32[]{:S(2)}, u32[]{:S(2)}) collective-permute-start(bf16[3,160,256]{2,1,0:T(8,128)(2,1)S(1)} %get-tuple-element.22), channel_id=1, source_target_pairs={{16,3},{17,0},{18,1},{19,2},{20,7},{21,4},{22,5},{23,6},{24,11},{2... | collective-permute-start | bytes 737288 | tf_op jit(solution)/shard_map/ppermute | solution.py:79
  220.1 21.3 %collective-permute-start.14 = (bf16[3,160,256]{2,1,0:T(8,128)(2,1)S(1)}, bf16[3,160,256]{2,1,0:T(8,128)(2,1)S(1)}, u32[]{:S(2)}, u32[]{:S(2)}) collective-permute-start(bf16[3,160,256]{2,1,0:T(8,128)(2,1)S(1)} %get-tuple-element.26), channel_id=1, source_target_pairs={{16,3},{17,0},{18,1},{19,2},{20,7},{21,4},{22,5},{23,6},{24,11},{2... | collective-permute-start | bytes 737288 | tf_op jit(solution)/shard_map/ppermute | solution.py:79
  225.4 21.3 %collective-permute-start.15 = (bf16[3,160,256]{2,1,0:T(8,128)(2,1)S(1)}, bf16[3,160,256]{2,1,0:T(8,128)(2,1)S(1)}, u32[]{:S(2)}, u32[]{:S(2)}) collective-permute-start(bf16[3,160,256]{2,1,0:T(8,128)(2,1)S(1)} %get-tuple-element.30), channel_id=1, source_target_pairs={{16,3},{17,0},{18,1},{19,2},{20,7},{21,4},{22,5},{23,6},{24,11},{2... | collective-permute-start | bytes 737288 | tf_op jit(solution)/shard_map/ppermute | solution.py:79
  246.8 1.9 copy-start.1
  (12 other events, 15.3 us)

commit v2 on v1

v2 whole, which is shorter than its diff:
```python
import functools
import math

import jax
import jax.numpy as jnp
from jax import lax
from jax.experimental import pallas as pl
from jax.experimental.pallas import tpu as pltpu
from jax.sharding import PartitionSpec as P

HEAD_DIM = 128
CHUNK_HEADS = 2
NT = (((1,), (1,)), ((), ()))


def grads_kernel(part_ref, pos_ref, q_ref, k_ref, v_ref, g_ref, out_ref, sum_ref, full_ref, *, parts):
    length = q_ref.shape[0]
    half = length // 2
    window = -(-half // 128) * 128
    rows = length // parts
    scaling = 1.0 / math.sqrt(HEAD_DIM)
    for b, lo in enumerate((0, length - window)):
        q = q_ref[lo : lo + window, :]
        k = k_ref[lo : lo + window, :]
        v = v_ref[lo : lo + window, :]
        g = g_ref[lo : lo + window, :]
        scores = lax.dot_general(q, k, NT, preferred_element_type=jnp.float32) * scaling
        qi = lo + lax.broadcasted_iota(jnp.int32, (window, window), 0)
        kj = lo + lax.broadcasted_iota(jnp.int32, (window, window), 1)
        start = qi - pos_ref[lo : lo + window, :]
        allowed = (kj <= qi) & (kj >= start)
        scores = jnp.where(allowed, scores, jnp.float32(-1e30))
        highest = jnp.max(scores, axis=1, keepdims=True)
        expont = jnp.exp(scores - highest)
        attn = expont / jnp.sum(expont, axis=1, keepdims=True)
        grad_v = jnp.dot(attn.T.astype(jnp.bfloat16), g, preferred_element_type=jnp.float32)
        grad_attn = lax.dot_general(g, v, NT, preferred_element_type=jnp.float32)
        delta = jnp.sum(attn * grad_attn, axis=1, keepdims=True)
        grad_scores = attn * (grad_attn - delta) * scaling
        grad_q = jnp.dot(grad_scores.astype(jnp.bfloat16), k, preferred_element_type=jnp.float32)
        grad_k = jnp.dot(grad_scores.T.astype(jnp.bfloat16), q, preferred_element_type=jnp.float32)
        keep = b * half - lo
        for i, grad in enumerate((grad_q, grad_k, grad_v)):
            full_ref[i, b * half : (b + 1) * half, :] = grad[keep : keep + half].astype(jnp.bfloat16)
    sum_ref[...] = jnp.sum(full_ref[...].astype(jnp.float32), axis=1)
    part = part_ref[0]
    for shift in range(parts):
        target = (part + shift) % parts
        out_ref[shift] = full_ref[:, pl.ds(pl.multiple_of(target * rows, 16), rows), :]


def chunk_grads(part, positions, query_rows, key_rows, value_rows, grad_rows, chunk, heads, parts):
    length = query_rows.shape[0]
    rows = length // parts
    width = heads * HEAD_DIM

    def column(h, part_ref):
        return (0, chunk * heads + h)

    in_block = pl.BlockSpec((length, HEAD_DIM), column)
    grid_spec = pltpu.PrefetchScalarGridSpec(
        num_scalar_prefetch=1,
        grid=(heads,),
        in_specs=[pl.BlockSpec((length, 1), lambda h, part_ref: (0, 0))] + [in_block] * 4,
        out_specs=[
            pl.BlockSpec((parts, 3, rows, HEAD_DIM), lambda h, part_ref: (0, 0, 0, h)),
            pl.BlockSpec((3, HEAD_DIM), lambda h, part_ref: (0, h)),
        ],
        scratch_shapes=[pltpu.VMEM((3, length, HEAD_DIM), jnp.bfloat16)],
    )
    return pl.pallas_call(
        functools.partial(grads_kernel, parts=parts),
        grid_spec=grid_spec,
        out_shape=[
            jax.ShapeDtypeStruct((parts, 3, rows, width), jnp.bfloat16),
            jax.ShapeDtypeStruct((3, width), jnp.float32),
        ],
    )(part, positions, query_rows, key_rows, value_rows, grad_rows)


def butterfly_sum(value, axis):
    count = lax.axis_size(axis)
    step = 1
    while step < count:
        value = value + lax.ppermute(value, axis, [(i, i ^ step) for i in range(count)])
        step *= 2
    return value


def per_device(queries, keys, values, grad_out, positions):
    query_rows = queries[0, 0]
    key_rows = keys[0, 0]
    value_rows = values[0, 0]
    grad_rows = grad_out[0, 0]
    token_positions = positions[0, 0].reshape(-1, 1)
    length, columns = query_rows.shape
    sections = lax.axis_size("section")
    parts = lax.axis_size("mp")
    replicas = lax.axis_size("dp")
    part = lax.axis_index("mp")
    rows = length // parts
    heads = min(CHUNK_HEADS, columns // HEAD_DIM)
    width = heads * HEAD_DIM
    chunk_count = columns // width
    part_arg = jnp.reshape(part, (1,)).astype(jnp.int32)

    def pairs(shift):
        return [
            ((s + 1) * parts + m, s * parts + (m + shift) % parts)
            for s in range(sections - 1)
            for m in range(parts)
        ]

    arrived = [[None] * chunk_count for _ in range(parts)]
    sums = []
    for c in range(chunk_count):
        grads, chunk_sums = chunk_grads(
            part_arg, token_positions, query_rows, key_rows, value_rows, grad_rows, c, heads, parts
        )
        sums.append(chunk_sums)
        for shift in range(parts):
            arrived[shift][c] = lax.ppermute(grads[shift], ("section", "mp"), pairs(shift))

    own = jnp.concatenate(sums, axis=1)
    slots = lax.dynamic_update_slice_in_dim(
        jnp.zeros((3, columns * parts), jnp.float32), own, part * columns, 1
    )
    totals = butterfly_sum(butterfly_sum(slots, "mp"), "dp")
    totals = lax.ppermute(totals, "section", [(s + 1, s) for s in range(sections - 1)])
    bias_grad = totals / math.sqrt(replicas * length)

    received = jnp.zeros((3, rows, columns * parts), jnp.bfloat16)
    for shift in range(parts):
        source = (part - shift) % parts
        for c in range(chunk_count):
            received = lax.dynamic_update_slice_in_dim(
                received, arrived[shift][c], source * columns + c * width, 2
            )
    return (received[None, None], bias_grad[None])


def solution(mesh):
    return jax.shard_map(
        per_device,
        mesh=mesh,
        in_specs=(
            P("section", "dp", None, "mp"),
            P("section", "dp", None, "mp"),
            P("section", "dp", None, "mp"),
            P("section", "dp", None, "mp"),
            P("section", "dp", None),
        ),
        out_specs=(P("section", "dp", None, "mp", None), P("section", None, None)),
        check_vma=False,
    )
```

time: 253 us -> 129 us (0.51); the launches traced: 249 us -> 129 us
  blocking collectives: 63.6 us -> 0 us
  matrix products: 55.1 us -> 0 us
  local copies, waits for them, and re-layouts: 47.7 us -> 10.9 us
  Pallas kernels: 0 us -> 26.7 us
  starting transfers between devices: 22.2 us -> 29.9 us
  waiting for transfers between devices: 55 us -> 59.7 us
  other arithmetic: 3.64 us -> 0.09 us
    psum x1 -> x0, blocking collectives: 63.6 us -> none  [per_device(): totals = lax.psum(slots, ('dp', 'mp'))]
    dot_general x16 -> x0, matrix products: 45.4 us -> none  [the longest x4 15.1 us: chunk_grads(): jnp.einsum('bhqk,bkhd->bqhd', grad_scores, k, preferred_element_type=jnp....]
    pallas_call x0 -> x4, Pallas kernels: none -> 26.7 us  [chunk_grads(): pl.pallas_call(functools.partial(grads_kernel, parts=parts), grid_spec=gr...]
    transpose x12 -> x0, local copies, waits for them, and re-layouts: 11.6 us -> none  [the longest x4 4.73 us: chunk_grads(): jnp.einsum('bhqk,bqhd->bkhd', attn_low, g, preferred_element_type=jnp.flo...]
    another operation x17 -> x1, local copies, waits for them, and re-layouts: 12.4 us -> 1.58 us  [per_device(): token_positions = positions[0, 0].reshape(-1, 1)]
    sub x4 -> x0, matrix products: 9.71 us -> none  [chunk_grads(): expont = jnp.exp(scores - highest)]
    ppermute x1, waiting for transfers between devices: 0.01 us -> 8.17 us  [per_device(): lax.ppermute(totals, 'section', [(s + 1, s) for s in range(sections - 1)])]
    ppermute x16 -> x20, starting transfers between devices: 20.9 us -> 28.7 us  [the longest x16 20.9 us: per_device(): lax.ppermute(grads[shift], ('section', 'mp'), pairs(shift))]
  transfers between devices with their start and end apart: 17 -> 21, of which waited for: 13 -> 15; matrix products, arithmetic and copies ran while one was open for 2% -> 5% of each run, Pallas kernels for 0% -> 0%
where the time goes in v2:
time: 129 us
  waiting for transfers between devices  59.7 us (46%)
  starting transfers between devices  29.9 us (23%)
  Pallas kernels  26.7 us (21%)
  local copies, waits for them, and re-layouts  10.9 us (8%)
  between operations  1.29 us (1%)
    ppermute x16, waiting for transfers between devices, per_device(): lax.ppermute(grads[shift], ('section', 'mp'), pairs(shift))  49.9 us
    pallas_call x4, Pallas kernels, chunk_grads(): pl.pallas_call(functools.partial(grads_kernel, parts=parts), grid_spec=gr...  26.7 us
    ppermute x16, starting transfers between devices, per_device(): lax.ppermute(grads[shift], ('section', 'mp'), pairs(shift))  20.9 us
    ppermute x1, waiting for transfers between devices, per_device(): lax.ppermute(totals, 'section', [(s + 1, s) for s in range(sections - 1)])  8.17 us
    ppermute x4, starting transfers between devices, butterfly_sum(): lax.ppermute(value, axis, [(i, i ^ step) for i in range(count)])  7.71 us
    squeeze x4, local copies, waits for them, and re-layouts, per_device(): grads[shift]  5.02 us
    unnamed x34, local copies, waits for them, and re-layouts  2.68 us
  transfers between devices with their start and end apart: 21, of which 15 were waited for; matrix products, arithmetic and copies ran while one was open for 5% of the time, Pallas kernels for 0%

profile of v2, /device:TPU:0, one launch (start us, length us, event | category | flops | bytes accessed | tf_op | source)
XLA Modules:
  0.0 128.7 jit_solution(16590385435201330269)
XLA Ops:
  0.6 1.6 %copy.8.pos_ref = s32[640,1]{1,0:T(8,128)} copy(s32[640,1]{0,1:T(1,128)} %bitcast.88) | data formatting | bytes 5120 | tf_op jit(solution)/shard_map/reshape;squeeze | solution.py:95
  2.2 6.7 %shard_map.68 = (bf16[4,3,160,256]{3,2,1,0:T(8,128)(2,1)}, f32[3,256]{1,0:T(4,128)}) custom-call(s32[1]{0:T(128)} %bitcast.part_ref, s32[640,1]{1,0:T(8,128)} %copy.8.pos_ref, bf16[640,1024]{1,0:T(8,128)(2,1)} %bitcast.72, bf16[640,1024]{1,0:T(8,128)(2,1)} %bitcast.76, bf16[640,1024]{1,0:T(8,128)(2,1)} %bitcast.80, bf16[640,1024]{1,0:T(8,128)(2,1)} %bitcast.84), custom_call_target="tpu_custom_call" | custom-call | tf_op jit(solution)/shard_map/pallas_call | solution.py:71
  8.9 6.7 %shard_map.69 = (bf16[4,3,160,256]{3,2,1,0:T(8,128)(2,1)}, f32[3,256]{1,0:T(4,128)}) custom-call(s32[1]{0:T(128)} %bitcast.part_ref, s32[640,1]{1,0:T(8,128)} %copy.8.pos_ref, bf16[640,1024]{1,0:T(8,128)(2,1)} %bitcast.73, bf16[640,1024]{1,0:T(8,128)(2,1)} %bitcast.77, bf16[640,1024]{1,0:T(8,128)(2,1)} %bitcast.81, bf16[640,1024]{1,0:T(8,128)(2,1)} %bitcast.85), custom_call_target="tpu_custom_call" | custom-call | tf_op jit(solution)/shard_map/pallas_call | solution.py:71
  15.5 6.6 %shard_map.70 = (bf16[4,3,160,256]{3,2,1,0:T(8,128)(2,1)}, f32[3,256]{1,0:T(4,128)}) custom-call(s32[1]{0:T(128)} %bitcast.part_ref, s32[640,1]{1,0:T(8,128)} %copy.8.pos_ref, bf16[640,1024]{1,0:T(8,128)(2,1)} %bitcast.74, bf16[640,1024]{1,0:T(8,128)(2,1)} %bitcast.78, bf16[640,1024]{1,0:T(8,128)(2,1)} %bitcast.82, bf16[640,1024]{1,0:T(8,128)(2,1)} %bitcast.86), custom_call_target="tpu_custom_call" | custom-call | tf_op jit(solution)/shard_map/pallas_call | solution.py:71
  22.2 6.8 %shard_map.71 = (bf16[4,3,160,256]{3,2,1,0:T(8,128)(2,1)}, f32[3,256]{1,0:T(4,128)}) custom-call(s32[1]{0:T(128)} %bitcast.part_ref, s32[640,1]{1,0:T(8,128)} %copy.8.pos_ref, bf16[640,1024]{1,0:T(8,128)(2,1)} %bitcast.75, bf16[640,1024]{1,0:T(8,128)(2,1)} %bitcast.79, bf16[640,1024]{1,0:T(8,128)(2,1)} %bitcast.83, bf16[640,1024]{1,0:T(8,128)(2,1)} %bitcast.87), custom_call_target="tpu_custom_call" | custom-call | tf_op jit(solution)/shard_map/pallas_call | solution.py:71
  31.3 2.9 %collective-permute-start.17 = (f32[3,4096]{1,0:T(4,128)S(1)}, f32[3,4096]{1,0:T(4,128)S(1)}, u32[]{:S(2)}, u32[]{:S(2)}) collective-permute-start(f32[3,4096]{1,0:T(4,128)S(1)} %add_dynamic-update-slice_fusion), channel_id=1, source_target_pairs={{0,2},{1,3},{2,0},{3,1},{4,6},{5,7},{6,4},{7,5},{8,10},{9,11},{10,... | collective-permute-start | bytes 147464 | tf_op jit(solution)/shard_map/ppermute | solution.py:85
  34.2 2.2 %slice_bitcast_fusion.3 = (bf16[3,160,256]{2,1,0:T(8,128)(2,1)S(1)}, bf16[3,160,256]{2,1,0:T(8,128)(2,1)}, bf16[3,160,256]{2,1,0:T(8,128)(2,1)}, bf16[3,160,256]{2,1,0:T(8,128)(2,1)}) fusion(bf16[4,3,160,256]{3,2,1,0:T(8,128)(2,1)} %get-tuple-element.10), kind=kLoop, calls=%fused_computation.19 | loop fusion | bytes 1966080 | tf_op jit(solution)/shard_map/squeeze | solution.py:122
  37.8 1.6 %collective-permute-start.18 = (f32[3,4096]{1,0:T(4,128)S(1)}, f32[3,4096]{1,0:T(4,128)S(1)}, u32[]{:S(2)}, u32[]{:S(2)}) collective-permute-start(f32[3,4096]{1,0:T(4,128)S(1)} %add.174), channel_id=1, source_target_pairs={{0,4},{4,0},{8,12},{12,8},{1,5},{5,1},{9,13},{13,9},{2,6},{6,2},{1... | collective-permute-start | bytes 147464 | tf_op jit(solution)/shard_map/ppermute | solution.py:85
  42.1 2.6 %collective-permute-start.19 = (f32[3,4096]{1,0:T(4,128)S(1)}, f32[3,4096]{1,0:T(4,128)S(1)}, u32[]{:S(2)}, u32[]{:S(2)}) collective-permute-start(f32[3,4096]{1,0:T(4,128)S(1)} %add.175), channel_id=1, source_target_pairs={{0,8},{4,12},{8,0},{12,4},{1,9},{5,13},{9,1},{13,5},{2,10},{6,14},... | collective-permute-start | bytes 147464 | tf_op jit(solution)/shard_map/ppermute | solution.py:85
  45.8 1.4 %collective-permute-start.2 = (bf16[3,160,256]{2,1,0:T(8,128)(2,1)}, bf16[3,160,256]{2,1,0:T(8,128)(2,1)S(1)}, u32[]{:S(2)}, u32[]{:S(2)}) collective-permute-start(bf16[3,160,256]{2,1,0:T(8,128)(2,1)} %get-tuple-element.29), channel_id=1, source_target_pairs={{16,0},{17,1},{18,2},{19,3},{20,4},{21,5},{22,6},{23,7},{24,8},{25... | collective-permute-start | bytes 737288 | tf_op jit(solution)/shard_map/ppermute | solution.py:122
  47.4 1.3 %collective-permute-start.20 = (f32[3,4096]{1,0:T(4,128)S(1)}, f32[3,4096]{1,0:T(4,128)S(1)}, u32[]{:S(2)}, u32[]{:S(2)}) collective-permute-start(f32[3,4096]{1,0:T(4,128)S(1)} %add.176), channel_id=1, source_target_pairs={{16,0},{17,1},{18,2},{19,3},{20,4},{21,5},{22,6},{23,7},{24,8},{25... | collective-permute-start | bytes 147464 | tf_op jit(solution)/shard_map/ppermute | solution.py:129
  49.6 1.4 %collective-permute-start.3 = (bf16[3,160,256]{2,1,0:T(8,128)(2,1)}, bf16[3,160,256]{2,1,0:T(8,128)(2,1)S(1)}, u32[]{:S(2)}, u32[]{:S(2)}) collective-permute-start(bf16[3,160,256]{2,1,0:T(8,128)(2,1)} %get-tuple-element.25), channel_id=1, source_target_pairs={{16,0},{17,1},{18,2},{19,3},{20,4},{21,5},{22,6},{23,7},{24,8},{25... | collective-permute-start | bytes 737288 | tf_op jit(solution)/shard_map/ppermute | solution.py:122
  51.2 8.2 %collective-permute-done.20 = f32[3,4096]{1,0:T(4,128)S(1)} collective-permute-done((f32[3,4096]{1,0:T(4,128)S(1)}, f32[3,4096]{1,0:T(4,128)S(1)}, u32[]{:S(2)}, u32[]{:S(2)}) %collective-permute-start.20) | collective-permute-done | bytes 49184 | tf_op jit(solution)/shard_map/ppermute | solution.py:129
  60.7 1.4 %collective-permute-start.5 = (bf16[3,160,256]{2,1,0:T(8,128)(2,1)}, bf16[3,160,256]{2,1,0:T(8,128)(2,1)S(1)}, u32[]{:S(2)}, u32[]{:S(2)}) collective-permute-start(bf16[3,160,256]{2,1,0:T(8,128)(2,1)} %get-tuple-element.32), channel_id=1, source_target_pairs={{16,1},{17,2},{18,3},{19,0},{20,5},{21,6},{22,7},{23,4},{24,9},{25... | collective-permute-start | bytes 737288 | tf_op jit(solution)/shard_map/ppermute | solution.py:122
  62.6 1.3 %collective-permute-start.6 = (bf16[3,160,256]{2,1,0:T(8,128)(2,1)S(1)}, bf16[3,160,256]{2,1,0:T(8,128)(2,1)S(1)}, u32[]{:S(2)}, u32[]{:S(2)}) collective-permute-start(bf16[3,160,256]{2,1,0:T(8,128)(2,1)S(1)} %copy-done.10), channel_id=1, source_target_pairs={{16,1},{17,2},{18,3},{19,0},{20,5},{21,6},{22,7},{23,4},{24,9},{25... | collective-permute-start | bytes 737288 | tf_op jit(solution)/shard_map/ppermute | solution.py:122
  64.0 1.3 %collective-permute-start.7 = (bf16[3,160,256]{2,1,0:T(8,128)(2,1)S(1)}, bf16[3,160,256]{2,1,0:T(8,128)(2,1)S(1)}, u32[]{:S(2)}, u32[]{:S(2)}) collective-permute-start(bf16[3,160,256]{2,1,0:T(8,128)(2,1)S(1)} %copy-done.11), channel_id=1, source_target_pairs={{16,1},{17,2},{18,3},{19,0},{20,5},{21,6},{22,7},{23,4},{24,9},{25... | collective-permute-start | bytes 737288 | tf_op jit(solution)/shard_map/ppermute | solution.py:122
  65.3 1.3 %collective-permute-start.8 = (bf16[3,160,256]{2,1,0:T(8,128)(2,1)S(1)}, bf16[3,160,256]{2,1,0:T(8,128)(2,1)S(1)}, u32[]{:S(2)}, u32[]{:S(2)}) collective-permute-start(bf16[3,160,256]{2,1,0:T(8,128)(2,1)S(1)} %copy-done.6), channel_id=1, source_target_pairs={{16,2},{17,3},{18,0},{19,1},{20,6},{21,7},{22,4},{23,5},{24,10},{2... | collective-permute-start | bytes 737288 | tf_op jit(solution)/shard_map/ppermute | solution.py:122
  66.7 4.0 %collective-permute-done.4 = bf16[3,160,256]{2,1,0:T(8,128)(2,1)S(1)} collective-permute-done((bf16[3,160,256]{2,1,0:T(8,128)(2,1)}, bf16[3,160,256]{2,1,0:T(8,128)(2,1)S(1)}, u32[]{:S(2)}, u32[]{:S(2)}) %collective-permute-start.4) | collective-permute-done | bytes 245792 | tf_op jit(solution)/shard_map/ppermute | solution.py:122
  70.6 1.3 collective-permute-start.9
  72.0 3.9 %collective-permute-done.5 = bf16[3,160,256]{2,1,0:T(8,128)(2,1)S(1)} collective-permute-done((bf16[3,160,256]{2,1,0:T(8,128)(2,1)}, bf16[3,160,256]{2,1,0:T(8,128)(2,1)S(1)}, u32[]{:S(2)}, u32[]{:S(2)}) %collective-permute-start.5) | collective-permute-done | bytes 245792 | tf_op jit(solution)/shard_map/ppermute | solution.py:122
  75.9 1.3 collective-permute-start.10
  77.2 3.9 %collective-permute-done.6 = bf16[3,160,256]{2,1,0:T(8,128)(2,1)S(1)} collective-permute-done((bf16[3,160,256]{2,1,0:T(8,128)(2,1)S(1)}, bf16[3,160,256]{2,1,0:T(8,128)(2,1)S(1)}, u32[]{:S(2)}, u32[]{:S(2)}) %collective-permute-start.6) | collective-permute-done | bytes 245792 | tf_op jit(solution)/shard_map/ppermute | solution.py:122
  82.5 3.9 %collective-permute-done.7 = bf16[3,160,256]{2,1,0:T(8,128)(2,1)S(1)} collective-permute-done((bf16[3,160,256]{2,1,0:T(8,128)(2,1)S(1)}, bf16[3,160,256]{2,1,0:T(8,128)(2,1)S(1)}, u32[]{:S(2)}, u32[]{:S(2)}) %collective-permute-start.7) | collective-permute-done | bytes 245792 | tf_op jit(solution)/shard_map/ppermute | solution.py:122
  87.8 1.3 %collective-permute-start.13 = (bf16[3,160,256]{2,1,0:T(8,128)(2,1)S(1)}, bf16[3,160,256]{2,1,0:T(8,128)(2,1)S(1)}, u32[]{:S(2)}, u32[]{:S(2)}) collective-permute-start(bf16[3,160,256]{2,1,0:T(8,128)(2,1)S(1)} %copy-done.4), channel_id=1, source_target_pairs={{16,3},{17,0},{18,1},{19,2},{20,7},{21,4},{22,5},{23,6},{24,11},{2... | collective-permute-start | bytes 737288 | tf_op jit(solution)/shard_map/ppermute | solution.py:122
  89.1 3.6 %collective-permute-done.9 = bf16[3,160,256]{2,1,0:T(8,128)(2,1)S(1)} collective-permute-done((bf16[3,160,256]{2,1,0:T(8,128)(2,1)S(1)}, bf16[3,160,256]{2,1,0:T(8,128)(2,1)S(1)}, u32[]{:S(2)}, u32[]{:S(2)}) %collective-permute-start.9) | collective-permute-done | bytes 245792 | tf_op jit(solution)/shard_map/ppermute | solution.py:122
  94.0 3.9 %collective-permute-done.10 = bf16[3,160,256]{2,1,0:T(8,128)(2,1)S(1)} collective-permute-done((bf16[3,160,256]{2,1,0:T(8,128)(2,1)S(1)}, bf16[3,160,256]{2,1,0:T(8,128)(2,1)S(1)}, u32[]{:S(2)}, u32[]{:S(2)}) %collective-permute-start.10) | collective-permute-done | bytes 245792 | tf_op jit(solution)/shard_map/ppermute | solution.py:122
  99.3 3.9 %collective-permute-done.11 = bf16[3,160,256]{2,1,0:T(8,128)(2,1)S(1)} collective-permute-done((bf16[3,160,256]{2,1,0:T(8,128)(2,1)S(1)}, bf16[3,160,256]{2,1,0:T(8,128)(2,1)S(1)}, u32[]{:S(2)}, u32[]{:S(2)}) %collective-permute-start.11) | collective-permute-done | bytes 245792 | tf_op jit(solution)/shard_map/ppermute | solution.py:122
  103.2 8.0 %collective-permute-done.12 = bf16[3,160,256]{2,1,0:T(8,128)(2,1)S(1)} collective-permute-done((bf16[3,160,256]{2,1,0:T(8,128)(2,1)S(1)}, bf16[3,160,256]{2,1,0:T(8,128)(2,1)S(1)}, u32[]{:S(2)}, u32[]{:S(2)}) %collective-permute-start.12) | collective-permute-done | bytes 245792 | tf_op jit(solution)/shard_map/ppermute | solution.py:122
  111.3 5.2 %collective-permute-done.13 = bf16[3,160,256]{2,1,0:T(8,128)(2,1)S(1)} collective-permute-done((bf16[3,160,256]{2,1,0:T(8,128)(2,1)S(1)}, bf16[3,160,256]{2,1,0:T(8,128)(2,1)S(1)}, u32[]{:S(2)}, u32[]{:S(2)}) %collective-permute-start.13) | collective-permute-done | bytes 245792 | tf_op jit(solution)/shard_map/ppermute | solution.py:122
  117.3 4.6 %collective-permute-done.14 = bf16[3,160,256]{2,1,0:T(8,128)(2,1)S(1)} collective-permute-done((bf16[3,160,256]{2,1,0:T(8,128)(2,1)S(1)}, bf16[3,160,256]{2,1,0:T(8,128)(2,1)S(1)}, u32[]{:S(2)}, u32[]{:S(2)}) %collective-permute-start.14) | collective-permute-done | bytes 245792 | tf_op jit(solution)/shard_map/ppermute | solution.py:122
  121.9 4.8 %collective-permute-done.15 = bf16[3,160,256]{2,1,0:T(8,128)(2,1)S(1)} collective-permute-done((bf16[3,160,256]{2,1,0:T(8,128)(2,1)S(1)}, bf16[3,160,256]{2,1,0:T(8,128)(2,1)S(1)}, u32[]{:S(2)}, u32[]{:S(2)}) %collective-permute-start.15) | collective-permute-done | bytes 245792 | tf_op jit(solution)/shard_map/ppermute | solution.py:122
  126.7 1.9 %copy-done = bf16[1,1,3,160,4096]{4,3,2,1,0:T(8,128)(2,1)} copy-done((bf16[1,1,3,160,4096]{4,3,2,1,0:T(8,128)(2,1)}, bf16[1,1,3,160,4096]{4,3,2,1,0:T(8,128)(2,1)S(1)}, u32[]{:S(2)}) %copy-start) | copy-done | bytes 3932184
  (78 shorter events, 16.4 us)
Async XLA Ops:
  22.2 17.2 %copy-start.3 = (bf16[4,3,160,256]{3,2,1,0:T(8,128)(2,1)S(1)}, bf16[4,3,160,256]{3,2,1,0:T(8,128)(2,1)}, u32[]{:S(2)}) copy-start(bf16[4,3,160,256]{3,2,1,0:T(8,128)(2,1)} %get-tuple-element.11) | copy-start | bytes 2949124
  22.2 22.6 %copy-start.2 = (bf16[4,3,160,256]{3,2,1,0:T(8,128)(2,1)S(1)}, bf16[4,3,160,256]{3,2,1,0:T(8,128)(2,1)}, u32[]{:S(2)}) copy-start(bf16[4,3,160,256]{3,2,1,0:T(8,128)(2,1)} %get-tuple-element.12) | copy-start | bytes 2949124
  29.0 19.7 %copy-start.1 = (bf16[4,3,160,256]{3,2,1,0:T(8,128)(2,1)S(1)}, bf16[4,3,160,256]{3,2,1,0:T(8,128)(2,1)}, u32[]{:S(2)}) copy-start(bf16[4,3,160,256]{3,2,1,0:T(8,128)(2,1)} %get-tuple-element.13) | copy-start | bytes 2949124
  29.9 1.4 %collective-permute-start.16 = (f32[3,4096]{1,0:T(4,128)S(1)}, f32[3,4096]{1,0:T(4,128)S(1)}, u32[]{:S(2)}, u32[]{:S(2)}) collective-permute-start(f32[3,4096]{1,0:T(4,128)S(1)} %constant_dynamic-update-slice_fusion.4), channel_id=1, source_target_pairs={{0,1},{1,0},{2,3},{3,2},{4,5},{5,4},{6,7},{7,6},{8,9},{9,8},{10,11... | collective-permute-start | bytes 147464 | tf_op jit(solution)/shard_map/ppermute | solution.py:85
  31.3 6.4 %collective-permute-start.17 = (f32[3,4096]{1,0:T(4,128)S(1)}, f32[3,4096]{1,0:T(4,128)S(1)}, u32[]{:S(2)}, u32[]{:S(2)}) collective-permute-start(f32[3,4096]{1,0:T(4,128)S(1)} %add_dynamic-update-slice_fusion), channel_id=1, source_target_pairs={{0,2},{1,3},{2,0},{3,1},{4,6},{5,7},{6,4},{7,5},{8,10},{9,11},{10,... | collective-permute-start | bytes 147464 | tf_op jit(solution)/shard_map/ppermute | solution.py:85
  36.5 24.2 %collective-permute-start = (bf16[3,160,256]{2,1,0:T(8,128)(2,1)}, bf16[3,160,256]{2,1,0:T(8,128)(2,1)S(1)}, u32[]{:S(2)}, u32[]{:S(2)}) collective-permute-start(bf16[3,160,256]{2,1,0:T(8,128)(2,1)} %get-tuple-element.37), channel_id=1, source_target_pairs={{16,0},{17,1},{18,2},{19,3},{20,4},{21,5},{22,6},{23,7},{24,8},{25... | collective-permute-start | bytes 737288 | tf_op jit(solution)/shard_map/ppermute | solution.py:122
  37.8 4.3 %collective-permute-start.18 = (f32[3,4096]{1,0:T(4,128)S(1)}, f32[3,4096]{1,0:T(4,128)S(1)}, u32[]{:S(2)}, u32[]{:S(2)}) collective-permute-start(f32[3,4096]{1,0:T(4,128)S(1)} %add.174), channel_id=1, source_target_pairs={{0,4},{4,0},{8,12},{12,8},{1,5},{5,1},{9,13},{13,9},{2,6},{6,2},{1... | collective-permute-start | bytes 147464 | tf_op jit(solution)/shard_map/ppermute | solution.py:85
  40.4 22.2 %collective-permute-start.1 = (bf16[3,160,256]{2,1,0:T(8,128)(2,1)}, bf16[3,160,256]{2,1,0:T(8,128)(2,1)S(1)}, u32[]{:S(2)}, u32[]{:S(2)}) collective-permute-start(bf16[3,160,256]{2,1,0:T(8,128)(2,1)} %get-tuple-element.33), channel_id=1, source_target_pairs={{16,0},{17,1},{18,2},{19,3},{20,4},{21,5},{22,6},{23,7},{24,8},{25... | collective-permute-start | bytes 737288 | tf_op jit(solution)/shard_map/ppermute | solution.py:122
  42.1 5.2 %collective-permute-start.19 = (f32[3,4096]{1,0:T(4,128)S(1)}, f32[3,4096]{1,0:T(4,128)S(1)}, u32[]{:S(2)}, u32[]{:S(2)}) collective-permute-start(f32[3,4096]{1,0:T(4,128)S(1)} %add.175), channel_id=1, source_target_pairs={{0,8},{4,12},{8,0},{12,4},{1,9},{5,13},{9,1},{13,5},{2,10},{6,14},... | collective-permute-start | bytes 147464 | tf_op jit(solution)/shard_map/ppermute | solution.py:85
  45.8 19.6 %copy-start.6 = (bf16[3,160,256]{2,1,0:T(8,128)(2,1)S(1)}, bf16[3,160,256]{2,1,0:T(8,128)(2,1)}, u32[]{:S(2)}) copy-start(bf16[3,160,256]{2,1,0:T(8,128)(2,1)} %get-tuple-element.35) | copy-start | bytes 737284
  45.8 18.2 %collective-permute-start.2 = (bf16[3,160,256]{2,1,0:T(8,128)(2,1)}, bf16[3,160,256]{2,1,0:T(8,128)(2,1)S(1)}, u32[]{:S(2)}, u32[]{:S(2)}) collective-permute-start(bf16[3,160,256]{2,1,0:T(8,128)(2,1)} %get-tuple-element.29), channel_id=1, source_target_pairs={{16,0},{17,1},{18,2},{19,3},{20,4},{21,5},{22,6},{23,7},{24,8},{25... | collective-permute-start | bytes 737288 | tf_op jit(solution)/shard_map/ppermute | solution.py:122
  47.4 11.9 %collective-permute-start.20 = (f32[3,4096]{1,0:T(4,128)S(1)}, f32[3,4096]{1,0:T(4,128)S(1)}, u32[]{:S(2)}, u32[]{:S(2)}) collective-permute-start(f32[3,4096]{1,0:T(4,128)S(1)} %add.176), channel_id=1, source_target_pairs={{16,0},{17,1},{18,2},{19,3},{20,4},{21,5},{22,6},{23,7},{24,8},{25... | collective-permute-start | bytes 147464 | tf_op jit(solution)/shard_map/ppermute | solution.py:129
  48.7 21.9 %copy-start.7 = (bf16[3,160,256]{2,1,0:T(8,128)(2,1)S(1)}, bf16[3,160,256]{2,1,0:T(8,128)(2,1)}, u32[]{:S(2)}) copy-start(bf16[3,160,256]{2,1,0:T(8,128)(2,1)} %get-tuple-element.31) | copy-start | bytes 737284
  48.7 27.2 %copy-start.8 = (bf16[3,160,256]{2,1,0:T(8,128)(2,1)S(1)}, bf16[3,160,256]{2,1,0:T(8,128)(2,1)}, u32[]{:S(2)}) copy-start(bf16[3,160,256]{2,1,0:T(8,128)(2,1)} %get-tuple-element.27) | copy-start | bytes 737284
  49.6 13.0 %copy-start.10 = (bf16[3,160,256]{2,1,0:T(8,128)(2,1)S(1)}, bf16[3,160,256]{2,1,0:T(8,128)(2,1)}, u32[]{:S(2)}) copy-start(bf16[3,160,256]{2,1,0:T(8,128)(2,1)} %get-tuple-element.28) | copy-start | bytes 737284
  49.6 14.4 %copy-start.11 = (bf16[3,160,256]{2,1,0:T(8,128)(2,1)S(1)}, bf16[3,160,256]{2,1,0:T(8,128)(2,1)}, u32[]{:S(2)}) copy-start(bf16[3,160,256]{2,1,0:T(8,128)(2,1)} %get-tuple-element.24) | copy-start | bytes 737284
  49.6 31.6 %copy-start.9 = (bf16[3,160,256]{2,1,0:T(8,128)(2,1)S(1)}, bf16[3,160,256]{2,1,0:T(8,128)(2,1)}, u32[]{:S(2)}) copy-start(bf16[3,160,256]{2,1,0:T(8,128)(2,1)} %get-tuple-element.23) | copy-start | bytes 737284
  49.6 15.7 %collective-permute-start.3 = (bf16[3,160,256]{2,1,0:T(8,128)(2,1)}, bf16[3,160,256]{2,1,0:T(8,128)(2,1)S(1)}, u32[]{:S(2)}, u32[]{:S(2)}) collective-permute-start(bf16[3,160,256]{2,1,0:T(8,128)(2,1)} %get-tuple-element.25), channel_id=1, source_target_pairs={{16,0},{17,1},{18,2},{19,3},{20,4},{21,5},{22,6},{23,7},{24,8},{25... | collective-permute-start | bytes 737288 | tf_op jit(solution)/shard_map/ppermute | solution.py:122
  59.3 11.3 %collective-permute-start.4 = (bf16[3,160,256]{2,1,0:T(8,128)(2,1)}, bf16[3,160,256]{2,1,0:T(8,128)(2,1)S(1)}, u32[]{:S(2)}, u32[]{:S(2)}) collective-permute-start(bf16[3,160,256]{2,1,0:T(8,128)(2,1)} %get-tuple-element.36), channel_id=1, source_target_pairs={{16,1},{17,2},{18,3},{19,0},{20,5},{21,6},{22,7},{23,4},{24,9},{25... | collective-permute-start | bytes 737288 | tf_op jit(solution)/shard_map/ppermute | solution.py:122
  60.7 27.1 %copy-start.4 = (bf16[3,160,256]{2,1,0:T(8,128)(2,1)S(1)}, bf16[3,160,256]{2,1,0:T(8,128)(2,1)}, u32[]{:S(2)}) copy-start(bf16[3,160,256]{2,1,0:T(8,128)(2,1)} %get-tuple-element.30) | copy-start | bytes 737284
  60.7 32.0 %copy-start.5 = (bf16[3,160,256]{2,1,0:T(8,128)(2,1)S(1)}, bf16[3,160,256]{2,1,0:T(8,128)(2,1)}, u32[]{:S(2)}) copy-start(bf16[3,160,256]{2,1,0:T(8,128)(2,1)} %get-tuple-element.26) | copy-start | bytes 737284
  60.7 15.2 %collective-permute-start.5 = (bf16[3,160,256]{2,1,0:T(8,128)(2,1)}, bf16[3,160,256]{2,1,0:T(8,128)(2,1)S(1)}, u32[]{:S(2)}, u32[]{:S(2)}) collective-permute-start(bf16[3,160,256]{2,1,0:T(8,128)(2,1)} %get-tuple-element.32), channel_id=1, source_target_pairs={{16,1},{17,2},{18,3},{19,0},{20,5},{21,6},{22,7},{23,4},{24,9},{25... | collective-permute-start | bytes 737288 | tf_op jit(solution)/shard_map/ppermute | solution.py:122
  62.6 18.5 %collective-permute-start.6 = (bf16[3,160,256]{2,1,0:T(8,128)(2,1)S(1)}, bf16[3,160,256]{2,1,0:T(8,128)(2,1)S(1)}, u32[]{:S(2)}, u32[]{:S(2)}) collective-permute-start(bf16[3,160,256]{2,1,0:T(8,128)(2,1)S(1)} %copy-done.10), channel_id=1, source_target_pairs={{16,1},{17,2},{18,3},{19,0},{20,5},{21,6},{22,7},{23,4},{24,9},{25... | collective-permute-start | bytes 737288 | tf_op jit(solution)/shard_map/ppermute | solution.py:122
  64.0 22.4 %collective-permute-start.7 = (bf16[3,160,256]{2,1,0:T(8,128)(2,1)S(1)}, bf16[3,160,256]{2,1,0:T(8,128)(2,1)S(1)}, u32[]{:S(2)}, u32[]{:S(2)}) collective-permute-start(bf16[3,160,256]{2,1,0:T(8,128)(2,1)S(1)} %copy-done.11), channel_id=1, source_target_pairs={{16,1},{17,2},{18,3},{19,0},{20,5},{21,6},{22,7},{23,4},{24,9},{25... | collective-permute-start | bytes 737288 | tf_op jit(solution)/shard_map/ppermute | solution.py:122
  65.3 22.4 %collective-permute-start.8 = (bf16[3,160,256]{2,1,0:T(8,128)(2,1)S(1)}, bf16[3,160,256]{2,1,0:T(8,128)(2,1)S(1)}, u32[]{:S(2)}, u32[]{:S(2)}) collective-permute-start(bf16[3,160,256]{2,1,0:T(8,128)(2,1)S(1)} %copy-done.6), channel_id=1, source_target_pairs={{16,2},{17,3},{18,0},{19,1},{20,6},{21,7},{22,4},{23,5},{24,10},{2... | collective-permute-start | bytes 737288 | tf_op jit(solution)/shard_map/ppermute | solution.py:122
  70.6 22.0 %collective-permute-start.9 = (bf16[3,160,256]{2,1,0:T(8,128)(2,1)S(1)}, bf16[3,160,256]{2,1,0:T(8,128)(2,1)S(1)}, u32[]{:S(2)}, u32[]{:S(2)}) collective-permute-start(bf16[3,160,256]{2,1,0:T(8,128)(2,1)S(1)} %copy-done.7), channel_id=1, source_target_pairs={{16,2},{17,3},{18,0},{19,1},{20,6},{21,7},{22,4},{23,5},{24,10},{2... | collective-permute-start | bytes 737288 | tf_op jit(solution)/shard_map/ppermute | solution.py:122
  75.9 22.0 %collective-permute-start.10 = (bf16[3,160,256]{2,1,0:T(8,128)(2,1)S(1)}, bf16[3,160,256]{2,1,0:T(8,128)(2,1)S(1)}, u32[]{:S(2)}, u32[]{:S(2)}) collective-permute-start(bf16[3,160,256]{2,1,0:T(8,128)(2,1)S(1)} %copy-done.8), channel_id=1, source_target_pairs={{16,2},{17,3},{18,0},{19,1},{20,6},{21,7},{22,4},{23,5},{24,10},{2... | collective-permute-start | bytes 737288 | tf_op jit(solution)/shard_map/ppermute | solution.py:122
  81.2 22.0 %collective-permute-start.11 = (bf16[3,160,256]{2,1,0:T(8,128)(2,1)S(1)}, bf16[3,160,256]{2,1,0:T(8,128)(2,1)S(1)}, u32[]{:S(2)}, u32[]{:S(2)}) collective-permute-start(bf16[3,160,256]{2,1,0:T(8,128)(2,1)S(1)} %copy-done.9), channel_id=1, source_target_pairs={{16,2},{17,3},{18,0},{19,1},{20,6},{21,7},{22,4},{23,5},{24,10},{2... | collective-permute-start | bytes 737288 | tf_op jit(solution)/shard_map/ppermute | solution.py:122
  86.4 24.8 %collective-permute-start.12 = (bf16[3,160,256]{2,1,0:T(8,128)(2,1)S(1)}, bf16[3,160,256]{2,1,0:T(8,128)(2,1)S(1)}, u32[]{:S(2)}, u32[]{:S(2)}) collective-permute-start(bf16[3,160,256]{2,1,0:T(8,128)(2,1)S(1)} %get-tuple-element.34), channel_id=1, source_target_pairs={{16,3},{17,0},{18,1},{19,2},{20,7},{21,4},{22,5},{23,6},{24,11},{2... | collective-permute-start | bytes 737288 | tf_op jit(solution)/shard_map/ppermute | solution.py:122
  87.8 28.8 %collective-permute-start.13 = (bf16[3,160,256]{2,1,0:T(8,128)(2,1)S(1)}, bf16[3,160,256]{2,1,0:T(8,128)(2,1)S(1)}, u32[]{:S(2)}, u32[]{:S(2)}) collective-permute-start(bf16[3,160,256]{2,1,0:T(8,128)(2,1)S(1)} %copy-done.4), channel_id=1, source_target_pairs={{16,3},{17,0},{18,1},{19,2},{20,7},{21,4},{22,5},{23,6},{24,11},{2... | collective-permute-start | bytes 737288 | tf_op jit(solution)/shard_map/ppermute | solution.py:122
  92.7 29.1 %collective-permute-start.14 = (bf16[3,160,256]{2,1,0:T(8,128)(2,1)S(1)}, bf16[3,160,256]{2,1,0:T(8,128)(2,1)S(1)}, u32[]{:S(2)}, u32[]{:S(2)}) collective-permute-start(bf16[3,160,256]{2,1,0:T(8,128)(2,1)S(1)} %copy-done.5), channel_id=1, source_target_pairs={{16,3},{17,0},{18,1},{19,2},{20,7},{21,4},{22,5},{23,6},{24,11},{2... | collective-permute-start | bytes 737288 | tf_op jit(solution)/shard_map/ppermute | solution.py:122
  97.9 28.7 %collective-permute-start.15 = (bf16[3,160,256]{2,1,0:T(8,128)(2,1)S(1)}, bf16[3,160,256]{2,1,0:T(8,128)(2,1)S(1)}, u32[]{:S(2)}, u32[]{:S(2)}) collective-permute-start(bf16[3,160,256]{2,1,0:T(8,128)(2,1)S(1)} %get-tuple-element.22), channel_id=1, source_target_pairs={{16,3},{17,0},{18,1},{19,2},{20,7},{21,4},{22,5},{23,6},{24,11},{2... | collective-permute-start | bytes 737288 | tf_op jit(solution)/shard_map/ppermute | solution.py:122
  (4 other events, 22.5 us)

commit v3 on v2

--- a/solution.py
+++ b/solution.py
@@ -10,10 +10,12 @@
 
 HEAD_DIM = 128
 CHUNK_HEADS = 2
+DEPTH = 2
 NT = (((1,), (1,)), ((), ()))
 
 
-def grads_kernel(part_ref, pos_ref, q_ref, k_ref, v_ref, g_ref, out_ref, sum_ref, full_ref, *, parts):
+def grads_kernel(part_ref, pos_ref, q_ref, k_ref, v_ref, g_ref, *refs, parts):
+    out_refs, sum_ref, full_ref = refs[:parts], refs[parts], refs[parts + 1]
     length = q_ref.shape[0]
     half = length // 2
     window = -(-half // 128) * 128
@@ -44,37 +46,33 @@
             full_ref[i, b * half : (b + 1) * half, :] = grad[keep : keep + half].astype(jnp.bfloat16)
     sum_ref[...] = jnp.sum(full_ref[...].astype(jnp.float32), axis=1)
     part = part_ref[0]
-    for shift in range(parts):
+    for shift, out_ref in enumerate(out_refs):
         target = (part + shift) % parts
-        out_ref[shift] = full_ref[:, pl.ds(pl.multiple_of(target * rows, 16), rows), :]
+        out_ref[...] = full_ref[:, pl.ds(pl.multiple_of(target * rows, 16), rows), :]
 
 
-def chunk_grads(part, positions, query_rows, key_rows, value_rows, grad_rows, chunk, heads, parts):
+def chunk_grads(part, positions, query_rows, key_rows, value_rows, grad_rows, first, heads, parts):
     length = query_rows.shape[0]
     rows = length // parts
     width = heads * HEAD_DIM
 
     def column(h, part_ref):
-        return (0, chunk * heads + h)
+        return (0, first + h)
 
     in_block = pl.BlockSpec((length, HEAD_DIM), column)
     grid_spec = pltpu.PrefetchScalarGridSpec(
         num_scalar_prefetch=1,
         grid=(heads,),
         in_specs=[pl.BlockSpec((length, 1), lambda h, part_ref: (0, 0))] + [in_block] * 4,
-        out_specs=[
-            pl.BlockSpec((parts, 3, rows, HEAD_DIM), lambda h, part_ref: (0, 0, 0, h)),
-            pl.BlockSpec((3, HEAD_DIM), lambda h, part_ref: (0, h)),
-        ],
+        out_specs=[pl.BlockSpec((3, rows, HEAD_DIM), lambda h, part_ref: (0, 0, h))] * parts
+        + [pl.BlockSpec((3, HEAD_DIM), lambda h, part_ref: (0, h))],
         scratch_shapes=[pltpu.VMEM((3, length, HEAD_DIM), jnp.bfloat16)],
     )
     return pl.pallas_call(
         functools.partial(grads_kernel, parts=parts),
         grid_spec=grid_spec,
-        out_shape=[
-            jax.ShapeDtypeStruct((parts, 3, rows, width), jnp.bfloat16),
-            jax.ShapeDtypeStruct((3, width), jnp.float32),
-        ],
+        out_shape=[jax.ShapeDtypeStruct((3, rows, width), jnp.bfloat16)] * parts
+        + [jax.ShapeDtypeStruct((3, width), jnp.float32)],
     )(part, positions, query_rows, key_rows, value_rows, grad_rows)
 
 
@@ -99,9 +97,13 @@
     replicas = lax.axis_size("dp")
     part = lax.axis_index("mp")
     rows = length // parts
-    heads = min(CHUNK_HEADS, columns // HEAD_DIM)
-    width = heads * HEAD_DIM
-    chunk_count = columns // width
+    head_count = columns // HEAD_DIM
+    sizes = [1] if head_count > 1 else []
+    while sum(sizes) + 1 < head_count:
+        sizes.append(min(CHUNK_HEADS, head_count - 1 - sum(sizes)))
+    sizes.append(head_count - sum(sizes))
+    firsts = [sum(sizes[:c]) for c in range(len(sizes))]
+    chunk_count = len(sizes)
     part_arg = jnp.reshape(part, (1,)).astype(jnp.int32)
 
     def pairs(shift):
@@ -113,10 +115,12 @@
 
     arrived = [[None] * chunk_count for _ in range(parts)]
     sums = []
+    operands = (query_rows, key_rows, value_rows, grad_rows)
     for c in range(chunk_count):
-        grads, chunk_sums = chunk_grads(
-            part_arg, token_positions, query_rows, key_rows, value_rows, grad_rows, c, heads, parts
-        )
+        if c >= DEPTH:
+            tied = lax.optimization_barrier((operands, [arrived[shift][c - DEPTH] for shift in range(parts)]))
+            operands = tied[0]
+        *grads, chunk_sums = chunk_grads(part_arg, token_positions, *operands, firsts[c], sizes[c], parts)
         sums.append(chunk_sums)
         for shift in range(parts):
             arrived[shift][c] = lax.ppermute(grads[shift], ("section", "mp"), pairs(shift))
@@ -134,7 +138,7 @@
         source = (part - shift) % parts
         for c in range(chunk_count):
             received = lax.dynamic_update_slice_in_dim(
-                received, arrived[shift][c], source * columns + c * width, 2
+                received, arrived[shift][c], source * columns + firsts[c] * HEAD_DIM, 2
             )
     return (received[None, None], bias_grad[None])
 

time: 129 us -> 128 us (level)
  waiting for transfers between devices: 59.7 us -> 43.6 us
  local copies, waits for them, and re-layouts: 10.9 us -> 20.6 us
  starting transfers between devices: 29.9 us -> 33.9 us
  Pallas kernels: 26.7 us -> 28.2 us
    ppermute x16 -> x20, waiting for transfers between devices: 49.9 us -> 27.7 us  [per_device(): lax.ppermute(grads[shift], ('section', 'mp'), pairs(shift))]
    dynamic_update_slice x16 -> x20, local copies, waits for them, and re-layouts: 0.39 us -> 13.8 us  [per_device(): lax.dynamic_update_slice_in_dim(received, arrived[shift][c], source * col...]
    ppermute x4, waiting for transfers between devices: 1.56 us -> 11.1 us  [butterfly_sum(): lax.ppermute(value, axis, [(i, i ^ step) for i in range(count)])]
    ppermute x16 -> x20, starting transfers between devices: 20.9 us -> 26.1 us  [per_device(): lax.ppermute(grads[shift], ('section', 'mp'), pairs(shift))]
    squeeze x4 -> x0, local copies, waits for them, and re-layouts: 5.02 us -> none  [per_device(): grads[shift]]
    ppermute x1, waiting for transfers between devices: 8.17 us -> 4.76 us  [per_device(): lax.ppermute(totals, 'section', [(s + 1, s) for s in range(sections - 1)])]
    broadcast_in_dim x1, local copies, waits for them, and re-layouts: 0.46 us -> 2.4 us  [per_device(): return (received[None, None], bias_grad[None])]
    pallas_call x4 -> x5, Pallas kernels: 26.7 us -> 28.2 us  [chunk_grads(): pl.pallas_call(functools.partial(grads_kernel, parts=parts), grid_spec=gr...]
  transfers between devices with their start and end apart: 21 -> 25, of which waited for: 15 -> 8; matrix products, arithmetic and copies ran while one was open for 5% -> 14% of each run, Pallas kernels for 0% -> 19%
where the time goes in v3:
time: 128 us
  waiting for transfers between devices  43.6 us (34%)
  starting transfers between devices  33.9 us (26%)
  Pallas kernels  28.2 us (22%)
  local copies, waits for them, and re-layouts  20.6 us (16%)
    pallas_call x5, Pallas kernels, chunk_grads(): pl.pallas_call(functools.partial(grads_kernel, parts=parts), grid_spec=gr...  28.2 us
    ppermute x20, waiting for transfers between devices, per_device(): lax.ppermute(grads[shift], ('section', 'mp'), pairs(shift))  27.7 us
    ppermute x20, starting transfers between devices, per_device(): lax.ppermute(grads[shift], ('section', 'mp'), pairs(shift))  26.1 us
    dynamic_update_slice x20, local copies, waits for them, and re-layouts, per_device(): lax.dynamic_update_slice_in_dim(received, arrived[shift][c], source * col...  13.8 us
    ppermute x4, waiting for transfers between devices, butterfly_sum(): lax.ppermute(value, axis, [(i, i ^ step) for i in range(count)])  11.1 us
    ppermute x4, starting transfers between devices, butterfly_sum(): lax.ppermute(value, axis, [(i, i ^ step) for i in range(count)])  6.57 us
    ppermute x1, waiting for transfers between devices, per_device(): lax.ppermute(totals, 'section', [(s + 1, s) for s in range(sections - 1)])  4.76 us
  transfers between devices with their start and end apart: 25, of which 8 were waited for; matrix products, arithmetic and copies ran while one was open for 14% of the time, Pallas kernels for 19%

profile of v3, /device:TPU:0, one launch (start us, length us, event | category | flops | bytes accessed | tf_op | source)
XLA Modules:
  0.0 127.5 jit_solution(16322884430444186739)
XLA Ops:
  0.6 1.6 %copy.8.pos_ref = s32[640,1]{1,0:T(8,128)} copy(s32[640,1]{0,1:T(1,128)} %bitcast.68) | data formatting | bytes 5120 | tf_op jit(solution)/shard_map/reshape;squeeze | solution.py:93
  2.2 4.2 %shard_map.68 = (bf16[3,160,128]{2,1,0:T(8,128)(2,1)}, bf16[3,160,128]{2,1,0:T(8,128)(2,1)}, bf16[3,160,128]{2,1,0:T(8,128)(2,1)}, bf16[3,160,128]{2,1,0:T(8,128)(2,1)}, f32[3,128]{1,0:T(4,128)}) custom-call(s32[1]{0:T(128)} %bitcast.part_ref, s32[640,1]{1,0:T(8,128)} %copy.8.pos_ref, bf16[640,1024]{1,0:T(8,128)(2,1)} %bitcast.48, ...), custom_call_target="tpu_custom_call" | custom-call | tf_op jit(solution)/shard_map/pallas_call | solution.py:71
  6.4 1.4 %collective-permute-start = (bf16[3,160,128]{2,1,0:T(8,128)(2,1)}, bf16[3,160,128]{2,1,0:T(8,128)(2,1)S(1)}, u32[]{:S(2)}, u32[]{:S(2)}) collective-permute-start(bf16[3,160,128]{2,1,0:T(8,128)(2,1)} %get-tuple-element.39), channel_id=1, source_target_pairs={{16,0},{17,1},{18,2},{19,3},{20,4},{21,5},{22,6},{23,7},{24,8},{25... | collective-permute-start | bytes 368648 | tf_op jit(solution)/shard_map/ppermute | solution.py:126
  7.9 1.3 %collective-permute-start.2 = (bf16[3,160,128]{2,1,0:T(8,128)(2,1)}, bf16[3,160,128]{2,1,0:T(8,128)(2,1)S(1)}, u32[]{:S(2)}, u32[]{:S(2)}) collective-permute-start(bf16[3,160,128]{2,1,0:T(8,128)(2,1)} %get-tuple-element.41), channel_id=1, source_target_pairs={{16,1},{17,2},{18,3},{19,0},{20,5},{21,6},{22,7},{23,4},{24,9},{25... | collective-permute-start | bytes 368648 | tf_op jit(solution)/shard_map/ppermute | solution.py:126
  9.2 6.6 %shard_map.69 = (bf16[3,160,256]{2,1,0:T(8,128)(2,1)}, bf16[3,160,256]{2,1,0:T(8,128)(2,1)}, bf16[3,160,256]{2,1,0:T(8,128)(2,1)}, bf16[3,160,256]{2,1,0:T(8,128)(2,1)}, f32[3,256]{1,0:T(4,128)}) custom-call(s32[1]{0:T(128)} %bitcast.part_ref, s32[640,1]{1,0:T(8,128)} %copy.8.pos_ref, bf16[640,1024]{1,0:T(8,128)(2,1)} %bitcast.49, ...), custom_call_target="tpu_custom_call" | custom-call | tf_op jit(solution)/shard_map/pallas_call | solution.py:71
  15.8 1.3 %collective-permute-start.1 = (bf16[3,160,256]{2,1,0:T(8,128)(2,1)}, bf16[3,160,256]{2,1,0:T(8,128)(2,1)S(1)}, u32[]{:S(2)}, u32[]{:S(2)}) collective-permute-start(bf16[3,160,256]{2,1,0:T(8,128)(2,1)} %get-tuple-element.40), channel_id=1, source_target_pairs={{16,0},{17,1},{18,2},{19,3},{20,4},{21,5},{22,6},{23,7},{24,8},{25... | collective-permute-start | bytes 737288 | tf_op jit(solution)/shard_map/ppermute | solution.py:126
  17.1 1.3 %collective-permute-start.6 = (bf16[3,160,256]{2,1,0:T(8,128)(2,1)}, bf16[3,160,256]{2,1,0:T(8,128)(2,1)S(1)}, u32[]{:S(2)}, u32[]{:S(2)}) collective-permute-start(bf16[3,160,256]{2,1,0:T(8,128)(2,1)} %get-tuple-element.49), channel_id=1, source_target_pairs={{16,1},{17,2},{18,3},{19,0},{20,5},{21,6},{22,7},{23,4},{24,9},{25... | collective-permute-start | bytes 737288 | tf_op jit(solution)/shard_map/ppermute | solution.py:126
  18.4 1.3 %collective-permute-start.7 = (bf16[3,160,256]{2,1,0:T(8,128)(2,1)}, bf16[3,160,256]{2,1,0:T(8,128)(2,1)S(1)}, u32[]{:S(2)}, u32[]{:S(2)}) collective-permute-start(bf16[3,160,256]{2,1,0:T(8,128)(2,1)} %get-tuple-element.50), channel_id=1, source_target_pairs={{16,2},{17,3},{18,0},{19,1},{20,6},{21,7},{22,4},{23,5},{24,10},{2... | collective-permute-start | bytes 737288 | tf_op jit(solution)/shard_map/ppermute | solution.py:126
  19.7 1.3 %collective-permute-start.3 = (bf16[3,160,128]{2,1,0:T(8,128)(2,1)S(1)}, bf16[3,160,128]{2,1,0:T(8,128)(2,1)S(1)}, u32[]{:S(2)}, u32[]{:S(2)}) collective-permute-start(bf16[3,160,128]{2,1,0:T(8,128)(2,1)S(1)} %copy-done.3), channel_id=1, source_target_pairs={{16,2},{17,3},{18,0},{19,1},{20,6},{21,7},{22,4},{23,5},{24,10},{2... | collective-permute-start | bytes 368648 | tf_op jit(solution)/shard_map/ppermute | solution.py:126
  21.0 1.3 %collective-permute-start.4 = (bf16[3,160,128]{2,1,0:T(8,128)(2,1)S(1)}, bf16[3,160,128]{2,1,0:T(8,128)(2,1)S(1)}, u32[]{:S(2)}, u32[]{:S(2)}) collective-permute-start(bf16[3,160,128]{2,1,0:T(8,128)(2,1)S(1)} %copy-done.2), channel_id=1, source_target_pairs={{16,3},{17,0},{18,1},{19,2},{20,7},{21,4},{22,5},{23,6},{24,11},{2... | collective-permute-start | bytes 368648 | tf_op jit(solution)/shard_map/ppermute | solution.py:126
  23.2 19.1 %collective-permute-done.3 = bf16[3,160,128]{2,1,0:T(8,128)(2,1)S(1)} collective-permute-done((bf16[3,160,128]{2,1,0:T(8,128)(2,1)S(1)}, bf16[3,160,128]{2,1,0:T(8,128)(2,1)S(1)}, u32[]{:S(2)}, u32[]{:S(2)}) %collective-permute-start.3) | collective-permute-done | bytes 122912 | tf_op jit(solution)/shard_map/ppermute | solution.py:126
  43.6 6.6 %shard_map.70 = (bf16[3,160,256]{2,1,0:T(8,128)(2,1)}, bf16[3,160,256]{2,1,0:T(8,128)(2,1)}, bf16[3,160,256]{2,1,0:T(8,128)(2,1)}, bf16[3,160,256]{2,1,0:T(8,128)(2,1)}, f32[3,256]{1,0:T(4,128)}) custom-call(s32[1]{0:T(128)} %bitcast.part_ref, s32[640,1]{1,0:T(8,128)} %copy.8.pos_ref, bf16[640,1024]{1,0:T(8,128)(2,1)} %bitcast.50, ...), custom_call_target="tpu_custom_call" | custom-call | tf_op jit(solution)/shard_map/pallas_call | solution.py:71
  50.2 1.3 %collective-permute-start.5 = (bf16[3,160,256]{2,1,0:T(8,128)(2,1)}, bf16[3,160,256]{2,1,0:T(8,128)(2,1)S(1)}, u32[]{:S(2)}, u32[]{:S(2)}) collective-permute-start(bf16[3,160,256]{2,1,0:T(8,128)(2,1)} %get-tuple-element.48), channel_id=1, source_target_pairs={{16,0},{17,1},{18,2},{19,3},{20,4},{21,5},{22,6},{23,7},{24,8},{25... | collective-permute-start | bytes 737288 | tf_op jit(solution)/shard_map/ppermute | solution.py:126
  51.5 1.3 %collective-permute-start.10 = (bf16[3,160,256]{2,1,0:T(8,128)(2,1)}, bf16[3,160,256]{2,1,0:T(8,128)(2,1)S(1)}, u32[]{:S(2)}, u32[]{:S(2)}) collective-permute-start(bf16[3,160,256]{2,1,0:T(8,128)(2,1)} %get-tuple-element.57), channel_id=1, source_target_pairs={{16,1},{17,2},{18,3},{19,0},{20,5},{21,6},{22,7},{23,4},{24,9},{25... | collective-permute-start | bytes 737288 | tf_op jit(solution)/shard_map/ppermute | solution.py:126
  52.8 1.3 %collective-permute-start.11 = (bf16[3,160,256]{2,1,0:T(8,128)(2,1)}, bf16[3,160,256]{2,1,0:T(8,128)(2,1)S(1)}, u32[]{:S(2)}, u32[]{:S(2)}) collective-permute-start(bf16[3,160,256]{2,1,0:T(8,128)(2,1)} %get-tuple-element.58), channel_id=1, source_target_pairs={{16,2},{17,3},{18,0},{19,1},{20,6},{21,7},{22,4},{23,5},{24,10},{2... | collective-permute-start | bytes 737288 | tf_op jit(solution)/shard_map/ppermute | solution.py:126
  54.1 1.3 %collective-permute-start.12 = (bf16[3,160,256]{2,1,0:T(8,128)(2,1)}, bf16[3,160,256]{2,1,0:T(8,128)(2,1)S(1)}, u32[]{:S(2)}, u32[]{:S(2)}) collective-permute-start(bf16[3,160,256]{2,1,0:T(8,128)(2,1)} %get-tuple-element.59), channel_id=1, source_target_pairs={{16,3},{17,0},{18,1},{19,2},{20,7},{21,4},{22,5},{23,6},{24,11},{2... | collective-permute-start | bytes 737288 | tf_op jit(solution)/shard_map/ppermute | solution.py:126
  55.4 2.4 %broadcast_in_dim.50 = bf16[1,1,3,160,4096]{4,3,2,1,0:T(8,128)(2,1)} broadcast(bf16[]{:T(256)} %constant.78.clone.1), dimensions={} | broadcast | bytes 3932162 | tf_op jit(solution)/shard_map/broadcast_in_dim | solution.py:143
  58.5 6.6 %shard_map.71 = (bf16[3,160,256]{2,1,0:T(8,128)(2,1)}, bf16[3,160,256]{2,1,0:T(8,128)(2,1)}, bf16[3,160,256]{2,1,0:T(8,128)(2,1)}, bf16[3,160,256]{2,1,0:T(8,128)(2,1)}, f32[3,256]{1,0:T(4,128)}) custom-call(s32[1]{0:T(128)} %bitcast.part_ref, s32[640,1]{1,0:T(8,128)} %copy.8.pos_ref, bf16[640,1024]{1,0:T(8,128)(2,1)} %bitcast.51, ...), custom_call_target="tpu_custom_call" | custom-call | tf_op jit(solution)/shard_map/pallas_call | solution.py:71
  65.1 1.3 %collective-permute-start.9 = (bf16[3,160,256]{2,1,0:T(8,128)(2,1)}, bf16[3,160,256]{2,1,0:T(8,128)(2,1)S(1)}, u32[]{:S(2)}, u32[]{:S(2)}) collective-permute-start(bf16[3,160,256]{2,1,0:T(8,128)(2,1)} %get-tuple-element.56), channel_id=1, source_target_pairs={{16,0},{17,1},{18,2},{19,3},{20,4},{21,5},{22,6},{23,7},{24,8},{25... | collective-permute-start | bytes 737288 | tf_op jit(solution)/shard_map/ppermute | solution.py:126
  68.4 1.3 %collective-permute-start.16 = (bf16[3,160,256]{2,1,0:T(8,128)(2,1)}, bf16[3,160,256]{2,1,0:T(8,128)(2,1)S(1)}, u32[]{:S(2)}, u32[]{:S(2)}) collective-permute-start(bf16[3,160,256]{2,1,0:T(8,128)(2,1)} %get-tuple-element.67), channel_id=1, source_target_pairs={{16,2},{17,3},{18,0},{19,1},{20,6},{21,7},{22,4},{23,5},{24,10},{2... | collective-permute-start | bytes 737288 | tf_op jit(solution)/shard_map/ppermute | solution.py:126
  70.7 1.5 %collective-permute-start.18 = (bf16[3,160,256]{2,1,0:T(8,128)(2,1)}, bf16[3,160,256]{2,1,0:T(8,128)(2,1)S(1)}, u32[]{:S(2)}, u32[]{:S(2)}) collective-permute-start(bf16[3,160,256]{2,1,0:T(8,128)(2,1)} %get-tuple-element.69), channel_id=1, source_target_pairs={{16,3},{17,0},{18,1},{19,2},{20,7},{21,4},{22,5},{23,6},{24,11},{2... | collective-permute-start | bytes 737288 | tf_op jit(solution)/shard_map/ppermute | solution.py:126
  72.2 3.7 %collective-permute-done.12 = bf16[3,160,256]{2,1,0:T(8,128)(2,1)S(1)} collective-permute-done((bf16[3,160,256]{2,1,0:T(8,128)(2,1)}, bf16[3,160,256]{2,1,0:T(8,128)(2,1)S(1)}, u32[]{:S(2)}, u32[]{:S(2)}) %collective-permute-start.12) | collective-permute-done | bytes 245792 | tf_op jit(solution)/shard_map/ppermute | solution.py:126
  75.9 4.2 %shard_map.72 = (bf16[3,160,128]{2,1,0:T(8,128)(2,1)}, bf16[3,160,128]{2,1,0:T(8,128)(2,1)}, bf16[3,160,128]{2,1,0:T(8,128)(2,1)}, bf16[3,160,128]{2,1,0:T(8,128)(2,1)}, f32[3,128]{1,0:T(4,128)}) custom-call(s32[1]{0:T(128)} %bitcast.part_ref, s32[640,1]{1,0:T(8,128)} %copy.8.pos_ref, bf16[640,1024]{1,0:T(8,128)(2,1)} %bitcast.52, ...), custom_call_target="tpu_custom_call" | custom-call | tf_op jit(solution)/shard_map/pallas_call | solution.py:71
  82.1 2.0 %collective-permute-start.21 = (f32[3,4096]{1,0:T(4,128)S(1)}, f32[3,4096]{1,0:T(4,128)S(1)}, u32[]{:S(2)}, u32[]{:S(2)}) collective-permute-start(f32[3,4096]{1,0:T(4,128)S(1)} %add_dynamic-update-slice_fusion), channel_id=1, source_target_pairs={{0,2},{1,3},{2,0},{3,1},{4,6},{5,7},{6,4},{7,5},{8,10},{9,11},{10,... | collective-permute-start | bytes 147464 | tf_op jit(solution)/shard_map/ppermute | solution.py:83
  84.8 8.4 %collective-permute-done.21 = f32[3,4096]{1,0:T(4,128)S(1)} collective-permute-done((f32[3,4096]{1,0:T(4,128)S(1)}, f32[3,4096]{1,0:T(4,128)S(1)}, u32[]{:S(2)}, u32[]{:S(2)}) %collective-permute-start.21) | collective-permute-done | bytes 49184 | tf_op jit(solution)/shard_map/ppermute | solution.py:83
  94.5 1.3 %collective-permute-start.15 = (bf16[3,160,128]{2,1,0:T(8,128)(2,1)}, bf16[3,160,128]{2,1,0:T(8,128)(2,1)S(1)}, u32[]{:S(2)}, u32[]{:S(2)}) collective-permute-start(bf16[3,160,128]{2,1,0:T(8,128)(2,1)} %get-tuple-element.66), channel_id=1, source_target_pairs={{16,1},{17,2},{18,3},{19,0},{20,5},{21,6},{22,7},{23,4},{24,9},{25... | collective-permute-start | bytes 368648 | tf_op jit(solution)/shard_map/ppermute | solution.py:126
  96.5 3.9 %collective-permute-done.13 = bf16[3,160,128]{2,1,0:T(8,128)(2,1)S(1)} collective-permute-done((bf16[3,160,128]{2,1,0:T(8,128)(2,1)}, bf16[3,160,128]{2,1,0:T(8,128)(2,1)S(1)}, u32[]{:S(2)}, u32[]{:S(2)}) %collective-permute-start.13) | collective-permute-done | bytes 122912 | tf_op jit(solution)/shard_map/ppermute | solution.py:126
  106.5 1.9 %collective-permute-start.22 = (f32[3,4096]{1,0:T(4,128)S(1)}, f32[3,4096]{1,0:T(4,128)S(1)}, u32[]{:S(2)}, u32[]{:S(2)}) collective-permute-start(f32[3,4096]{1,0:T(4,128)S(1)} %add.214), channel_id=1, source_target_pairs={{0,4},{4,0},{8,12},{12,8},{1,5},{5,1},{9,13},{13,9},{2,6},{6,2},{1... | collective-permute-start | bytes 147464 | tf_op jit(solution)/shard_map/ppermute | solution.py:83
  114.5 2.6 %collective-permute-start.23 = (f32[3,4096]{1,0:T(4,128)S(1)}, f32[3,4096]{1,0:T(4,128)S(1)}, u32[]{:S(2)}, u32[]{:S(2)}) collective-permute-start(f32[3,4096]{1,0:T(4,128)S(1)} %add.215), channel_id=1, source_target_pairs={{0,8},{4,12},{8,0},{12,4},{1,9},{5,13},{9,1},{13,5},{2,10},{6,14},... | collective-permute-start | bytes 147464 | tf_op jit(solution)/shard_map/ppermute | solution.py:83
  117.9 2.2 %collective-permute-done.23 = f32[3,4096]{1,0:T(4,128)S(1)} collective-permute-done((f32[3,4096]{1,0:T(4,128)S(1)}, f32[3,4096]{1,0:T(4,128)S(1)}, u32[]{:S(2)}, u32[]{:S(2)}) %collective-permute-start.23) | collective-permute-done | bytes 49184 | tf_op jit(solution)/shard_map/ppermute | solution.py:83
  120.1 1.3 %collective-permute-start.24 = (f32[3,4096]{1,0:T(4,128)S(1)}, f32[3,4096]{1,0:T(4,128)S(1)}, u32[]{:S(2)}, u32[]{:S(2)}) collective-permute-start(f32[3,4096]{1,0:T(4,128)S(1)} %add.216), channel_id=1, source_target_pairs={{16,0},{17,1},{18,2},{19,3},{20,4},{21,5},{22,6},{23,7},{24,8},{25... | collective-permute-start | bytes 147464 | tf_op jit(solution)/shard_map/ppermute | solution.py:133
  122.1 4.8 %collective-permute-done.24 = f32[3,4096]{1,0:T(4,128)S(1)} collective-permute-done((f32[3,4096]{1,0:T(4,128)S(1)}, f32[3,4096]{1,0:T(4,128)S(1)}, u32[]{:S(2)}, u32[]{:S(2)}) %collective-permute-start.24) | collective-permute-done | bytes 49184 | tf_op jit(solution)/shard_map/ppermute | solution.py:133
  (66 shorter events, 24.8 us)
Async XLA Ops:
  6.4 13.3 %copy-start.3 = (bf16[3,160,128]{2,1,0:T(8,128)(2,1)S(1)}, bf16[3,160,128]{2,1,0:T(8,128)(2,1)}, u32[]{:S(2)}) copy-start(bf16[3,160,128]{2,1,0:T(8,128)(2,1)} %get-tuple-element.42) | copy-start | bytes 368644
  6.4 14.6 %copy-start.2 = (bf16[3,160,128]{2,1,0:T(8,128)(2,1)S(1)}, bf16[3,160,128]{2,1,0:T(8,128)(2,1)}, u32[]{:S(2)}) copy-start(bf16[3,160,128]{2,1,0:T(8,128)(2,1)} %get-tuple-element.43) | copy-start | bytes 368644
  6.4 15.9 %copy-start.1 = (f32[3,128]{1,0:T(4,128)S(1)}, f32[3,128]{1,0:T(4,128)}, u32[]{:S(2)}) copy-start(f32[3,128]{1,0:T(4,128)} %get-tuple-element.71) | copy-start | bytes 4612
  6.4 13.2 %collective-permute-start = (bf16[3,160,128]{2,1,0:T(8,128)(2,1)}, bf16[3,160,128]{2,1,0:T(8,128)(2,1)S(1)}, u32[]{:S(2)}, u32[]{:S(2)}) collective-permute-start(bf16[3,160,128]{2,1,0:T(8,128)(2,1)} %get-tuple-element.39), channel_id=1, source_target_pairs={{16,0},{17,1},{18,2},{19,3},{20,4},{21,5},{22,6},{23,7},{24,8},{25... | collective-permute-start | bytes 368648 | tf_op jit(solution)/shard_map/ppermute | solution.py:126
  7.9 13.1 %collective-permute-start.2 = (bf16[3,160,128]{2,1,0:T(8,128)(2,1)}, bf16[3,160,128]{2,1,0:T(8,128)(2,1)S(1)}, u32[]{:S(2)}, u32[]{:S(2)}) collective-permute-start(bf16[3,160,128]{2,1,0:T(8,128)(2,1)} %get-tuple-element.41), channel_id=1, source_target_pairs={{16,1},{17,2},{18,3},{19,0},{20,5},{21,6},{22,7},{23,4},{24,9},{25... | collective-permute-start | bytes 368648 | tf_op jit(solution)/shard_map/ppermute | solution.py:126
  15.8 35.7 %collective-permute-start.1 = (bf16[3,160,256]{2,1,0:T(8,128)(2,1)}, bf16[3,160,256]{2,1,0:T(8,128)(2,1)S(1)}, u32[]{:S(2)}, u32[]{:S(2)}) collective-permute-start(bf16[3,160,256]{2,1,0:T(8,128)(2,1)} %get-tuple-element.40), channel_id=1, source_target_pairs={{16,0},{17,1},{18,2},{19,3},{20,4},{21,5},{22,6},{23,7},{24,8},{25... | collective-permute-start | bytes 737288 | tf_op jit(solution)/shard_map/ppermute | solution.py:126
  17.1 35.8 %collective-permute-start.6 = (bf16[3,160,256]{2,1,0:T(8,128)(2,1)}, bf16[3,160,256]{2,1,0:T(8,128)(2,1)S(1)}, u32[]{:S(2)}, u32[]{:S(2)}) collective-permute-start(bf16[3,160,256]{2,1,0:T(8,128)(2,1)} %get-tuple-element.49), channel_id=1, source_target_pairs={{16,1},{17,2},{18,3},{19,0},{20,5},{21,6},{22,7},{23,4},{24,9},{25... | collective-permute-start | bytes 737288 | tf_op jit(solution)/shard_map/ppermute | solution.py:126
  18.4 35.8 %collective-permute-start.7 = (bf16[3,160,256]{2,1,0:T(8,128)(2,1)}, bf16[3,160,256]{2,1,0:T(8,128)(2,1)S(1)}, u32[]{:S(2)}, u32[]{:S(2)}) collective-permute-start(bf16[3,160,256]{2,1,0:T(8,128)(2,1)} %get-tuple-element.50), channel_id=1, source_target_pairs={{16,2},{17,3},{18,0},{19,1},{20,6},{21,7},{22,4},{23,5},{24,10},{2... | collective-permute-start | bytes 737288 | tf_op jit(solution)/shard_map/ppermute | solution.py:126
  19.7 22.6 %collective-permute-start.3 = (bf16[3,160,128]{2,1,0:T(8,128)(2,1)S(1)}, bf16[3,160,128]{2,1,0:T(8,128)(2,1)S(1)}, u32[]{:S(2)}, u32[]{:S(2)}) collective-permute-start(bf16[3,160,128]{2,1,0:T(8,128)(2,1)S(1)} %copy-done.3), channel_id=1, source_target_pairs={{16,2},{17,3},{18,0},{19,1},{20,6},{21,7},{22,4},{23,5},{24,10},{2... | collective-permute-start | bytes 368648 | tf_op jit(solution)/shard_map/ppermute | solution.py:126
  21.0 22.6 %collective-permute-start.4 = (bf16[3,160,128]{2,1,0:T(8,128)(2,1)S(1)}, bf16[3,160,128]{2,1,0:T(8,128)(2,1)S(1)}, u32[]{:S(2)}, u32[]{:S(2)}) collective-permute-start(bf16[3,160,128]{2,1,0:T(8,128)(2,1)S(1)} %copy-done.2), channel_id=1, source_target_pairs={{16,3},{17,0},{18,1},{19,2},{20,7},{21,4},{22,5},{23,6},{24,11},{2... | collective-permute-start | bytes 368648 | tf_op jit(solution)/shard_map/ppermute | solution.py:126
  42.3 16.2 %collective-permute-start.8 = (bf16[3,160,256]{2,1,0:T(8,128)(2,1)}, bf16[3,160,256]{2,1,0:T(8,128)(2,1)S(1)}, u32[]{:S(2)}, u32[]{:S(2)}) collective-permute-start(bf16[3,160,256]{2,1,0:T(8,128)(2,1)} %get-tuple-element.51), channel_id=1, source_target_pairs={{16,3},{17,0},{18,1},{19,2},{20,7},{21,4},{22,5},{23,6},{24,11},{2... | collective-permute-start | bytes 737288 | tf_op jit(solution)/shard_map/ppermute | solution.py:126
  50.2 8.3 %copy-start = (f32[3,256]{1,0:T(4,128)S(1)}, f32[3,256]{1,0:T(4,128)}, u32[]{:S(2)}) copy-start(f32[3,256]{1,0:T(4,128)} %get-tuple-element.73) | copy-start | bytes 9220
  50.2 16.9 %collective-permute-start.5 = (bf16[3,160,256]{2,1,0:T(8,128)(2,1)}, bf16[3,160,256]{2,1,0:T(8,128)(2,1)S(1)}, u32[]{:S(2)}, u32[]{:S(2)}) collective-permute-start(bf16[3,160,256]{2,1,0:T(8,128)(2,1)} %get-tuple-element.48), channel_id=1, source_target_pairs={{16,0},{17,1},{18,2},{19,3},{20,4},{21,5},{22,6},{23,7},{24,8},{25... | collective-permute-start | bytes 737288 | tf_op jit(solution)/shard_map/ppermute | solution.py:126
  51.5 16.9 %collective-permute-start.10 = (bf16[3,160,256]{2,1,0:T(8,128)(2,1)}, bf16[3,160,256]{2,1,0:T(8,128)(2,1)S(1)}, u32[]{:S(2)}, u32[]{:S(2)}) collective-permute-start(bf16[3,160,256]{2,1,0:T(8,128)(2,1)} %get-tuple-element.57), channel_id=1, source_target_pairs={{16,1},{17,2},{18,3},{19,0},{20,5},{21,6},{22,7},{23,4},{24,9},{25... | collective-permute-start | bytes 737288 | tf_op jit(solution)/shard_map/ppermute | solution.py:126
  52.8 17.9 %collective-permute-start.11 = (bf16[3,160,256]{2,1,0:T(8,128)(2,1)}, bf16[3,160,256]{2,1,0:T(8,128)(2,1)S(1)}, u32[]{:S(2)}, u32[]{:S(2)}) collective-permute-start(bf16[3,160,256]{2,1,0:T(8,128)(2,1)} %get-tuple-element.58), channel_id=1, source_target_pairs={{16,2},{17,3},{18,0},{19,1},{20,6},{21,7},{22,4},{23,5},{24,10},{2... | collective-permute-start | bytes 737288 | tf_op jit(solution)/shard_map/ppermute | solution.py:126
  54.1 21.7 %collective-permute-start.12 = (bf16[3,160,256]{2,1,0:T(8,128)(2,1)}, bf16[3,160,256]{2,1,0:T(8,128)(2,1)S(1)}, u32[]{:S(2)}, u32[]{:S(2)}) collective-permute-start(bf16[3,160,256]{2,1,0:T(8,128)(2,1)} %get-tuple-element.59), channel_id=1, source_target_pairs={{16,3},{17,0},{18,1},{19,2},{20,7},{21,4},{22,5},{23,6},{24,11},{2... | collective-permute-start | bytes 737288 | tf_op jit(solution)/shard_map/ppermute | solution.py:126
  65.1 29.4 %collective-permute-start.9 = (bf16[3,160,256]{2,1,0:T(8,128)(2,1)}, bf16[3,160,256]{2,1,0:T(8,128)(2,1)S(1)}, u32[]{:S(2)}, u32[]{:S(2)}) collective-permute-start(bf16[3,160,256]{2,1,0:T(8,128)(2,1)} %get-tuple-element.56), channel_id=1, source_target_pairs={{16,0},{17,1},{18,2},{19,3},{20,4},{21,5},{22,6},{23,7},{24,8},{25... | collective-permute-start | bytes 737288 | tf_op jit(solution)/shard_map/ppermute | solution.py:126
  67.1 37.3 %collective-permute-start.14 = (bf16[3,160,256]{2,1,0:T(8,128)(2,1)}, bf16[3,160,256]{2,1,0:T(8,128)(2,1)S(1)}, u32[]{:S(2)}, u32[]{:S(2)}) collective-permute-start(bf16[3,160,256]{2,1,0:T(8,128)(2,1)} %get-tuple-element.65), channel_id=1, source_target_pairs={{16,1},{17,2},{18,3},{19,0},{20,5},{21,6},{22,7},{23,4},{24,9},{25... | collective-permute-start | bytes 737288 | tf_op jit(solution)/shard_map/ppermute | solution.py:126
  68.4 42.7 %collective-permute-start.16 = (bf16[3,160,256]{2,1,0:T(8,128)(2,1)}, bf16[3,160,256]{2,1,0:T(8,128)(2,1)S(1)}, u32[]{:S(2)}, u32[]{:S(2)}) collective-permute-start(bf16[3,160,256]{2,1,0:T(8,128)(2,1)} %get-tuple-element.67), channel_id=1, source_target_pairs={{16,2},{17,3},{18,0},{19,1},{20,6},{21,7},{22,4},{23,5},{24,10},{2... | collective-permute-start | bytes 737288 | tf_op jit(solution)/shard_map/ppermute | solution.py:126
  70.7 46.4 %collective-permute-start.18 = (bf16[3,160,256]{2,1,0:T(8,128)(2,1)}, bf16[3,160,256]{2,1,0:T(8,128)(2,1)S(1)}, u32[]{:S(2)}, u32[]{:S(2)}) collective-permute-start(bf16[3,160,256]{2,1,0:T(8,128)(2,1)} %get-tuple-element.69), channel_id=1, source_target_pairs={{16,3},{17,0},{18,1},{19,2},{20,7},{21,4},{22,5},{23,6},{24,11},{2... | collective-permute-start | bytes 737288 | tf_op jit(solution)/shard_map/ppermute | solution.py:126
  80.8 1.3 %collective-permute-start.20 = (f32[3,4096]{1,0:T(4,128)S(1)}, f32[3,4096]{1,0:T(4,128)S(1)}, u32[]{:S(2)}, u32[]{:S(2)}) collective-permute-start(f32[3,4096]{1,0:T(4,128)S(1)} %constant_dynamic-update-slice_fusion.5), channel_id=1, source_target_pairs={{0,1},{1,0},{2,3},{3,2},{4,5},{5,4},{6,7},{7,6},{8,9},{9,8},{10,11... | collective-permute-start | bytes 147464 | tf_op jit(solution)/shard_map/ppermute | solution.py:83
  82.1 11.1 %collective-permute-start.21 = (f32[3,4096]{1,0:T(4,128)S(1)}, f32[3,4096]{1,0:T(4,128)S(1)}, u32[]{:S(2)}, u32[]{:S(2)}) collective-permute-start(f32[3,4096]{1,0:T(4,128)S(1)} %add_dynamic-update-slice_fusion), channel_id=1, source_target_pairs={{0,2},{1,3},{2,0},{3,1},{4,6},{5,7},{6,4},{7,5},{8,10},{9,11},{10,... | collective-permute-start | bytes 147464 | tf_op jit(solution)/shard_map/ppermute | solution.py:83
  93.2 7.2 %collective-permute-start.13 = (bf16[3,160,128]{2,1,0:T(8,128)(2,1)}, bf16[3,160,128]{2,1,0:T(8,128)(2,1)S(1)}, u32[]{:S(2)}, u32[]{:S(2)}) collective-permute-start(bf16[3,160,128]{2,1,0:T(8,128)(2,1)} %get-tuple-element.64), channel_id=1, source_target_pairs={{16,0},{17,1},{18,2},{19,3},{20,4},{21,5},{22,6},{23,7},{24,8},{25... | collective-permute-start | bytes 368648 | tf_op jit(solution)/shard_map/ppermute | solution.py:126
  94.5 11.9 %collective-permute-start.15 = (bf16[3,160,128]{2,1,0:T(8,128)(2,1)}, bf16[3,160,128]{2,1,0:T(8,128)(2,1)S(1)}, u32[]{:S(2)}, u32[]{:S(2)}) collective-permute-start(bf16[3,160,128]{2,1,0:T(8,128)(2,1)} %get-tuple-element.66), channel_id=1, source_target_pairs={{16,1},{17,2},{18,3},{19,0},{20,5},{21,6},{22,7},{23,4},{24,9},{25... | collective-permute-start | bytes 368648 | tf_op jit(solution)/shard_map/ppermute | solution.py:126
  100.4 11.4 %collective-permute-start.17 = (bf16[3,160,128]{2,1,0:T(8,128)(2,1)}, bf16[3,160,128]{2,1,0:T(8,128)(2,1)S(1)}, u32[]{:S(2)}, u32[]{:S(2)}) collective-permute-start(bf16[3,160,128]{2,1,0:T(8,128)(2,1)} %get-tuple-element.68), channel_id=1, source_target_pairs={{16,2},{17,3},{18,0},{19,1},{20,6},{21,7},{22,4},{23,5},{24,10},{2... | collective-permute-start | bytes 368648 | tf_op jit(solution)/shard_map/ppermute | solution.py:126
  104.4 17.0 %collective-permute-start.19 = (bf16[3,160,128]{2,1,0:T(8,128)(2,1)}, bf16[3,160,128]{2,1,0:T(8,128)(2,1)S(1)}, u32[]{:S(2)}, u32[]{:S(2)}) collective-permute-start(bf16[3,160,128]{2,1,0:T(8,128)(2,1)} %get-tuple-element.70), channel_id=1, source_target_pairs={{16,3},{17,0},{18,1},{19,2},{20,7},{21,4},{22,5},{23,6},{24,11},{2... | collective-permute-start | bytes 368648 | tf_op jit(solution)/shard_map/ppermute | solution.py:126
  106.5 8.1 %collective-permute-start.22 = (f32[3,4096]{1,0:T(4,128)S(1)}, f32[3,4096]{1,0:T(4,128)S(1)}, u32[]{:S(2)}, u32[]{:S(2)}) collective-permute-start(f32[3,4096]{1,0:T(4,128)S(1)} %add.214), channel_id=1, source_target_pairs={{0,4},{4,0},{8,12},{12,8},{1,5},{5,1},{9,13},{13,9},{2,6},{6,2},{1... | collective-permute-start | bytes 147464 | tf_op jit(solution)/shard_map/ppermute | solution.py:83
  114.5 5.6 %collective-permute-start.23 = (f32[3,4096]{1,0:T(4,128)S(1)}, f32[3,4096]{1,0:T(4,128)S(1)}, u32[]{:S(2)}, u32[]{:S(2)}) collective-permute-start(f32[3,4096]{1,0:T(4,128)S(1)} %add.215), channel_id=1, source_target_pairs={{0,8},{4,12},{8,0},{12,4},{1,9},{5,13},{9,1},{13,5},{2,10},{6,14},... | collective-permute-start | bytes 147464 | tf_op jit(solution)/shard_map/ppermute | solution.py:83
  120.1 6.7 %collective-permute-start.24 = (f32[3,4096]{1,0:T(4,128)S(1)}, f32[3,4096]{1,0:T(4,128)S(1)}, u32[]{:S(2)}, u32[]{:S(2)}) collective-permute-start(f32[3,4096]{1,0:T(4,128)S(1)} %add.216), channel_id=1, source_target_pairs={{16,0},{17,1},{18,2},{19,3},{20,4},{21,5},{22,6},{23,7},{24,8},{25... | collective-permute-start | bytes 147464 | tf_op jit(solution)/shard_map/ppermute | solution.py:133

commit v4 on v3

--- a/solution.py
+++ b/solution.py
@@ -9,7 +9,6 @@
 from jax.sharding import PartitionSpec as P
 
 HEAD_DIM = 128
-CHUNK_HEADS = 2
 DEPTH = 2
 NT = (((1,), (1,)), ((), ()))
 
@@ -98,10 +97,9 @@
     part = lax.axis_index("mp")
     rows = length // parts
     head_count = columns // HEAD_DIM
-    sizes = [1] if head_count > 1 else []
-    while sum(sizes) + 1 < head_count:
-        sizes.append(min(CHUNK_HEADS, head_count - 1 - sum(sizes)))
-    sizes.append(head_count - sum(sizes))
+    sizes = [1]
+    while sum(sizes) < head_count:
+        sizes.append(min(2 * sizes[-1] + 1, head_count - sum(sizes)))
     firsts = [sum(sizes[:c]) for c in range(len(sizes))]
     chunk_count = len(sizes)
     part_arg = jnp.reshape(part, (1,)).astype(jnp.int32)
@@ -126,11 +124,14 @@
             arrived[shift][c] = lax.ppermute(grads[shift], ("section", "mp"), pairs(shift))
 
     own = jnp.concatenate(sums, axis=1)
-    slots = lax.dynamic_update_slice_in_dim(
-        jnp.zeros((3, columns * parts), jnp.float32), own, part * columns, 1
-    )
-    totals = butterfly_sum(butterfly_sum(slots, "mp"), "dp")
-    totals = lax.ppermute(totals, "section", [(s + 1, s) for s in range(sections - 1)])
+    if chunk_count > 1:
+        own = lax.optimization_barrier((own, [arrived[shift][-2] for shift in range(parts)]))[0]
+    own = butterfly_sum(own, "dp")
+    totals = jnp.zeros((3, columns * parts), jnp.float32)
+    for shift in range(parts):
+        source = (part - shift) % parts
+        piece = lax.ppermute(own, ("section", "mp"), pairs(shift))
+        totals = lax.dynamic_update_slice_in_dim(totals, piece, source * columns, 1)
     bias_grad = totals / math.sqrt(replicas * length)
 
     received = jnp.zeros((3, rows, columns * parts), jnp.bfloat16)

time: 128 us -> 149 us (1.16)
  waiting for transfers between devices: 43.6 us -> 92 us
  local copies, waits for them, and re-layouts: 20.6 us -> 5.46 us
  starting transfers between devices: 33.9 us -> 25.1 us
  Pallas kernels: 28.2 us -> 24.1 us
    ppermute x1 -> x4, waiting for transfers between devices: 4.76 us -> 49.7 us  [per_device(): piece = lax.ppermute(own, ('section', 'mp'), pairs(shift))]
    ppermute x20 -> x12, waiting for transfers between devices: 27.7 us -> 40.8 us  [per_device(): lax.ppermute(grads[shift], ('section', 'mp'), pairs(shift))]
    dynamic_update_slice x20 -> x12, local copies, waits for them, and re-layouts: 13.8 us -> 0.75 us  [per_device(): lax.dynamic_update_slice_in_dim(received, arrived[shift][c], source * col...]
    ppermute x20 -> x12, starting transfers between devices: 26.1 us -> 15.6 us  [per_device(): lax.ppermute(grads[shift], ('section', 'mp'), pairs(shift))]
    ppermute x4 -> x2, waiting for transfers between devices: 11.1 us -> 1.51 us  [butterfly_sum(): lax.ppermute(value, axis, [(i, i ^ step) for i in range(count)])]
    pallas_call x5 -> x3, Pallas kernels: 28.2 us -> 24.1 us  [chunk_grads(): pl.pallas_call(functools.partial(grads_kernel, parts=parts), grid_spec=gr...]
    ppermute x1 -> x4, starting transfers between devices: 1.29 us -> 5.12 us  [per_device(): piece = lax.ppermute(own, ('section', 'mp'), pairs(shift))]
    ppermute x4 -> x2, starting transfers between devices: 6.57 us -> 4.41 us  [butterfly_sum(): lax.ppermute(value, axis, [(i, i ^ step) for i in range(count)])]
  transfers between devices with their start and end apart: 25 -> 18, of which waited for: 8 -> 7; matrix products, arithmetic and copies ran while one was open for 14% -> 2% of each run, Pallas kernels for 19% -> 13%
where the time goes in v4:
time: 149 us
  waiting for transfers between devices  92 us (62%)
  starting transfers between devices  25.1 us (17%)
  Pallas kernels  24.1 us (16%)
  local copies, waits for them, and re-layouts  5.46 us (4%)
    ppermute x4, waiting for transfers between devices, per_device(): piece = lax.ppermute(own, ('section', 'mp'), pairs(shift))  49.7 us
    ppermute x12, waiting for transfers between devices, per_device(): lax.ppermute(grads[shift], ('section', 'mp'), pairs(shift))  40.8 us
    pallas_call x3, Pallas kernels, chunk_grads(): pl.pallas_call(functools.partial(grads_kernel, parts=parts), grid_spec=gr...  24.1 us
    ppermute x12, starting transfers between devices, per_device(): lax.ppermute(grads[shift], ('section', 'mp'), pairs(shift))  15.6 us
    ppermute x4, starting transfers between devices, per_device(): piece = lax.ppermute(own, ('section', 'mp'), pairs(shift))  5.12 us
    ppermute x2, starting transfers between devices, butterfly_sum(): lax.ppermute(value, axis, [(i, i ^ step) for i in range(count)])  4.41 us
  transfers between devices with their start and end apart: 18, of which 7 were waited for; matrix products, arithmetic and copies ran while one was open for 2% of the time, Pallas kernels for 13%

profile of v4, /device:TPU:0, one launch (start us, length us, event | category | flops | bytes accessed | tf_op | source)
XLA Modules:
  0.0 148.5 jit_solution(2276419189233785961)
XLA Ops:
  0.6 1.6 %copy.7.pos_ref = s32[640,1]{1,0:T(8,128)} copy(s32[640,1]{0,1:T(1,128)} %bitcast.42) | data formatting | bytes 5120 | tf_op jit(solution)/shard_map/reshape;squeeze | solution.py:92
  2.2 4.2 %shard_map.68 = (bf16[3,160,128]{2,1,0:T(8,128)(2,1)}, bf16[3,160,128]{2,1,0:T(8,128)(2,1)}, bf16[3,160,128]{2,1,0:T(8,128)(2,1)}, bf16[3,160,128]{2,1,0:T(8,128)(2,1)}, f32[3,128]{1,0:T(4,128)}) custom-call(s32[1]{0:T(128)} %bitcast.part_ref, s32[640,1]{1,0:T(8,128)} %copy.7.pos_ref, bf16[640,1024]{1,0:T(8,128)(2,1)} %bitcast.30, ...), custom_call_target="tpu_custom_call" | custom-call | tf_op jit(solution)/shard_map/pallas_call | solution.py:70
  6.4 1.4 collective-permute-start
  7.9 1.3 collective-permute-start.2
  9.2 8.9 %shard_map.69 = (bf16[3,160,384]{2,1,0:T(8,128)(2,1)}, bf16[3,160,384]{2,1,0:T(8,128)(2,1)}, bf16[3,160,384]{2,1,0:T(8,128)(2,1)}, bf16[3,160,384]{2,1,0:T(8,128)(2,1)}, f32[3,384]{1,0:T(4,128)}) custom-call(s32[1]{0:T(128)} %bitcast.part_ref, s32[640,1]{1,0:T(8,128)} %copy.7.pos_ref, bf16[640,1024]{1,0:T(8,128)(2,1)} %bitcast.31, ...), custom_call_target="tpu_custom_call" | custom-call | tf_op jit(solution)/shard_map/pallas_call | solution.py:70
  18.1 1.3 collective-permute-start.1
  19.4 1.3 collective-permute-start.6
  20.6 1.3 collective-permute-start.8
  22.0 1.3 collective-permute-start.10
  23.3 1.3 collective-permute-start.3
  24.6 34.7 %collective-permute-done.3 = bf16[3,160,128]{2,1,0:T(8,128)(2,1)S(1)} collective-permute-done((bf16[3,160,128]{2,1,0:T(8,128)(2,1)S(1)}, bf16[3,160,128]{2,1,0:T(8,128)(2,1)S(1)}, u32[]{:S(2)}, u32[]{:S(2)}) %collective-permute-start.3) | collective-permute-done | bytes 122912 | tf_op jit(solution)/shard_map/ppermute | solution.py:124
  59.2 1.3 collective-permute-start.4
  60.5 6.1 %collective-permute-done.4 = bf16[3,160,128]{2,1,0:T(8,128)(2,1)S(1)} collective-permute-done((bf16[3,160,128]{2,1,0:T(8,128)(2,1)S(1)}, bf16[3,160,128]{2,1,0:T(8,128)(2,1)S(1)}, u32[]{:S(2)}, u32[]{:S(2)}) %collective-permute-start.4) | collective-permute-done | bytes 122912 | tf_op jit(solution)/shard_map/ppermute | solution.py:124
  66.7 11.1 %shard_map.70 = (bf16[3,160,512]{2,1,0:T(8,128)(2,1)}, bf16[3,160,512]{2,1,0:T(8,128)(2,1)}, bf16[3,160,512]{2,1,0:T(8,128)(2,1)}, bf16[3,160,512]{2,1,0:T(8,128)(2,1)}, f32[3,512]{1,0:T(4,128)}) custom-call(s32[1]{0:T(128)} %bitcast.part_ref, s32[640,1]{1,0:T(8,128)} %copy.7.pos_ref, bf16[640,1024]{1,0:T(8,128)(2,1)} %bitcast.32, ...), custom_call_target="tpu_custom_call" | custom-call | tf_op jit(solution)/shard_map/pallas_call | solution.py:70
  77.7 0.7 pad_maximum_fusion
  78.5 1.7 %collective-permute-start.12 = (f32[3,1024]{1,0:T(4,128)S(1)}, f32[3,1024]{1,0:T(4,128)S(1)}, u32[]{:S(2)}, u32[]{:S(2)}) collective-permute-start(f32[3,1024]{1,0:T(4,128)S(1)} %pad_maximum_fusion), channel_id=1, source_target_pairs={{0,4},{4,0},{8,12},{12,8},{1,5},{5,1},{9,13},{13,9},{2,6},{6,2},{1... | collective-permute-start | bytes 36872 | tf_op jit(solution)/shard_map/ppermute | solution.py:82
  80.2 1.3 collective-permute-start.5
  81.5 1.3 collective-permute-start.7
  82.8 1.3 collective-permute-start.9
  84.1 1.3 collective-permute-start.11
  85.4 2.7 %collective-permute-start.13 = (f32[3,1024]{1,0:T(4,128)S(1)}, f32[3,1024]{1,0:T(4,128)S(1)}, u32[]{:S(2)}, u32[]{:S(2)}) collective-permute-start(f32[3,1024]{1,0:T(4,128)S(1)} %add.130), channel_id=1, source_target_pairs={{0,8},{4,12},{8,0},{12,4},{1,9},{5,13},{9,1},{13,5},{2,10},{6,14},... | collective-permute-start | bytes 36872 | tf_op jit(solution)/shard_map/ppermute | solution.py:82
  88.6 1.5 %collective-permute-done.13 = f32[3,1024]{1,0:T(4,128)S(1)} collective-permute-done((f32[3,1024]{1,0:T(4,128)S(1)}, f32[3,1024]{1,0:T(4,128)S(1)}, u32[]{:S(2)}, u32[]{:S(2)}) %collective-permute-start.13) | collective-permute-done | bytes 12320 | tf_op jit(solution)/shard_map/ppermute | solution.py:82
  90.1 1.3 collective-permute-start.14
  91.5 36.1 %collective-permute-done.14 = f32[3,1024]{1,0:T(4,128)S(1)} collective-permute-done((f32[3,1024]{1,0:T(4,128)S(1)}, f32[3,1024]{1,0:T(4,128)S(1)}, u32[]{:S(2)}, u32[]{:S(2)}) %collective-permute-start.14) | collective-permute-done | bytes 12320 | tf_op jit(solution)/shard_map/ppermute | solution.py:133
  127.6 1.3 collective-permute-start.15
  129.0 4.6 %collective-permute-done.15 = f32[3,1024]{1,0:T(4,128)S(1)} collective-permute-done((f32[3,1024]{1,0:T(4,128)S(1)}, f32[3,1024]{1,0:T(4,128)S(1)}, u32[]{:S(2)}, u32[]{:S(2)}) %collective-permute-start.15) | collective-permute-done | bytes 12320 | tf_op jit(solution)/shard_map/ppermute | solution.py:133
  133.6 1.3 collective-permute-start.16
  134.9 5.2 %collective-permute-done.16 = f32[3,1024]{1,0:T(4,128)S(1)} collective-permute-done((f32[3,1024]{1,0:T(4,128)S(1)}, f32[3,1024]{1,0:T(4,128)S(1)}, u32[]{:S(2)}, u32[]{:S(2)}) %collective-permute-start.16) | collective-permute-done | bytes 12320 | tf_op jit(solution)/shard_map/ppermute | solution.py:133
  140.1 1.3 collective-permute-start.17
  141.4 3.7 %collective-permute-done.17 = f32[3,1024]{1,0:T(4,128)S(1)} collective-permute-done((f32[3,1024]{1,0:T(4,128)S(1)}, f32[3,1024]{1,0:T(4,128)S(1)}, u32[]{:S(2)}, u32[]{:S(2)}) %collective-permute-start.17) | collective-permute-done | bytes 12320 | tf_op jit(solution)/shard_map/ppermute | solution.py:133
  145.2 0.7 broadcast_in_dim.48
  146.6 1.9 %copy-done = bf16[1,1,3,160,4096]{4,3,2,1,0:T(8,128)(2,1)} copy-done((bf16[1,1,3,160,4096]{4,3,2,1,0:T(8,128)(2,1)}, bf16[1,1,3,160,4096]{4,3,2,1,0:T(8,128)(2,1)S(1)}, u32[]{:S(2)}) %copy-start) | copy-done | bytes 3932184
  (41 shorter events, 1.4 us)
Async XLA Ops:
  6.4 16.8 %copy-start.4 = (bf16[3,160,128]{2,1,0:T(8,128)(2,1)S(1)}, bf16[3,160,128]{2,1,0:T(8,128)(2,1)}, u32[]{:S(2)}) copy-start(bf16[3,160,128]{2,1,0:T(8,128)(2,1)} %get-tuple-element.25) | copy-start | bytes 368644
  6.4 52.8 %copy-start.3 = (bf16[3,160,128]{2,1,0:T(8,128)(2,1)S(1)}, bf16[3,160,128]{2,1,0:T(8,128)(2,1)}, u32[]{:S(2)}) copy-start(bf16[3,160,128]{2,1,0:T(8,128)(2,1)} %get-tuple-element.26) | copy-start | bytes 368644
  6.4 15.5 %collective-permute-start = (bf16[3,160,128]{2,1,0:T(8,128)(2,1)}, bf16[3,160,128]{2,1,0:T(8,128)(2,1)S(1)}, u32[]{:S(2)}, u32[]{:S(2)}) collective-permute-start(bf16[3,160,128]{2,1,0:T(8,128)(2,1)} %get-tuple-element.22), channel_id=1, source_target_pairs={{16,0},{17,1},{18,2},{19,3},{20,4},{21,5},{22,6},{23,7},{24,8},{25... | collective-permute-start | bytes 368648 | tf_op jit(solution)/shard_map/ppermute | solution.py:124
  7.9 15.4 %collective-permute-start.2 = (bf16[3,160,128]{2,1,0:T(8,128)(2,1)}, bf16[3,160,128]{2,1,0:T(8,128)(2,1)S(1)}, u32[]{:S(2)}, u32[]{:S(2)}) collective-permute-start(bf16[3,160,128]{2,1,0:T(8,128)(2,1)} %get-tuple-element.24), channel_id=1, source_target_pairs={{16,1},{17,2},{18,3},{19,0},{20,5},{21,6},{22,7},{23,4},{24,9},{25... | collective-permute-start | bytes 368648 | tf_op jit(solution)/shard_map/ppermute | solution.py:124
  18.0 59.7 %copy-start.1 = (f32[3,384]{1,0:T(4,128)S(1)}, f32[3,384]{1,0:T(4,128)}, u32[]{:S(2)}) copy-start(f32[3,384]{1,0:T(4,128)} %get-tuple-element.39) | copy-start | bytes 13828
  18.0 59.7 %copy-start.2 = (f32[3,128]{1,0:T(4,128)S(1)}, f32[3,128]{1,0:T(4,128)}, u32[]{:S(2)}) copy-start(f32[3,128]{1,0:T(4,128)} %get-tuple-element.38) | copy-start | bytes 4612
  18.1 60.4 %collective-permute-start.1 = (bf16[3,160,384]{2,1,0:T(8,128)(2,1)}, bf16[3,160,384]{2,1,0:T(8,128)(2,1)S(1)}, u32[]{:S(2)}, u32[]{:S(2)}) collective-permute-start(bf16[3,160,384]{2,1,0:T(8,128)(2,1)} %get-tuple-element.23), channel_id=1, source_target_pairs={{16,0},{17,1},{18,2},{19,3},{20,4},{21,5},{22,6},{23,7},{24,8},{25... | collective-permute-start | bytes 1105928 | tf_op jit(solution)/shard_map/ppermute | solution.py:124
  19.4 59.1 %collective-permute-start.6 = (bf16[3,160,384]{2,1,0:T(8,128)(2,1)}, bf16[3,160,384]{2,1,0:T(8,128)(2,1)S(1)}, u32[]{:S(2)}, u32[]{:S(2)}) collective-permute-start(bf16[3,160,384]{2,1,0:T(8,128)(2,1)} %get-tuple-element.32), channel_id=1, source_target_pairs={{16,1},{17,2},{18,3},{19,0},{20,5},{21,6},{22,7},{23,4},{24,9},{25... | collective-permute-start | bytes 1105928 | tf_op jit(solution)/shard_map/ppermute | solution.py:124
  20.6 57.8 %collective-permute-start.8 = (bf16[3,160,384]{2,1,0:T(8,128)(2,1)}, bf16[3,160,384]{2,1,0:T(8,128)(2,1)S(1)}, u32[]{:S(2)}, u32[]{:S(2)}) collective-permute-start(bf16[3,160,384]{2,1,0:T(8,128)(2,1)} %get-tuple-element.34), channel_id=1, source_target_pairs={{16,2},{17,3},{18,0},{19,1},{20,6},{21,7},{22,4},{23,5},{24,10},{2... | collective-permute-start | bytes 1105928 | tf_op jit(solution)/shard_map/ppermute | solution.py:124
  22.0 56.5 %collective-permute-start.10 = (bf16[3,160,384]{2,1,0:T(8,128)(2,1)}, bf16[3,160,384]{2,1,0:T(8,128)(2,1)S(1)}, u32[]{:S(2)}, u32[]{:S(2)}) collective-permute-start(bf16[3,160,384]{2,1,0:T(8,128)(2,1)} %get-tuple-element.36), channel_id=1, source_target_pairs={{16,3},{17,0},{18,1},{19,2},{20,7},{21,4},{22,5},{23,6},{24,11},{2... | collective-permute-start | bytes 1105928 | tf_op jit(solution)/shard_map/ppermute | solution.py:124
  23.3 36.0 %collective-permute-start.3 = (bf16[3,160,128]{2,1,0:T(8,128)(2,1)S(1)}, bf16[3,160,128]{2,1,0:T(8,128)(2,1)S(1)}, u32[]{:S(2)}, u32[]{:S(2)}) collective-permute-start(bf16[3,160,128]{2,1,0:T(8,128)(2,1)S(1)} %copy-done.4), channel_id=1, source_target_pairs={{16,2},{17,3},{18,0},{19,1},{20,6},{21,7},{22,4},{23,5},{24,10},{2... | collective-permute-start | bytes 368648 | tf_op jit(solution)/shard_map/ppermute | solution.py:124
  59.2 7.4 %collective-permute-start.4 = (bf16[3,160,128]{2,1,0:T(8,128)(2,1)S(1)}, bf16[3,160,128]{2,1,0:T(8,128)(2,1)S(1)}, u32[]{:S(2)}, u32[]{:S(2)}) collective-permute-start(bf16[3,160,128]{2,1,0:T(8,128)(2,1)S(1)} %copy-done.3), channel_id=1, source_target_pairs={{16,3},{17,0},{18,1},{19,2},{20,7},{21,4},{22,5},{23,6},{24,11},{2... | collective-permute-start | bytes 368648 | tf_op jit(solution)/shard_map/ppermute | solution.py:124
  78.5 6.9 %collective-permute-start.12 = (f32[3,1024]{1,0:T(4,128)S(1)}, f32[3,1024]{1,0:T(4,128)S(1)}, u32[]{:S(2)}, u32[]{:S(2)}) collective-permute-start(f32[3,1024]{1,0:T(4,128)S(1)} %pad_maximum_fusion), channel_id=1, source_target_pairs={{0,4},{4,0},{8,12},{12,8},{1,5},{5,1},{9,13},{13,9},{2,6},{6,2},{1... | collective-permute-start | bytes 36872 | tf_op jit(solution)/shard_map/ppermute | solution.py:82
  80.2 65.6 %collective-permute-start.5 = (bf16[3,160,512]{2,1,0:T(8,128)(2,1)}, bf16[3,160,512]{2,1,0:T(8,128)(2,1)S(1)}, u32[]{:S(2)}, u32[]{:S(2)}) collective-permute-start(bf16[3,160,512]{2,1,0:T(8,128)(2,1)} %get-tuple-element.31), channel_id=1, source_target_pairs={{16,0},{17,1},{18,2},{19,3},{20,4},{21,5},{22,6},{23,7},{24,8},{25... | collective-permute-start | bytes 1474568 | tf_op jit(solution)/shard_map/ppermute | solution.py:124
  81.5 64.6 %collective-permute-start.7 = (bf16[3,160,512]{2,1,0:T(8,128)(2,1)}, bf16[3,160,512]{2,1,0:T(8,128)(2,1)S(1)}, u32[]{:S(2)}, u32[]{:S(2)}) collective-permute-start(bf16[3,160,512]{2,1,0:T(8,128)(2,1)} %get-tuple-element.33), channel_id=1, source_target_pairs={{16,1},{17,2},{18,3},{19,0},{20,5},{21,6},{22,7},{23,4},{24,9},{25... | collective-permute-start | bytes 1474568 | tf_op jit(solution)/shard_map/ppermute | solution.py:124
  82.8 63.5 %collective-permute-start.9 = (bf16[3,160,512]{2,1,0:T(8,128)(2,1)}, bf16[3,160,512]{2,1,0:T(8,128)(2,1)S(1)}, u32[]{:S(2)}, u32[]{:S(2)}) collective-permute-start(bf16[3,160,512]{2,1,0:T(8,128)(2,1)} %get-tuple-element.35), channel_id=1, source_target_pairs={{16,2},{17,3},{18,0},{19,1},{20,6},{21,7},{22,4},{23,5},{24,10},{2... | collective-permute-start | bytes 1474568 | tf_op jit(solution)/shard_map/ppermute | solution.py:124
  84.1 62.4 %collective-permute-start.11 = (bf16[3,160,512]{2,1,0:T(8,128)(2,1)}, bf16[3,160,512]{2,1,0:T(8,128)(2,1)S(1)}, u32[]{:S(2)}, u32[]{:S(2)}) collective-permute-start(bf16[3,160,512]{2,1,0:T(8,128)(2,1)} %get-tuple-element.37), channel_id=1, source_target_pairs={{16,3},{17,0},{18,1},{19,2},{20,7},{21,4},{22,5},{23,6},{24,11},{2... | collective-permute-start | bytes 1474568 | tf_op jit(solution)/shard_map/ppermute | solution.py:124
  85.4 4.7 %collective-permute-start.13 = (f32[3,1024]{1,0:T(4,128)S(1)}, f32[3,1024]{1,0:T(4,128)S(1)}, u32[]{:S(2)}, u32[]{:S(2)}) collective-permute-start(f32[3,1024]{1,0:T(4,128)S(1)} %add.130), channel_id=1, source_target_pairs={{0,8},{4,12},{8,0},{12,4},{1,9},{5,13},{9,1},{13,5},{2,10},{6,14},... | collective-permute-start | bytes 36872 | tf_op jit(solution)/shard_map/ppermute | solution.py:82
  90.1 37.5 %collective-permute-start.14 = (f32[3,1024]{1,0:T(4,128)S(1)}, f32[3,1024]{1,0:T(4,128)S(1)}, u32[]{:S(2)}, u32[]{:S(2)}) collective-permute-start(f32[3,1024]{1,0:T(4,128)S(1)} %add.131), channel_id=1, source_target_pairs={{16,0},{17,1},{18,2},{19,3},{20,4},{21,5},{22,6},{23,7},{24,8},{25... | collective-permute-start | bytes 36872 | tf_op jit(solution)/shard_map/ppermute | solution.py:133
  127.6 5.9 %collective-permute-start.15 = (f32[3,1024]{1,0:T(4,128)S(1)}, f32[3,1024]{1,0:T(4,128)S(1)}, u32[]{:S(2)}, u32[]{:S(2)}) collective-permute-start(f32[3,1024]{1,0:T(4,128)S(1)} %add.131), channel_id=1, source_target_pairs={{16,1},{17,2},{18,3},{19,0},{20,5},{21,6},{22,7},{23,4},{24,9},{25... | collective-permute-start | bytes 36872 | tf_op jit(solution)/shard_map/ppermute | solution.py:133
  133.6 6.5 %collective-permute-start.16 = (f32[3,1024]{1,0:T(4,128)S(1)}, f32[3,1024]{1,0:T(4,128)S(1)}, u32[]{:S(2)}, u32[]{:S(2)}) collective-permute-start(f32[3,1024]{1,0:T(4,128)S(1)} %add.131), channel_id=1, source_target_pairs={{16,2},{17,3},{18,0},{19,1},{20,6},{21,7},{22,4},{23,5},{24,10},{2... | collective-permute-start | bytes 36872 | tf_op jit(solution)/shard_map/ppermute | solution.py:133
  140.1 5.0 %collective-permute-start.17 = (f32[3,1024]{1,0:T(4,128)S(1)}, f32[3,1024]{1,0:T(4,128)S(1)}, u32[]{:S(2)}, u32[]{:S(2)}) collective-permute-start(f32[3,1024]{1,0:T(4,128)S(1)} %add.131), channel_id=1, source_target_pairs={{16,3},{17,0},{18,1},{19,2},{20,7},{21,4},{22,5},{23,6},{24,11},{2... | collective-permute-start | bytes 36872 | tf_op jit(solution)/shard_map/ppermute | solution.py:133
  146.6 1.9 %copy-start = (bf16[1,1,3,160,4096]{4,3,2,1,0:T(8,128)(2,1)}, bf16[1,1,3,160,4096]{4,3,2,1,0:T(8,128)(2,1)S(1)}, u32[]{:S(2)}) copy-start(bf16[1,1,3,160,4096]{4,3,2,1,0:T(8,128)(2,1)S(1)} %bitcast_dynamic-update-slice_fusion) | copy-start | bytes 11796484

commit v5 on v4

--- a/solution.py
+++ b/solution.py
@@ -124,14 +124,12 @@
             arrived[shift][c] = lax.ppermute(grads[shift], ("section", "mp"), pairs(shift))
 
     own = jnp.concatenate(sums, axis=1)
-    if chunk_count > 1:
-        own = lax.optimization_barrier((own, [arrived[shift][-2] for shift in range(parts)]))[0]
-    own = butterfly_sum(own, "dp")
-    totals = jnp.zeros((3, columns * parts), jnp.float32)
-    for shift in range(parts):
-        source = (part - shift) % parts
-        piece = lax.ppermute(own, ("section", "mp"), pairs(shift))
-        totals = lax.dynamic_update_slice_in_dim(totals, piece, source * columns, 1)
+    section = lax.axis_index("section")
+    slots = jnp.zeros((sections, 3, columns * parts), jnp.float32)
+    slots = lax.dynamic_update_slice(slots, own[None], (section - 1, 0, part * columns))
+    slots = jnp.where(section > 0, slots, 0.0)
+    totals = lax.psum(slots, ("section", "dp", "mp"))
+    totals = lax.dynamic_index_in_dim(totals, section, 0, keepdims=False)
     bias_grad = totals / math.sqrt(replicas * length)
 
     received = jnp.zeros((3, rows, columns * parts), jnp.bfloat16)

time: 149 us -> 218 us (1.46)
  waiting for transfers between devices: 92 us -> 147 us
  between operations: 1.03 us -> 14.4 us
  starting transfers between devices: 25.1 us -> 15.6 us
  local copies, waits for them, and re-layouts: 5.46 us -> 14.1 us
    psum x0 -> x1, waiting for transfers between devices: none -> 122 us  [per_device(): totals = lax.psum(slots, ('section', 'dp', 'mp'))]
    ppermute x6 -> x0, waiting for transfers between devices: 51.2 us -> none  [the longest x4 49.7 us: per_device(): piece = lax.ppermute(own, ('section', 'mp'), pairs(shift))]
    ppermute x12, waiting for transfers between devices: 40.8 us -> 25 us  [per_device(): lax.ppermute(grads[shift], ('section', 'mp'), pairs(shift))]
    ppermute x6 -> x0, starting transfers between devices: 9.53 us -> none  [the longest x4 5.12 us: per_device(): piece = lax.ppermute(own, ('section', 'mp'), pairs(shift))]
    dynamic_update_slice x12, local copies, waits for them, and re-layouts: 0.75 us -> 8.98 us  [per_device(): lax.dynamic_update_slice_in_dim(received, arrived[shift][c], source * col...]
  transfers between devices with their start and end apart: 18 -> 13, of which waited for: 7 -> 4; matrix products, arithmetic and copies ran while one was open for 2% -> 6% of each run, Pallas kernels for 13% -> 9%
where the time goes in v5:
time: 218 us; the launch traced here: 217 us
  waiting for transfers between devices  147 us (67%)
  Pallas kernels  24.2 us (11%)
  starting transfers between devices  15.6 us (7%)
  between operations  14.4 us (7%)
  local copies, waits for them, and re-layouts  14.1 us (6%)
  other arithmetic  2.29 us (1%)
    psum x1, waiting for transfers between devices, per_device(): totals = lax.psum(slots, ('section', 'dp', 'mp'))  122 us
    ppermute x12, waiting for transfers between devices, per_device(): lax.ppermute(grads[shift], ('section', 'mp'), pairs(shift))  25 us
    pallas_call x3, Pallas kernels, chunk_grads(): pl.pallas_call(functools.partial(grads_kernel, parts=parts), grid_spec=gr...  24.2 us
    ppermute x12, starting transfers between devices, per_device(): lax.ppermute(grads[shift], ('section', 'mp'), pairs(shift))  15.6 us
    dynamic_update_slice x12, local copies, waits for them, and re-layouts, per_device(): lax.dynamic_update_slice_in_dim(received, arrived[shift][c], source * col...  8.98 us
  transfers between devices with their start and end apart: 13, of which 4 were waited for; matrix products, arithmetic and copies ran while one was open for 6% of the time, Pallas kernels for 9%

profile of v5, /device:TPU:0, one launch (start us, length us, event | category | flops | bytes accessed | tf_op | source)
XLA Modules:
  0.0 217.4 jit_solution(9390575318318813662)
XLA Ops:
  7.2 1.6 copy.8.pos_ref
  8.8 4.2 %shard_map.68 = (bf16[3,160,128]{2,1,0:T(8,128)(2,1)}, bf16[3,160,128]{2,1,0:T(8,128)(2,1)}, bf16[3,160,128]{2,1,0:T(8,128)(2,1)}, bf16[3,160,128]{2,1,0:T(8,128)(2,1)}, f32[3,128]{1,0:T(4,128)}) custom-call(s32[1]{0:T(128)} %bitcast.part_ref, s32[640,1]{1,0:T(8,128)} %copy.8.pos_ref, bf16[640,1024]{1,0:T(8,128)(2,1)} %bitcast.33, ...), custom_call_target="tpu_custom_call" | custom-call | tf_op jit(solution)/shard_map/pallas_call | solution.py:70
  13.0 1.3 collective-permute-start
  14.3 1.3 collective-permute-start.2
  15.6 1.3 collective-permute-start.3
  16.9 1.3 collective-permute-start.4
  18.2 8.9 %shard_map.69 = (bf16[3,160,384]{2,1,0:T(8,128)(2,1)}, bf16[3,160,384]{2,1,0:T(8,128)(2,1)}, bf16[3,160,384]{2,1,0:T(8,128)(2,1)}, bf16[3,160,384]{2,1,0:T(8,128)(2,1)}, f32[3,384]{1,0:T(4,128)}) custom-call(s32[1]{0:T(128)} %bitcast.part_ref, s32[640,1]{1,0:T(8,128)} %copy.8.pos_ref, bf16[640,1024]{1,0:T(8,128)(2,1)} %bitcast.34, ...), custom_call_target="tpu_custom_call" | custom-call | tf_op jit(solution)/shard_map/pallas_call | solution.py:70
  27.1 1.3 collective-permute-start.1
  28.6 1.3 collective-permute-start.6
  29.9 1.3 collective-permute-start.8
  31.2 1.3 collective-permute-start.10
  32.5 11.1 %shard_map.70 = (bf16[3,160,512]{2,1,0:T(8,128)(2,1)}, bf16[3,160,512]{2,1,0:T(8,128)(2,1)}, bf16[3,160,512]{2,1,0:T(8,128)(2,1)}, bf16[3,160,512]{2,1,0:T(8,128)(2,1)}, f32[3,512]{1,0:T(4,128)}) custom-call(s32[1]{0:T(128)} %bitcast.part_ref, s32[640,1]{1,0:T(8,128)} %copy.8.pos_ref, bf16[640,1024]{1,0:T(8,128)(2,1)} %bitcast.35, ...), custom_call_target="tpu_custom_call" | custom-call | tf_op jit(solution)/shard_map/pallas_call | solution.py:70
  43.6 1.4 collective-permute-start.5
  45.1 0.7 maximum_select_fusion
  46.9 2.4 %broadcast_in_dim.35 = bf16[1,1,3,160,4096]{4,3,2,1,0:T(8,128)(2,1)} broadcast(bf16[]{:T(256)} %constant.71.clone.1), dimensions={} | broadcast | bytes 3932162 | tf_op jit(solution)/shard_map/broadcast_in_dim | solution.py:142
  50.0 121.8 %all-reduce.2.cloned.1.call-done = f32[2,3,4096]{2,0,1:T(2,128)} async-done(((f32[2,3,4096]{2,0,1:T(2,128)}), f32[2,3,4096]{2,0,1:T(2,128)}) %all-reduce.2.cloned.1.call-update) | async-done | bytes 98320 | tf_op jit(solution)/shard_map/psum | solution.py:131
  171.8 1.6 dynamic-slice_multiply_fusion
  173.3 1.3 collective-permute-start.7
  174.6 0.8 bitcast_dynamic-update-slice_fusion.7
  175.4 1.3 collective-permute-start.9
  176.7 0.8 bitcast_dynamic-update-slice_fusion.3
  178.2 1.3 collective-permute-start.11
  179.5 0.8 bitcast_dynamic-update-slice_fusion.6
  180.2 9.6 %collective-permute-done.7 = bf16[3,160,512]{2,1,0:T(8,128)(2,1)S(1)} collective-permute-done((bf16[3,160,512]{2,1,0:T(8,128)(2,1)}, bf16[3,160,512]{2,1,0:T(8,128)(2,1)S(1)}, u32[]{:S(2)}, u32[]{:S(2)}) %collective-permute-start.7) | collective-permute-done | bytes 491552 | tf_op jit(solution)/shard_map/ppermute | solution.py:124
  189.8 0.8 bitcast_dynamic-update-slice_fusion.2
  190.7 0.7 bitcast_dynamic-update-slice_fusion.9
  191.3 0.8 bitcast_dynamic-update-slice_fusion.5
  192.1 7.8 %collective-permute-done.9 = bf16[3,160,512]{2,1,0:T(8,128)(2,1)S(1)} collective-permute-done((bf16[3,160,512]{2,1,0:T(8,128)(2,1)S(1)}, bf16[3,160,512]{2,1,0:T(8,128)(2,1)S(1)}, u32[]{:S(2)}, u32[]{:S(2)}) %collective-permute-start.9) | collective-permute-done | bytes 491552 | tf_op jit(solution)/shard_map/ppermute | solution.py:124
  199.9 0.8 bitcast_dynamic-update-slice_fusion.1
  201.4 0.8 bitcast_dynamic-update-slice_fusion.4
  202.1 7.6 %collective-permute-done.11 = bf16[3,160,512]{2,1,0:T(8,128)(2,1)S(1)} collective-permute-done((bf16[3,160,512]{2,1,0:T(8,128)(2,1)S(1)}, bf16[3,160,512]{2,1,0:T(8,128)(2,1)S(1)}, u32[]{:S(2)}, u32[]{:S(2)}) %collective-permute-start.11) | collective-permute-done | bytes 491552 | tf_op jit(solution)/shard_map/ppermute | solution.py:124
  209.7 0.8 bitcast_dynamic-update-slice_fusion
  (27 shorter events, 3.2 us)
Async XLA Ops:
  7.2 164.6 %all-reduce.2.cloned.1.call-start = ((), (), s32[]{:S(2)}) async-start(), calls=%async_computation | async-start | bytes 196608 | tf_op jit(solution)/shard_map/psum | solution.py:131
  13.0 15.6 %collective-permute-start = (bf16[3,160,128]{2,1,0:T(8,128)(2,1)}, bf16[3,160,128]{2,1,0:T(8,128)(2,1)S(1)}, u32[]{:S(2)}, u32[]{:S(2)}) collective-permute-start(bf16[3,160,128]{2,1,0:T(8,128)(2,1)} %get-tuple-element.21), channel_id=1, source_target_pairs={{16,0},{17,1},{18,2},{19,3},{20,4},{21,5},{22,6},{23,7},{24,8},{25... | collective-permute-start | bytes 368648 | tf_op jit(solution)/shard_map/ppermute | solution.py:124
  14.3 15.6 %collective-permute-start.2 = (bf16[3,160,128]{2,1,0:T(8,128)(2,1)}, bf16[3,160,128]{2,1,0:T(8,128)(2,1)S(1)}, u32[]{:S(2)}, u32[]{:S(2)}) collective-permute-start(bf16[3,160,128]{2,1,0:T(8,128)(2,1)} %get-tuple-element.23), channel_id=1, source_target_pairs={{16,1},{17,2},{18,3},{19,0},{20,5},{21,6},{22,7},{23,4},{24,9},{25... | collective-permute-start | bytes 368648 | tf_op jit(solution)/shard_map/ppermute | solution.py:124
  15.6 15.6 %collective-permute-start.3 = (bf16[3,160,128]{2,1,0:T(8,128)(2,1)}, bf16[3,160,128]{2,1,0:T(8,128)(2,1)S(1)}, u32[]{:S(2)}, u32[]{:S(2)}) collective-permute-start(bf16[3,160,128]{2,1,0:T(8,128)(2,1)} %get-tuple-element.24), channel_id=1, source_target_pairs={{16,2},{17,3},{18,0},{19,1},{20,6},{21,7},{22,4},{23,5},{24,10},{2... | collective-permute-start | bytes 368648 | tf_op jit(solution)/shard_map/ppermute | solution.py:124
  16.9 15.6 %collective-permute-start.4 = (bf16[3,160,128]{2,1,0:T(8,128)(2,1)}, bf16[3,160,128]{2,1,0:T(8,128)(2,1)S(1)}, u32[]{:S(2)}, u32[]{:S(2)}) collective-permute-start(bf16[3,160,128]{2,1,0:T(8,128)(2,1)} %get-tuple-element.25), channel_id=1, source_target_pairs={{16,3},{17,0},{18,1},{19,2},{20,7},{21,4},{22,5},{23,6},{24,11},{2... | collective-permute-start | bytes 368648 | tf_op jit(solution)/shard_map/ppermute | solution.py:124
  27.1 17.9 %copy-start.1 = (f32[3,384]{1,0:T(4,128)S(1)}, f32[3,384]{1,0:T(4,128)}, u32[]{:S(2)}) copy-start(f32[3,384]{1,0:T(4,128)} %get-tuple-element.38) | copy-start | bytes 13828
  27.1 17.9 %copy-start.2 = (f32[3,128]{1,0:T(4,128)S(1)}, f32[3,128]{1,0:T(4,128)}, u32[]{:S(2)}) copy-start(f32[3,128]{1,0:T(4,128)} %get-tuple-element.37) | copy-start | bytes 4612
  27.1 146.2 %collective-permute-start.1 = (bf16[3,160,384]{2,1,0:T(8,128)(2,1)}, bf16[3,160,384]{2,1,0:T(8,128)(2,1)S(1)}, u32[]{:S(2)}, u32[]{:S(2)}) collective-permute-start(bf16[3,160,384]{2,1,0:T(8,128)(2,1)} %get-tuple-element.22), channel_id=1, source_target_pairs={{16,0},{17,1},{18,2},{19,3},{20,4},{21,5},{22,6},{23,7},{24,8},{25... | collective-permute-start | bytes 1105928 | tf_op jit(solution)/shard_map/ppermute | solution.py:124
  28.6 149.6 %collective-permute-start.6 = (bf16[3,160,384]{2,1,0:T(8,128)(2,1)}, bf16[3,160,384]{2,1,0:T(8,128)(2,1)S(1)}, u32[]{:S(2)}, u32[]{:S(2)}) collective-permute-start(bf16[3,160,384]{2,1,0:T(8,128)(2,1)} %get-tuple-element.31), channel_id=1, source_target_pairs={{16,1},{17,2},{18,3},{19,0},{20,5},{21,6},{22,7},{23,4},{24,9},{25... | collective-permute-start | bytes 1105928 | tf_op jit(solution)/shard_map/ppermute | solution.py:124
  29.9 161.4 %collective-permute-start.8 = (bf16[3,160,384]{2,1,0:T(8,128)(2,1)}, bf16[3,160,384]{2,1,0:T(8,128)(2,1)S(1)}, u32[]{:S(2)}, u32[]{:S(2)}) collective-permute-start(bf16[3,160,384]{2,1,0:T(8,128)(2,1)} %get-tuple-element.33), channel_id=1, source_target_pairs={{16,2},{17,3},{18,0},{19,1},{20,6},{21,7},{22,4},{23,5},{24,10},{2... | collective-permute-start | bytes 1105928 | tf_op jit(solution)/shard_map/ppermute | solution.py:124
  31.2 170.2 %collective-permute-start.10 = (bf16[3,160,384]{2,1,0:T(8,128)(2,1)}, bf16[3,160,384]{2,1,0:T(8,128)(2,1)S(1)}, u32[]{:S(2)}, u32[]{:S(2)}) collective-permute-start(bf16[3,160,384]{2,1,0:T(8,128)(2,1)} %get-tuple-element.35), channel_id=1, source_target_pairs={{16,3},{17,0},{18,1},{19,2},{20,7},{21,4},{22,5},{23,6},{24,11},{2... | collective-permute-start | bytes 1105928 | tf_op jit(solution)/shard_map/ppermute | solution.py:124
  43.6 131.8 %copy-start.4 = (bf16[3,160,512]{2,1,0:T(8,128)(2,1)S(1)}, bf16[3,160,512]{2,1,0:T(8,128)(2,1)}, u32[]{:S(2)}) copy-start(bf16[3,160,512]{2,1,0:T(8,128)(2,1)} %get-tuple-element.34) | copy-start | bytes 1474564
  43.6 134.6 %copy-start.3 = (bf16[3,160,512]{2,1,0:T(8,128)(2,1)S(1)}, bf16[3,160,512]{2,1,0:T(8,128)(2,1)}, u32[]{:S(2)}) copy-start(bf16[3,160,512]{2,1,0:T(8,128)(2,1)} %get-tuple-element.36) | copy-start | bytes 1474564
  43.6 131.8 %collective-permute-start.5 = (bf16[3,160,512]{2,1,0:T(8,128)(2,1)}, bf16[3,160,512]{2,1,0:T(8,128)(2,1)S(1)}, u32[]{:S(2)}, u32[]{:S(2)}) collective-permute-start(bf16[3,160,512]{2,1,0:T(8,128)(2,1)} %get-tuple-element.30), channel_id=1, source_target_pairs={{16,0},{17,1},{18,2},{19,3},{20,4},{21,5},{22,6},{23,7},{24,8},{25... | collective-permute-start | bytes 1474568 | tf_op jit(solution)/shard_map/ppermute | solution.py:124
  46.3 0.6 copy-start
  173.3 16.5 %collective-permute-start.7 = (bf16[3,160,512]{2,1,0:T(8,128)(2,1)}, bf16[3,160,512]{2,1,0:T(8,128)(2,1)S(1)}, u32[]{:S(2)}, u32[]{:S(2)}) collective-permute-start(bf16[3,160,512]{2,1,0:T(8,128)(2,1)} %get-tuple-element.32), channel_id=1, source_target_pairs={{16,1},{17,2},{18,3},{19,0},{20,5},{21,6},{22,7},{23,4},{24,9},{25... | collective-permute-start | bytes 1474568 | tf_op jit(solution)/shard_map/ppermute | solution.py:124
  175.4 24.5 %collective-permute-start.9 = (bf16[3,160,512]{2,1,0:T(8,128)(2,1)S(1)}, bf16[3,160,512]{2,1,0:T(8,128)(2,1)S(1)}, u32[]{:S(2)}, u32[]{:S(2)}) collective-permute-start(bf16[3,160,512]{2,1,0:T(8,128)(2,1)S(1)} %copy-done.4), channel_id=1, source_target_pairs={{16,2},{17,3},{18,0},{19,1},{20,6},{21,7},{22,4},{23,5},{24,10},{2... | collective-permute-start | bytes 1474568 | tf_op jit(solution)/shard_map/ppermute | solution.py:124
  178.2 31.6 %collective-permute-start.11 = (bf16[3,160,512]{2,1,0:T(8,128)(2,1)S(1)}, bf16[3,160,512]{2,1,0:T(8,128)(2,1)S(1)}, u32[]{:S(2)}, u32[]{:S(2)}) collective-permute-start(bf16[3,160,512]{2,1,0:T(8,128)(2,1)S(1)} %copy-done.3), channel_id=1, source_target_pairs={{16,3},{17,0},{18,1},{19,2},{20,7},{21,4},{22,5},{23,6},{24,11},{2... | collective-permute-start | bytes 1474568 | tf_op jit(solution)/shard_map/ppermute | solution.py:124
Sparse Core Ops, SparseCore 0:
  47.1 124.6 all-reduce.1

commit v6 on v3

--- a/solution.py
+++ b/solution.py
@@ -9,8 +9,6 @@
 from jax.sharding import PartitionSpec as P
 
 HEAD_DIM = 128
-CHUNK_HEADS = 2
-DEPTH = 2
 NT = (((1,), (1,)), ((), ()))
 
 
@@ -76,15 +74,6 @@
     )(part, positions, query_rows, key_rows, value_rows, grad_rows)
 
 
-def butterfly_sum(value, axis):
-    count = lax.axis_size(axis)
-    step = 1
-    while step < count:
-        value = value + lax.ppermute(value, axis, [(i, i ^ step) for i in range(count)])
-        step *= 2
-    return value
-
-
 def per_device(queries, keys, values, grad_out, positions):
     query_rows = queries[0, 0]
     key_rows = keys[0, 0]
@@ -98,10 +87,8 @@
     part = lax.axis_index("mp")
     rows = length // parts
     head_count = columns // HEAD_DIM
-    sizes = [1] if head_count > 1 else []
-    while sum(sizes) + 1 < head_count:
-        sizes.append(min(CHUNK_HEADS, head_count - 1 - sum(sizes)))
-    sizes.append(head_count - sum(sizes))
+    lead = max(1, head_count // 4)
+    sizes = [lead, head_count - lead] if head_count > lead else [head_count]
     firsts = [sum(sizes[:c]) for c in range(len(sizes))]
     chunk_count = len(sizes)
     part_arg = jnp.reshape(part, (1,)).astype(jnp.int32)
@@ -115,22 +102,41 @@
 
     arrived = [[None] * chunk_count for _ in range(parts)]
     sums = []
-    operands = (query_rows, key_rows, value_rows, grad_rows)
     for c in range(chunk_count):
-        if c >= DEPTH:
-            tied = lax.optimization_barrier((operands, [arrived[shift][c - DEPTH] for shift in range(parts)]))
-            operands = tied[0]
-        *grads, chunk_sums = chunk_grads(part_arg, token_positions, *operands, firsts[c], sizes[c], parts)
+        *grads, chunk_sums = chunk_grads(
+            part_arg, token_positions, query_rows, key_rows, value_rows, grad_rows, firsts[c], sizes[c], parts
+        )
         sums.append(chunk_sums)
+        tie = []
+        if c == chunk_count - 1:
+            own = jnp.concatenate(sums, axis=1)
+            if c > 0:
+                own = lax.optimization_barrier((own, [arrived[shift][c - 1] for shift in range(parts)]))[0]
+            relayed = lax.ppermute(own, "section", [(s + 1, s) for s in range(sections - 1)])
+            tie.append(relayed)
+        if c > 0:
+            tie += [arrived[shift][c - 1] for shift in range(parts)]
+        if tie:
+            grads = lax.optimization_barrier((grads, tie))[0]
         for shift in range(parts):
             arrived[shift][c] = lax.ppermute(grads[shift], ("section", "mp"), pairs(shift))
 
-    own = jnp.concatenate(sums, axis=1)
+    def receivers_sum(value, axis):
+        count = lax.axis_size(axis)
+        step = 1
+        while step < count:
+            ring = [(s * count + i, s * count + (i ^ step)) for s in range(sections - 1) for i in range(count)]
+            value = value + lax.ppermute(value, ("section", axis), ring)
+            step *= 2
+        return value
+
+    if chunk_count > 1:
+        relayed = lax.optimization_barrier((relayed, arrived[0][-1]))[0]
+    reduced = receivers_sum(relayed, "dp")
     slots = lax.dynamic_update_slice_in_dim(
-        jnp.zeros((3, columns * parts), jnp.float32), own, part * columns, 1
+        jnp.zeros((3, columns * parts), jnp.float32), reduced, part * columns, 1
     )
-    totals = butterfly_sum(butterfly_sum(slots, "mp"), "dp")
-    totals = lax.ppermute(totals, "section", [(s + 1, s) for s in range(sections - 1)])
+    totals = receivers_sum(slots, "mp")
     bias_grad = totals / math.sqrt(replicas * length)
 
     received = jnp.zeros((3, rows, columns * parts), jnp.bfloat16)

time: 128 us -> 111 us (0.87)
  local copies, waits for them, and re-layouts: 20.6 us -> 5.02 us
  waiting for transfers between devices: 43.6 us -> 55.1 us
  starting transfers between devices: 33.9 us -> 26.6 us
  Pallas kernels: 28.2 us -> 22.3 us
    ppermute x20 -> x8, waiting for transfers between devices: 27.7 us -> 49.6 us  [per_device(): lax.ppermute(grads[shift], ('section', 'mp'), pairs(shift))]
    ppermute x20 -> x8, starting transfers between devices: 26.1 us -> 10.3 us  [per_device(): lax.ppermute(grads[shift], ('section', 'mp'), pairs(shift))]
    dynamic_update_slice x20 -> x8, local copies, waits for them, and re-layouts: 13.8 us -> 0.46 us  [per_device(): lax.dynamic_update_slice_in_dim(received, arrived[shift][c], source * col...]
    ppermute x5, waiting for transfers between devices: 15.9 us -> 5.53 us  [the longest x1 4.33 us: per_device(): lax.ppermute(own, 'section', [(s + 1, s) for s in range(sections - 1)])]
    ppermute x5, starting transfers between devices: 7.86 us -> 16.3 us  [the longest x4 15 us: receivers_sum(): value = value + lax.ppermute(value, ('section', axis), ring)]
    pallas_call x5 -> x2, Pallas kernels: 28.2 us -> 22.3 us  [chunk_grads(): pl.pallas_call(functools.partial(grads_kernel, parts=parts), grid_spec=gr...]
    broadcast_in_dim x1, local copies, waits for them, and re-layouts: 2.4 us -> 0.46 us  [per_device(): return (received[None, None], bias_grad[None])]
  transfers between devices with their start and end apart: 25 -> 13, of which waited for: 8 -> 8; matrix products, arithmetic and copies ran while one was open for 14% -> 2% of each run, Pallas kernels for 19% -> 14%
where the time goes in v6:
time: 111 us
  waiting for transfers between devices  55.1 us (50%)
  starting transfers between devices  26.6 us (24%)
  Pallas kernels  22.3 us (20%)
  local copies, waits for them, and re-layouts  5.02 us (5%)
    ppermute x8, waiting for transfers between devices, per_device(): lax.ppermute(grads[shift], ('section', 'mp'), pairs(shift))  49.6 us
    pallas_call x2, Pallas kernels, chunk_grads(): pl.pallas_call(functools.partial(grads_kernel, parts=parts), grid_spec=gr...  22.3 us
    ppermute x4, starting transfers between devices, receivers_sum(): value = value + lax.ppermute(value, ('section', axis), ring)  15 us
    ppermute x8, starting transfers between devices, per_device(): lax.ppermute(grads[shift], ('section', 'mp'), pairs(shift))  10.3 us
    ppermute x1, waiting for transfers between devices, per_device(): lax.ppermute(own, 'section', [(s + 1, s) for s in range(sections - 1)])  4.33 us
    unnamed x9, local copies, waits for them, and re-layouts  2.5 us
  transfers between devices with their start and end apart: 13, of which 8 were waited for; matrix products, arithmetic and copies ran while one was open for 2% of the time, Pallas kernels for 14%

profile of v6, /device:TPU:0, one launch (start us, length us, event | category | flops | bytes accessed | tf_op | source)
XLA Modules:
  0.0 110.9 jit_solution(2345971015083912320)
XLA Ops:
  0.6 1.6 %copy.8.pos_ref = s32[640,1]{1,0:T(8,128)} copy(s32[640,1]{0,1:T(1,128)} %bitcast.32) | data formatting | bytes 5120 | tf_op jit(solution)/shard_map/reshape;squeeze | solution.py:82
  2.2 6.7 %shard_map.68 = (bf16[3,160,256]{2,1,0:T(8,128)(2,1)}, bf16[3,160,256]{2,1,0:T(8,128)(2,1)}, bf16[3,160,256]{2,1,0:T(8,128)(2,1)}, bf16[3,160,256]{2,1,0:T(8,128)(2,1)}, f32[3,256]{1,0:T(4,128)}) custom-call(s32[1]{0:T(128)} %bitcast.part_ref, s32[640,1]{1,0:T(8,128)} %copy.8.pos_ref, bf16[640,1024]{1,0:T(8,128)(2,1)} %bitcast.24, ...), custom_call_target="tpu_custom_call" | custom-call | tf_op jit(solution)/shard_map/pallas_call | solution.py:69
  8.9 1.3 %collective-permute-start = (bf16[3,160,256]{2,1,0:T(8,128)(2,1)}, bf16[3,160,256]{2,1,0:T(8,128)(2,1)S(1)}, u32[]{:S(2)}, u32[]{:S(2)}) collective-permute-start(bf16[3,160,256]{2,1,0:T(8,128)(2,1)} %get-tuple-element.18), channel_id=1, source_target_pairs={{16,0},{17,1},{18,2},{19,3},{20,4},{21,5},{22,6},{23,7},{24,8},{25... | collective-permute-start | bytes 737288 | tf_op jit(solution)/shard_map/ppermute | solution.py:122
  10.2 1.3 %collective-permute-start.1 = (bf16[3,160,256]{2,1,0:T(8,128)(2,1)}, bf16[3,160,256]{2,1,0:T(8,128)(2,1)S(1)}, u32[]{:S(2)}, u32[]{:S(2)}) collective-permute-start(bf16[3,160,256]{2,1,0:T(8,128)(2,1)} %get-tuple-element.25), channel_id=1, source_target_pairs={{16,1},{17,2},{18,3},{19,0},{20,5},{21,6},{22,7},{23,4},{24,9},{25... | collective-permute-start | bytes 737288 | tf_op jit(solution)/shard_map/ppermute | solution.py:122
  11.5 1.3 %collective-permute-start.2 = (bf16[3,160,256]{2,1,0:T(8,128)(2,1)}, bf16[3,160,256]{2,1,0:T(8,128)(2,1)S(1)}, u32[]{:S(2)}, u32[]{:S(2)}) collective-permute-start(bf16[3,160,256]{2,1,0:T(8,128)(2,1)} %get-tuple-element.26), channel_id=1, source_target_pairs={{16,2},{17,3},{18,0},{19,1},{20,6},{21,7},{22,4},{23,5},{24,10},{2... | collective-permute-start | bytes 737288 | tf_op jit(solution)/shard_map/ppermute | solution.py:122
  12.8 1.3 %collective-permute-start.3 = (bf16[3,160,256]{2,1,0:T(8,128)(2,1)}, bf16[3,160,256]{2,1,0:T(8,128)(2,1)S(1)}, u32[]{:S(2)}, u32[]{:S(2)}) collective-permute-start(bf16[3,160,256]{2,1,0:T(8,128)(2,1)} %get-tuple-element.27), channel_id=1, source_target_pairs={{16,3},{17,0},{18,1},{19,2},{20,7},{21,4},{22,5},{23,6},{24,11},{2... | collective-permute-start | bytes 737288 | tf_op jit(solution)/shard_map/ppermute | solution.py:122
  14.1 15.6 %shard_map.69 = (bf16[3,160,768]{2,1,0:T(8,128)(2,1)}, bf16[3,160,768]{2,1,0:T(8,128)(2,1)}, bf16[3,160,768]{2,1,0:T(8,128)(2,1)}, bf16[3,160,768]{2,1,0:T(8,128)(2,1)}, f32[3,768]{1,0:T(4,128)}) custom-call(s32[1]{0:T(128)} %bitcast.part_ref, s32[640,1]{1,0:T(8,128)} %copy.8.pos_ref, bf16[640,1024]{1,0:T(8,128)(2,1)} %bitcast.25, ...), custom_call_target="tpu_custom_call" | custom-call | tf_op jit(solution)/shard_map/pallas_call | solution.py:69
  29.7 0.8 pad_maximum_fusion
  30.5 2.3 %collective-permute-done.2 = bf16[3,160,256]{2,1,0:T(8,128)(2,1)S(1)} collective-permute-done((bf16[3,160,256]{2,1,0:T(8,128)(2,1)}, bf16[3,160,256]{2,1,0:T(8,128)(2,1)S(1)}, u32[]{:S(2)}, u32[]{:S(2)}) %collective-permute-start.2) | collective-permute-done | bytes 245792 | tf_op jit(solution)/shard_map/ppermute | solution.py:122
  32.8 1.5 %collective-permute-done.3 = bf16[3,160,256]{2,1,0:T(8,128)(2,1)S(1)} collective-permute-done((bf16[3,160,256]{2,1,0:T(8,128)(2,1)}, bf16[3,160,256]{2,1,0:T(8,128)(2,1)S(1)}, u32[]{:S(2)}, u32[]{:S(2)}) %collective-permute-start.3) | collective-permute-done | bytes 245792 | tf_op jit(solution)/shard_map/ppermute | solution.py:122
  34.3 1.3 %collective-permute-start.4 = (f32[3,1024]{1,0:T(4,128)S(1)}, f32[3,1024]{1,0:T(4,128)S(1)}, u32[]{:S(2)}, u32[]{:S(2)}) collective-permute-start(f32[3,1024]{1,0:T(4,128)S(1)} %pad_maximum_fusion), channel_id=1, source_target_pairs={{16,0},{17,1},{18,2},{19,3},{20,4},{21,5},{22,6},{23,7},{24,8},{25... | collective-permute-start | bytes 36872 | tf_op jit(solution)/shard_map/ppermute | solution.py:115
  35.6 4.3 %collective-permute-done.4 = f32[3,1024]{1,0:T(4,128)S(1)} collective-permute-done((f32[3,1024]{1,0:T(4,128)S(1)}, f32[3,1024]{1,0:T(4,128)S(1)}, u32[]{:S(2)}, u32[]{:S(2)}) %collective-permute-start.4) | collective-permute-done | bytes 12320 | tf_op jit(solution)/shard_map/ppermute | solution.py:115
  40.0 1.3 %collective-permute-start.5 = (bf16[3,160,768]{2,1,0:T(8,128)(2,1)}, bf16[3,160,768]{2,1,0:T(8,128)(2,1)S(1)}, u32[]{:S(2)}, u32[]{:S(2)}) collective-permute-start(bf16[3,160,768]{2,1,0:T(8,128)(2,1)} %get-tuple-element.29), channel_id=1, source_target_pairs={{16,0},{17,1},{18,2},{19,3},{20,4},{21,5},{22,6},{23,7},{24,8},{25... | collective-permute-start | bytes 2211848 | tf_op jit(solution)/shard_map/ppermute | solution.py:122
  41.3 1.3 %collective-permute-start.6 = (bf16[3,160,768]{2,1,0:T(8,128)(2,1)}, bf16[3,160,768]{2,1,0:T(8,128)(2,1)S(1)}, u32[]{:S(2)}, u32[]{:S(2)}) collective-permute-start(bf16[3,160,768]{2,1,0:T(8,128)(2,1)} %get-tuple-element.30), channel_id=1, source_target_pairs={{16,1},{17,2},{18,3},{19,0},{20,5},{21,6},{22,7},{23,4},{24,9},{25... | collective-permute-start | bytes 2211848 | tf_op jit(solution)/shard_map/ppermute | solution.py:122
  42.7 0.5 broadcast_in_dim.26
  43.2 0.6 copy-done.3
  43.8 1.3 %collective-permute-start.7 = (bf16[3,160,768]{2,1,0:T(8,128)(2,1)S(1)}, bf16[3,160,768]{2,1,0:T(8,128)(2,1)S(1)}, u32[]{:S(2)}, u32[]{:S(2)}) collective-permute-start(bf16[3,160,768]{2,1,0:T(8,128)(2,1)S(1)} %copy-done.3), channel_id=1, source_target_pairs={{16,2},{17,3},{18,0},{19,1},{20,6},{21,7},{22,4},{23,5},{24,10},{2... | collective-permute-start | bytes 2211848 | tf_op jit(solution)/shard_map/ppermute | solution.py:122
  45.1 1.3 %collective-permute-start.8 = (bf16[3,160,768]{2,1,0:T(8,128)(2,1)S(1)}, bf16[3,160,768]{2,1,0:T(8,128)(2,1)S(1)}, u32[]{:S(2)}, u32[]{:S(2)}) collective-permute-start(bf16[3,160,768]{2,1,0:T(8,128)(2,1)S(1)} %copy-done.2), channel_id=1, source_target_pairs={{16,3},{17,0},{18,1},{19,2},{20,7},{21,4},{22,5},{23,6},{24,11},{2... | collective-permute-start | bytes 2211848 | tf_op jit(solution)/shard_map/ppermute | solution.py:122
  46.4 14.8 %collective-permute-done.5 = bf16[3,160,768]{2,1,0:T(8,128)(2,1)S(1)} collective-permute-done((bf16[3,160,768]{2,1,0:T(8,128)(2,1)}, bf16[3,160,768]{2,1,0:T(8,128)(2,1)S(1)}, u32[]{:S(2)}, u32[]{:S(2)}) %collective-permute-start.5) | collective-permute-done | bytes 737312 | tf_op jit(solution)/shard_map/ppermute | solution.py:122
  61.1 4.2 %collective-permute-start.9 = (f32[3,1024]{1,0:T(4,128)S(1)}, f32[3,1024]{1,0:T(4,128)S(1)}, u32[]{:S(2)}, u32[]{:S(2)}) collective-permute-start(f32[3,1024]{1,0:T(4,128)S(1)} %collective-permute-done.4), channel_id=1, source_target_pairs={{0,4},{4,0},{8,12},{12,8},{1,5},{5,1},{9,13},{13,9},{2,6},{6,2},{1... | collective-permute-start | bytes 36872 | tf_op jit(solution)/shard_map/ppermute | solution.py:129
  65.4 0.1 bitcast_dynamic-update-slice_fusion.3
  65.5 9.0 %collective-permute-done.6 = bf16[3,160,768]{2,1,0:T(8,128)(2,1)S(1)} collective-permute-done((bf16[3,160,768]{2,1,0:T(8,128)(2,1)}, bf16[3,160,768]{2,1,0:T(8,128)(2,1)S(1)}, u32[]{:S(2)}, u32[]{:S(2)}) %collective-permute-start.6) | collective-permute-done | bytes 737312 | tf_op jit(solution)/shard_map/ppermute | solution.py:122
  74.7 6.9 %collective-permute-start.10 = (f32[3,1024]{1,0:T(4,128)S(1)}, f32[3,1024]{1,0:T(4,128)S(1)}, u32[]{:S(2)}, u32[]{:S(2)}) collective-permute-start(f32[3,1024]{1,0:T(4,128)S(1)} %add.92), channel_id=1, source_target_pairs={{0,8},{4,12},{8,0},{12,4},{1,9},{5,13},{9,1},{13,5},{2,10},{6,14},... | collective-permute-start | bytes 36872 | tf_op jit(solution)/shard_map/ppermute | solution.py:129
  81.6 12.9 %collective-permute-done.7 = bf16[3,160,768]{2,1,0:T(8,128)(2,1)S(1)} collective-permute-done((bf16[3,160,768]{2,1,0:T(8,128)(2,1)S(1)}, bf16[3,160,768]{2,1,0:T(8,128)(2,1)S(1)}, u32[]{:S(2)}, u32[]{:S(2)}) %collective-permute-start.7) | collective-permute-done | bytes 737312 | tf_op jit(solution)/shard_map/ppermute | solution.py:122
  94.5 0.1 bitcast_dynamic-update-slice_fusion.1
  94.6 1.9 %collective-permute-start.11 = (f32[3,4096]{1,0:T(4,128)S(1)}, f32[3,4096]{1,0:T(4,128)S(1)}, u32[]{:S(2)}, u32[]{:S(2)}) collective-permute-start(f32[3,4096]{1,0:T(4,128)S(1)} %get-tuple-element.38), channel_id=1, source_target_pairs={{0,1},{1,0},{2,3},{3,2},{4,5},{5,4},{6,7},{7,6},{8,9},{9,8},{10,11... | collective-permute-start | bytes 147464 | tf_op jit(solution)/shard_map/ppermute | solution.py:129
  96.6 1.2 %collective-permute-done.11 = f32[3,4096]{1,0:T(4,128)S(1)} collective-permute-done((f32[3,4096]{1,0:T(4,128)S(1)}, f32[3,4096]{1,0:T(4,128)S(1)}, u32[]{:S(2)}, u32[]{:S(2)}) %collective-permute-start.11) | collective-permute-done | bytes 49184 | tf_op jit(solution)/shard_map/ppermute | solution.py:129
  97.8 1.9 %collective-permute-start.12 = (f32[3,4096]{1,0:T(4,128)S(1)}, f32[3,4096]{1,0:T(4,128)S(1)}, u32[]{:S(2)}, u32[]{:S(2)}) collective-permute-start(f32[3,4096]{1,0:T(4,128)S(1)} %add_dynamic-update-slice_fusion), channel_id=1, source_target_pairs={{0,2},{1,3},{2,0},{3,1},{4,6},{5,7},{6,4},{7,5},{8,10},{9,11},{10,... | collective-permute-start | bytes 147464 | tf_op jit(solution)/shard_map/ppermute | solution.py:129
  99.7 9.1 %collective-permute-done.8 = bf16[3,160,768]{2,1,0:T(8,128)(2,1)S(1)} collective-permute-done((bf16[3,160,768]{2,1,0:T(8,128)(2,1)S(1)}, bf16[3,160,768]{2,1,0:T(8,128)(2,1)S(1)}, u32[]{:S(2)}, u32[]{:S(2)}) %collective-permute-start.8) | collective-permute-done | bytes 737312 | tf_op jit(solution)/shard_map/ppermute | solution.py:122
  108.8 0.1 bitcast_dynamic-update-slice_fusion
  109.0 0.8 copy.10
  109.8 1.1 copy-done
  (21 shorter events, 0.3 us)
Async XLA Ops:
  8.9 20.8 %copy-start.1 = (f32[3,256]{1,0:T(4,128)S(1)}, f32[3,256]{1,0:T(4,128)}, u32[]{:S(2)}) copy-start(f32[3,256]{1,0:T(4,128)} %get-tuple-element.23) | copy-start | bytes 9220
  8.9 21.6 %collective-permute-start = (bf16[3,160,256]{2,1,0:T(8,128)(2,1)}, bf16[3,160,256]{2,1,0:T(8,128)(2,1)S(1)}, u32[]{:S(2)}, u32[]{:S(2)}) collective-permute-start(bf16[3,160,256]{2,1,0:T(8,128)(2,1)} %get-tuple-element.18), channel_id=1, source_target_pairs={{16,0},{17,1},{18,2},{19,3},{20,4},{21,5},{22,6},{23,7},{24,8},{25... | collective-permute-start | bytes 737288 | tf_op jit(solution)/shard_map/ppermute | solution.py:122
  10.2 20.3 %collective-permute-start.1 = (bf16[3,160,256]{2,1,0:T(8,128)(2,1)}, bf16[3,160,256]{2,1,0:T(8,128)(2,1)S(1)}, u32[]{:S(2)}, u32[]{:S(2)}) collective-permute-start(bf16[3,160,256]{2,1,0:T(8,128)(2,1)} %get-tuple-element.25), channel_id=1, source_target_pairs={{16,1},{17,2},{18,3},{19,0},{20,5},{21,6},{22,7},{23,4},{24,9},{25... | collective-permute-start | bytes 737288 | tf_op jit(solution)/shard_map/ppermute | solution.py:122
  11.5 21.3 %collective-permute-start.2 = (bf16[3,160,256]{2,1,0:T(8,128)(2,1)}, bf16[3,160,256]{2,1,0:T(8,128)(2,1)S(1)}, u32[]{:S(2)}, u32[]{:S(2)}) collective-permute-start(bf16[3,160,256]{2,1,0:T(8,128)(2,1)} %get-tuple-element.26), channel_id=1, source_target_pairs={{16,2},{17,3},{18,0},{19,1},{20,6},{21,7},{22,4},{23,5},{24,10},{2... | collective-permute-start | bytes 737288 | tf_op jit(solution)/shard_map/ppermute | solution.py:122
  12.8 21.5 %collective-permute-start.3 = (bf16[3,160,256]{2,1,0:T(8,128)(2,1)}, bf16[3,160,256]{2,1,0:T(8,128)(2,1)S(1)}, u32[]{:S(2)}, u32[]{:S(2)}) collective-permute-start(bf16[3,160,256]{2,1,0:T(8,128)(2,1)} %get-tuple-element.27), channel_id=1, source_target_pairs={{16,3},{17,0},{18,1},{19,2},{20,7},{21,4},{22,5},{23,6},{24,11},{2... | collective-permute-start | bytes 737288 | tf_op jit(solution)/shard_map/ppermute | solution.py:122
  29.7 15.4 %copy-start.2 = (bf16[3,160,768]{2,1,0:T(8,128)(2,1)S(1)}, bf16[3,160,768]{2,1,0:T(8,128)(2,1)}, u32[]{:S(2)}) copy-start(bf16[3,160,768]{2,1,0:T(8,128)(2,1)} %get-tuple-element.32) | copy-start | bytes 2211844
  34.3 5.6 %collective-permute-start.4 = (f32[3,1024]{1,0:T(4,128)S(1)}, f32[3,1024]{1,0:T(4,128)S(1)}, u32[]{:S(2)}, u32[]{:S(2)}) collective-permute-start(f32[3,1024]{1,0:T(4,128)S(1)} %pad_maximum_fusion), channel_id=1, source_target_pairs={{16,0},{17,1},{18,2},{19,3},{20,4},{21,5},{22,6},{23,7},{24,8},{25... | collective-permute-start | bytes 36872 | tf_op jit(solution)/shard_map/ppermute | solution.py:115
  40.0 21.2 %collective-permute-start.5 = (bf16[3,160,768]{2,1,0:T(8,128)(2,1)}, bf16[3,160,768]{2,1,0:T(8,128)(2,1)S(1)}, u32[]{:S(2)}, u32[]{:S(2)}) collective-permute-start(bf16[3,160,768]{2,1,0:T(8,128)(2,1)} %get-tuple-element.29), channel_id=1, source_target_pairs={{16,0},{17,1},{18,2},{19,3},{20,4},{21,5},{22,6},{23,7},{24,8},{25... | collective-permute-start | bytes 2211848 | tf_op jit(solution)/shard_map/ppermute | solution.py:122
  41.3 33.2 %collective-permute-start.6 = (bf16[3,160,768]{2,1,0:T(8,128)(2,1)}, bf16[3,160,768]{2,1,0:T(8,128)(2,1)S(1)}, u32[]{:S(2)}, u32[]{:S(2)}) collective-permute-start(bf16[3,160,768]{2,1,0:T(8,128)(2,1)} %get-tuple-element.30), channel_id=1, source_target_pairs={{16,1},{17,2},{18,3},{19,0},{20,5},{21,6},{22,7},{23,4},{24,9},{25... | collective-permute-start | bytes 2211848 | tf_op jit(solution)/shard_map/ppermute | solution.py:122
  42.6 1.1 %copy-start.3 = (bf16[3,160,768]{2,1,0:T(8,128)(2,1)S(1)}, bf16[3,160,768]{2,1,0:T(8,128)(2,1)}, u32[]{:S(2)}) copy-start(bf16[3,160,768]{2,1,0:T(8,128)(2,1)} %get-tuple-element.31) | copy-start | bytes 2211844
  43.8 50.7 %collective-permute-start.7 = (bf16[3,160,768]{2,1,0:T(8,128)(2,1)S(1)}, bf16[3,160,768]{2,1,0:T(8,128)(2,1)S(1)}, u32[]{:S(2)}, u32[]{:S(2)}) collective-permute-start(bf16[3,160,768]{2,1,0:T(8,128)(2,1)S(1)} %copy-done.3), channel_id=1, source_target_pairs={{16,2},{17,3},{18,0},{19,1},{20,6},{21,7},{22,4},{23,5},{24,10},{2... | collective-permute-start | bytes 2211848 | tf_op jit(solution)/shard_map/ppermute | solution.py:122
  45.1 63.8 %collective-permute-start.8 = (bf16[3,160,768]{2,1,0:T(8,128)(2,1)S(1)}, bf16[3,160,768]{2,1,0:T(8,128)(2,1)S(1)}, u32[]{:S(2)}, u32[]{:S(2)}) collective-permute-start(bf16[3,160,768]{2,1,0:T(8,128)(2,1)S(1)} %copy-done.2), channel_id=1, source_target_pairs={{16,3},{17,0},{18,1},{19,2},{20,7},{21,4},{22,5},{23,6},{24,11},{2... | collective-permute-start | bytes 2211848 | tf_op jit(solution)/shard_map/ppermute | solution.py:122
  61.1 13.5 %collective-permute-start.9 = (f32[3,1024]{1,0:T(4,128)S(1)}, f32[3,1024]{1,0:T(4,128)S(1)}, u32[]{:S(2)}, u32[]{:S(2)}) collective-permute-start(f32[3,1024]{1,0:T(4,128)S(1)} %collective-permute-done.4), channel_id=1, source_target_pairs={{0,4},{4,0},{8,12},{12,8},{1,5},{5,1},{9,13},{13,9},{2,6},{6,2},{1... | collective-permute-start | bytes 36872 | tf_op jit(solution)/shard_map/ppermute | solution.py:129
  74.7 19.9 %collective-permute-start.10 = (f32[3,1024]{1,0:T(4,128)S(1)}, f32[3,1024]{1,0:T(4,128)S(1)}, u32[]{:S(2)}, u32[]{:S(2)}) collective-permute-start(f32[3,1024]{1,0:T(4,128)S(1)} %add.92), channel_id=1, source_target_pairs={{0,8},{4,12},{8,0},{12,4},{1,9},{5,13},{9,1},{13,5},{2,10},{6,14},... | collective-permute-start | bytes 36872 | tf_op jit(solution)/shard_map/ppermute | solution.py:129
  94.6 3.1 %collective-permute-start.11 = (f32[3,4096]{1,0:T(4,128)S(1)}, f32[3,4096]{1,0:T(4,128)S(1)}, u32[]{:S(2)}, u32[]{:S(2)}) collective-permute-start(f32[3,4096]{1,0:T(4,128)S(1)} %get-tuple-element.38), channel_id=1, source_target_pairs={{0,1},{1,0},{2,3},{3,2},{4,5},{5,4},{6,7},{7,6},{8,9},{9,8},{10,11... | collective-permute-start | bytes 147464 | tf_op jit(solution)/shard_map/ppermute | solution.py:129
  97.8 11.1 %collective-permute-start.12 = (f32[3,4096]{1,0:T(4,128)S(1)}, f32[3,4096]{1,0:T(4,128)S(1)}, u32[]{:S(2)}, u32[]{:S(2)}) collective-permute-start(f32[3,4096]{1,0:T(4,128)S(1)} %add_dynamic-update-slice_fusion), channel_id=1, source_target_pairs={{0,2},{1,3},{2,0},{3,1},{4,6},{5,7},{6,4},{7,5},{8,10},{9,11},{10,... | collective-permute-start | bytes 147464 | tf_op jit(solution)/shard_map/ppermute | solution.py:129
  108.9 1.9 %copy-start = (bf16[1,1,3,160,4096]{4,3,2,1,0:T(8,128)(2,1)}, bf16[1,1,3,160,4096]{4,3,2,1,0:T(8,128)(2,1)S(1)}, u32[]{:S(2)}) copy-start(bf16[1,1,3,160,4096]{4,3,2,1,0:T(8,128)(2,1)S(1)} %bitcast_dynamic-update-slice_fusion) | copy-start | bytes 11796484

commit v7 on v6

--- a/solution.py
+++ b/solution.py
@@ -110,8 +110,6 @@
         tie = []
         if c == chunk_count - 1:
             own = jnp.concatenate(sums, axis=1)
-            if c > 0:
-                own = lax.optimization_barrier((own, [arrived[shift][c - 1] for shift in range(parts)]))[0]
             relayed = lax.ppermute(own, "section", [(s + 1, s) for s in range(sections - 1)])
             tie.append(relayed)
         if c > 0:

time: 111 us -> 108 us (0.973); the launches traced: 111 us -> 106 us
  waiting for transfers between devices: 55.1 us -> 52.6 us
  starting transfers between devices: 26.6 us -> 24.8 us
    ppermute x8, waiting for transfers between devices: 49.6 us -> 44.7 us  [per_device(): lax.ppermute(grads[shift], ('section', 'mp'), pairs(shift))]
    ppermute x1, waiting for transfers between devices: 4.33 us -> 6.76 us  [per_device(): lax.ppermute(own, 'section', [(s + 1, s) for s in range(sections - 1)])]
    ppermute x4, starting transfers between devices: 15 us -> 13.2 us  [receivers_sum(): value = value + lax.ppermute(value, ('section', axis), ring)]
    unnamed x9 -> x5, local copies, waits for them, and re-layouts: 2.5 us -> 1.9 us
  transfers between devices with their start and end apart: 13 -> 13, of which waited for: 8 -> 6; matrix products, arithmetic and copies ran while one was open for 2% -> 2% of each run, Pallas kernels for 14% -> 15%
where the time goes in v7:
time: 108 us; the launch traced here: 106 us
  waiting for transfers between devices  52.6 us (49%)
  starting transfers between devices  24.8 us (23%)
  Pallas kernels  22.3 us (21%)
  local copies, waits for them, and re-layouts  4.41 us (4%)
    ppermute x8, waiting for transfers between devices, per_device(): lax.ppermute(grads[shift], ('section', 'mp'), pairs(shift))  44.7 us
    pallas_call x2, Pallas kernels, chunk_grads(): pl.pallas_call(functools.partial(grads_kernel, parts=parts), grid_spec=gr...  22.3 us
    ppermute x4, starting transfers between devices, receivers_sum(): value = value + lax.ppermute(value, ('section', axis), ring)  13.2 us
    ppermute x8, starting transfers between devices, per_device(): lax.ppermute(grads[shift], ('section', 'mp'), pairs(shift))  10.3 us
    ppermute x1, waiting for transfers between devices, per_device(): lax.ppermute(own, 'section', [(s + 1, s) for s in range(sections - 1)])  6.76 us
  transfers between devices with their start and end apart: 13, of which 6 were waited for; matrix products, arithmetic and copies ran while one was open for 2% of the time, Pallas kernels for 15%

profile of v7, /device:TPU:0, one launch (start us, length us, event | category | flops | bytes accessed | tf_op | source)
XLA Modules:
  0.0 105.9 jit_solution(13627081440847743224)
XLA Ops:
  0.6 1.6 %copy.8.pos_ref = s32[640,1]{1,0:T(8,128)} copy(s32[640,1]{0,1:T(1,128)} %bitcast.32) | data formatting | bytes 5120 | tf_op jit(solution)/shard_map/reshape;squeeze | solution.py:82
  2.2 6.7 %shard_map.68 = (bf16[3,160,256]{2,1,0:T(8,128)(2,1)}, bf16[3,160,256]{2,1,0:T(8,128)(2,1)}, bf16[3,160,256]{2,1,0:T(8,128)(2,1)}, bf16[3,160,256]{2,1,0:T(8,128)(2,1)}, f32[3,256]{1,0:T(4,128)}) custom-call(s32[1]{0:T(128)} %bitcast.part_ref, s32[640,1]{1,0:T(8,128)} %copy.8.pos_ref, bf16[640,1024]{1,0:T(8,128)(2,1)} %bitcast.24, ...), custom_call_target="tpu_custom_call" | custom-call | tf_op jit(solution)/shard_map/pallas_call | solution.py:69
  8.9 1.3 %collective-permute-start = (bf16[3,160,256]{2,1,0:T(8,128)(2,1)}, bf16[3,160,256]{2,1,0:T(8,128)(2,1)S(1)}, u32[]{:S(2)}, u32[]{:S(2)}) collective-permute-start(bf16[3,160,256]{2,1,0:T(8,128)(2,1)} %get-tuple-element.17), channel_id=1, source_target_pairs={{16,0},{17,1},{18,2},{19,3},{20,4},{21,5},{22,6},{23,7},{24,8},{25... | collective-permute-start | bytes 737288 | tf_op jit(solution)/shard_map/ppermute | solution.py:120
  10.2 1.3 %collective-permute-start.2 = (bf16[3,160,256]{2,1,0:T(8,128)(2,1)}, bf16[3,160,256]{2,1,0:T(8,128)(2,1)S(1)}, u32[]{:S(2)}, u32[]{:S(2)}) collective-permute-start(bf16[3,160,256]{2,1,0:T(8,128)(2,1)} %get-tuple-element.24), channel_id=1, source_target_pairs={{16,1},{17,2},{18,3},{19,0},{20,5},{21,6},{22,7},{23,4},{24,9},{25... | collective-permute-start | bytes 737288 | tf_op jit(solution)/shard_map/ppermute | solution.py:120
  11.5 1.3 %collective-permute-start.3 = (bf16[3,160,256]{2,1,0:T(8,128)(2,1)}, bf16[3,160,256]{2,1,0:T(8,128)(2,1)S(1)}, u32[]{:S(2)}, u32[]{:S(2)}) collective-permute-start(bf16[3,160,256]{2,1,0:T(8,128)(2,1)} %get-tuple-element.25), channel_id=1, source_target_pairs={{16,2},{17,3},{18,0},{19,1},{20,6},{21,7},{22,4},{23,5},{24,10},{2... | collective-permute-start | bytes 737288 | tf_op jit(solution)/shard_map/ppermute | solution.py:120
  12.8 1.3 %collective-permute-start.4 = (bf16[3,160,256]{2,1,0:T(8,128)(2,1)}, bf16[3,160,256]{2,1,0:T(8,128)(2,1)S(1)}, u32[]{:S(2)}, u32[]{:S(2)}) collective-permute-start(bf16[3,160,256]{2,1,0:T(8,128)(2,1)} %get-tuple-element.26), channel_id=1, source_target_pairs={{16,3},{17,0},{18,1},{19,2},{20,7},{21,4},{22,5},{23,6},{24,11},{2... | collective-permute-start | bytes 737288 | tf_op jit(solution)/shard_map/ppermute | solution.py:120
  14.1 15.6 %shard_map.69 = (bf16[3,160,768]{2,1,0:T(8,128)(2,1)}, bf16[3,160,768]{2,1,0:T(8,128)(2,1)}, bf16[3,160,768]{2,1,0:T(8,128)(2,1)}, bf16[3,160,768]{2,1,0:T(8,128)(2,1)}, f32[3,768]{1,0:T(4,128)}) custom-call(s32[1]{0:T(128)} %bitcast.part_ref, s32[640,1]{1,0:T(8,128)} %copy.8.pos_ref, bf16[640,1024]{1,0:T(8,128)(2,1)} %bitcast.25, ...), custom_call_target="tpu_custom_call" | custom-call | tf_op jit(solution)/shard_map/pallas_call | solution.py:69
  29.7 0.7 pad_maximum_fusion
  30.4 1.3 %collective-permute-start.1 = (f32[3,1024]{1,0:T(4,128)S(1)}, f32[3,1024]{1,0:T(4,128)S(1)}, u32[]{:S(2)}, u32[]{:S(2)}) collective-permute-start(f32[3,1024]{1,0:T(4,128)S(1)} %pad_maximum_fusion), channel_id=1, source_target_pairs={{16,0},{17,1},{18,2},{19,3},{20,4},{21,5},{22,6},{23,7},{24,8},{25... | collective-permute-start | bytes 36872 | tf_op jit(solution)/shard_map/ppermute | solution.py:113
  31.7 6.8 %collective-permute-done.1 = f32[3,1024]{1,0:T(4,128)S(1)} collective-permute-done((f32[3,1024]{1,0:T(4,128)S(1)}, f32[3,1024]{1,0:T(4,128)S(1)}, u32[]{:S(2)}, u32[]{:S(2)}) %collective-permute-start.1) | collective-permute-done | bytes 12320 | tf_op jit(solution)/shard_map/ppermute | solution.py:113
  38.5 0.0 collective-permute-done.4
  38.5 1.3 %collective-permute-start.5 = (bf16[3,160,768]{2,1,0:T(8,128)(2,1)}, bf16[3,160,768]{2,1,0:T(8,128)(2,1)S(1)}, u32[]{:S(2)}, u32[]{:S(2)}) collective-permute-start(bf16[3,160,768]{2,1,0:T(8,128)(2,1)} %get-tuple-element.27), channel_id=1, source_target_pairs={{16,0},{17,1},{18,2},{19,3},{20,4},{21,5},{22,6},{23,7},{24,8},{25... | collective-permute-start | bytes 2211848 | tf_op jit(solution)/shard_map/ppermute | solution.py:120
  39.8 1.3 %collective-permute-start.6 = (bf16[3,160,768]{2,1,0:T(8,128)(2,1)}, bf16[3,160,768]{2,1,0:T(8,128)(2,1)S(1)}, u32[]{:S(2)}, u32[]{:S(2)}) collective-permute-start(bf16[3,160,768]{2,1,0:T(8,128)(2,1)} %get-tuple-element.28), channel_id=1, source_target_pairs={{16,1},{17,2},{18,3},{19,0},{20,5},{21,6},{22,7},{23,4},{24,9},{25... | collective-permute-start | bytes 2211848 | tf_op jit(solution)/shard_map/ppermute | solution.py:120
  41.2 1.3 %collective-permute-start.7 = (bf16[3,160,768]{2,1,0:T(8,128)(2,1)}, bf16[3,160,768]{2,1,0:T(8,128)(2,1)S(1)}, u32[]{:S(2)}, u32[]{:S(2)}) collective-permute-start(bf16[3,160,768]{2,1,0:T(8,128)(2,1)} %get-tuple-element.29), channel_id=1, source_target_pairs={{16,2},{17,3},{18,0},{19,1},{20,6},{21,7},{22,4},{23,5},{24,10},{2... | collective-permute-start | bytes 2211848 | tf_op jit(solution)/shard_map/ppermute | solution.py:120
  42.5 1.3 %collective-permute-start.8 = (bf16[3,160,768]{2,1,0:T(8,128)(2,1)}, bf16[3,160,768]{2,1,0:T(8,128)(2,1)S(1)}, u32[]{:S(2)}, u32[]{:S(2)}) collective-permute-start(bf16[3,160,768]{2,1,0:T(8,128)(2,1)} %get-tuple-element.30), channel_id=1, source_target_pairs={{16,3},{17,0},{18,1},{19,2},{20,7},{21,4},{22,5},{23,6},{24,11},{2... | collective-permute-start | bytes 2211848 | tf_op jit(solution)/shard_map/ppermute | solution.py:120
  43.8 0.5 broadcast_in_dim.26
  44.3 15.7 %collective-permute-done.5 = bf16[3,160,768]{2,1,0:T(8,128)(2,1)S(1)} collective-permute-done((bf16[3,160,768]{2,1,0:T(8,128)(2,1)}, bf16[3,160,768]{2,1,0:T(8,128)(2,1)S(1)}, u32[]{:S(2)}, u32[]{:S(2)}) %collective-permute-start.5) | collective-permute-done | bytes 737312 | tf_op jit(solution)/shard_map/ppermute | solution.py:120
  60.0 3.6 %collective-permute-start.9 = (f32[3,1024]{1,0:T(4,128)S(1)}, f32[3,1024]{1,0:T(4,128)S(1)}, u32[]{:S(2)}, u32[]{:S(2)}) collective-permute-start(f32[3,1024]{1,0:T(4,128)S(1)} %collective-permute-done.1), channel_id=1, source_target_pairs={{0,4},{4,0},{8,12},{12,8},{1,5},{5,1},{9,13},{13,9},{2,6},{6,2},{1... | collective-permute-start | bytes 36872 | tf_op jit(solution)/shard_map/ppermute | solution.py:127
  63.6 0.1 bitcast_dynamic-update-slice_fusion.3
  63.7 8.3 %collective-permute-done.6 = bf16[3,160,768]{2,1,0:T(8,128)(2,1)S(1)} collective-permute-done((bf16[3,160,768]{2,1,0:T(8,128)(2,1)}, bf16[3,160,768]{2,1,0:T(8,128)(2,1)S(1)}, u32[]{:S(2)}, u32[]{:S(2)}) %collective-permute-start.6) | collective-permute-done | bytes 737312 | tf_op jit(solution)/shard_map/ppermute | solution.py:120
  72.1 0.1 bitcast_dynamic-update-slice_fusion.2
  72.2 4.5 %collective-permute-start.10 = (f32[3,1024]{1,0:T(4,128)S(1)}, f32[3,1024]{1,0:T(4,128)S(1)}, u32[]{:S(2)}, u32[]{:S(2)}) collective-permute-start(f32[3,1024]{1,0:T(4,128)S(1)} %add.92), channel_id=1, source_target_pairs={{0,8},{4,12},{8,0},{12,4},{1,9},{5,13},{9,1},{13,5},{2,10},{6,14},... | collective-permute-start | bytes 36872 | tf_op jit(solution)/shard_map/ppermute | solution.py:127
  76.7 15.0 %collective-permute-done.7 = bf16[3,160,768]{2,1,0:T(8,128)(2,1)S(1)} collective-permute-done((bf16[3,160,768]{2,1,0:T(8,128)(2,1)}, bf16[3,160,768]{2,1,0:T(8,128)(2,1)S(1)}, u32[]{:S(2)}, u32[]{:S(2)}) %collective-permute-start.7) | collective-permute-done | bytes 737312 | tf_op jit(solution)/shard_map/ppermute | solution.py:120
  91.8 0.1 bitcast_dynamic-update-slice_fusion.1
  91.9 1.9 %collective-permute-start.11 = (f32[3,4096]{1,0:T(4,128)S(1)}, f32[3,4096]{1,0:T(4,128)S(1)}, u32[]{:S(2)}, u32[]{:S(2)}) collective-permute-start(f32[3,4096]{1,0:T(4,128)S(1)} %get-tuple-element.36), channel_id=1, source_target_pairs={{0,1},{1,0},{2,3},{3,2},{4,5},{5,4},{6,7},{7,6},{8,9},{9,8},{10,11... | collective-permute-start | bytes 147464 | tf_op jit(solution)/shard_map/ppermute | solution.py:127
  93.9 1.2 %collective-permute-done.11 = f32[3,4096]{1,0:T(4,128)S(1)} collective-permute-done((f32[3,4096]{1,0:T(4,128)S(1)}, f32[3,4096]{1,0:T(4,128)S(1)}, u32[]{:S(2)}, u32[]{:S(2)}) %collective-permute-start.11) | collective-permute-done | bytes 49184 | tf_op jit(solution)/shard_map/ppermute | solution.py:127
  95.1 3.2 %collective-permute-start.12 = (f32[3,4096]{1,0:T(4,128)S(1)}, f32[3,4096]{1,0:T(4,128)S(1)}, u32[]{:S(2)}, u32[]{:S(2)}) collective-permute-start(f32[3,4096]{1,0:T(4,128)S(1)} %add_dynamic-update-slice_fusion), channel_id=1, source_target_pairs={{0,2},{1,3},{2,0},{3,1},{4,6},{5,7},{6,4},{7,5},{8,10},{9,11},{10,... | collective-permute-start | bytes 147464 | tf_op jit(solution)/shard_map/ppermute | solution.py:127
  98.3 5.6 %collective-permute-done.8 = bf16[3,160,768]{2,1,0:T(8,128)(2,1)S(1)} collective-permute-done((bf16[3,160,768]{2,1,0:T(8,128)(2,1)}, bf16[3,160,768]{2,1,0:T(8,128)(2,1)S(1)}, u32[]{:S(2)}, u32[]{:S(2)}) %collective-permute-start.8) | collective-permute-done | bytes 737312 | tf_op jit(solution)/shard_map/ppermute | solution.py:120
  103.9 0.1 bitcast_dynamic-update-slice_fusion
  104.0 0.0 copy-start
  104.0 0.8 copy.10
  104.8 1.1 %copy-done = bf16[1,1,3,160,4096]{4,3,2,1,0:T(8,128)(2,1)} copy-done((bf16[1,1,3,160,4096]{4,3,2,1,0:T(8,128)(2,1)}, bf16[1,1,3,160,4096]{4,3,2,1,0:T(8,128)(2,1)S(1)}, u32[]{:S(2)}) %copy-start) | copy-done | bytes 3932184
  (17 shorter events, 0.2 us)
Async XLA Ops:
  8.9 20.8 %copy-start.1 = (f32[3,256]{1,0:T(4,128)S(1)}, f32[3,256]{1,0:T(4,128)}, u32[]{:S(2)}) copy-start(f32[3,256]{1,0:T(4,128)} %get-tuple-element.22) | copy-start | bytes 9220
  8.9 29.6 %collective-permute-start = (bf16[3,160,256]{2,1,0:T(8,128)(2,1)}, bf16[3,160,256]{2,1,0:T(8,128)(2,1)S(1)}, u32[]{:S(2)}, u32[]{:S(2)}) collective-permute-start(bf16[3,160,256]{2,1,0:T(8,128)(2,1)} %get-tuple-element.17), channel_id=1, source_target_pairs={{16,0},{17,1},{18,2},{19,3},{20,4},{21,5},{22,6},{23,7},{24,8},{25... | collective-permute-start | bytes 737288 | tf_op jit(solution)/shard_map/ppermute | solution.py:120
  10.2 28.3 %collective-permute-start.2 = (bf16[3,160,256]{2,1,0:T(8,128)(2,1)}, bf16[3,160,256]{2,1,0:T(8,128)(2,1)S(1)}, u32[]{:S(2)}, u32[]{:S(2)}) collective-permute-start(bf16[3,160,256]{2,1,0:T(8,128)(2,1)} %get-tuple-element.24), channel_id=1, source_target_pairs={{16,1},{17,2},{18,3},{19,0},{20,5},{21,6},{22,7},{23,4},{24,9},{25... | collective-permute-start | bytes 737288 | tf_op jit(solution)/shard_map/ppermute | solution.py:120
  11.5 27.0 %collective-permute-start.3 = (bf16[3,160,256]{2,1,0:T(8,128)(2,1)}, bf16[3,160,256]{2,1,0:T(8,128)(2,1)S(1)}, u32[]{:S(2)}, u32[]{:S(2)}) collective-permute-start(bf16[3,160,256]{2,1,0:T(8,128)(2,1)} %get-tuple-element.25), channel_id=1, source_target_pairs={{16,2},{17,3},{18,0},{19,1},{20,6},{21,7},{22,4},{23,5},{24,10},{2... | collective-permute-start | bytes 737288 | tf_op jit(solution)/shard_map/ppermute | solution.py:120
  12.8 25.7 %collective-permute-start.4 = (bf16[3,160,256]{2,1,0:T(8,128)(2,1)}, bf16[3,160,256]{2,1,0:T(8,128)(2,1)S(1)}, u32[]{:S(2)}, u32[]{:S(2)}) collective-permute-start(bf16[3,160,256]{2,1,0:T(8,128)(2,1)} %get-tuple-element.26), channel_id=1, source_target_pairs={{16,3},{17,0},{18,1},{19,2},{20,7},{21,4},{22,5},{23,6},{24,11},{2... | collective-permute-start | bytes 737288 | tf_op jit(solution)/shard_map/ppermute | solution.py:120
  30.4 8.0 %collective-permute-start.1 = (f32[3,1024]{1,0:T(4,128)S(1)}, f32[3,1024]{1,0:T(4,128)S(1)}, u32[]{:S(2)}, u32[]{:S(2)}) collective-permute-start(f32[3,1024]{1,0:T(4,128)S(1)} %pad_maximum_fusion), channel_id=1, source_target_pairs={{16,0},{17,1},{18,2},{19,3},{20,4},{21,5},{22,6},{23,7},{24,8},{25... | collective-permute-start | bytes 36872 | tf_op jit(solution)/shard_map/ppermute | solution.py:113
  38.5 21.5 %collective-permute-start.5 = (bf16[3,160,768]{2,1,0:T(8,128)(2,1)}, bf16[3,160,768]{2,1,0:T(8,128)(2,1)S(1)}, u32[]{:S(2)}, u32[]{:S(2)}) collective-permute-start(bf16[3,160,768]{2,1,0:T(8,128)(2,1)} %get-tuple-element.27), channel_id=1, source_target_pairs={{16,0},{17,1},{18,2},{19,3},{20,4},{21,5},{22,6},{23,7},{24,8},{25... | collective-permute-start | bytes 2211848 | tf_op jit(solution)/shard_map/ppermute | solution.py:120
  39.8 32.2 %collective-permute-start.6 = (bf16[3,160,768]{2,1,0:T(8,128)(2,1)}, bf16[3,160,768]{2,1,0:T(8,128)(2,1)S(1)}, u32[]{:S(2)}, u32[]{:S(2)}) collective-permute-start(bf16[3,160,768]{2,1,0:T(8,128)(2,1)} %get-tuple-element.28), channel_id=1, source_target_pairs={{16,1},{17,2},{18,3},{19,0},{20,5},{21,6},{22,7},{23,4},{24,9},{25... | collective-permute-start | bytes 2211848 | tf_op jit(solution)/shard_map/ppermute | solution.py:120
  41.2 50.6 %collective-permute-start.7 = (bf16[3,160,768]{2,1,0:T(8,128)(2,1)}, bf16[3,160,768]{2,1,0:T(8,128)(2,1)S(1)}, u32[]{:S(2)}, u32[]{:S(2)}) collective-permute-start(bf16[3,160,768]{2,1,0:T(8,128)(2,1)} %get-tuple-element.29), channel_id=1, source_target_pairs={{16,2},{17,3},{18,0},{19,1},{20,6},{21,7},{22,4},{23,5},{24,10},{2... | collective-permute-start | bytes 2211848 | tf_op jit(solution)/shard_map/ppermute | solution.py:120
  42.5 61.4 %collective-permute-start.8 = (bf16[3,160,768]{2,1,0:T(8,128)(2,1)}, bf16[3,160,768]{2,1,0:T(8,128)(2,1)S(1)}, u32[]{:S(2)}, u32[]{:S(2)}) collective-permute-start(bf16[3,160,768]{2,1,0:T(8,128)(2,1)} %get-tuple-element.30), channel_id=1, source_target_pairs={{16,3},{17,0},{18,1},{19,2},{20,7},{21,4},{22,5},{23,6},{24,11},{2... | collective-permute-start | bytes 2211848 | tf_op jit(solution)/shard_map/ppermute | solution.py:120
  60.0 12.2 %collective-permute-start.9 = (f32[3,1024]{1,0:T(4,128)S(1)}, f32[3,1024]{1,0:T(4,128)S(1)}, u32[]{:S(2)}, u32[]{:S(2)}) collective-permute-start(f32[3,1024]{1,0:T(4,128)S(1)} %collective-permute-done.1), channel_id=1, source_target_pairs={{0,4},{4,0},{8,12},{12,8},{1,5},{5,1},{9,13},{13,9},{2,6},{6,2},{1... | collective-permute-start | bytes 36872 | tf_op jit(solution)/shard_map/ppermute | solution.py:127
  72.2 19.6 %collective-permute-start.10 = (f32[3,1024]{1,0:T(4,128)S(1)}, f32[3,1024]{1,0:T(4,128)S(1)}, u32[]{:S(2)}, u32[]{:S(2)}) collective-permute-start(f32[3,1024]{1,0:T(4,128)S(1)} %add.92), channel_id=1, source_target_pairs={{0,8},{4,12},{8,0},{12,4},{1,9},{5,13},{9,1},{13,5},{2,10},{6,14},... | collective-permute-start | bytes 36872 | tf_op jit(solution)/shard_map/ppermute | solution.py:127
  91.9 3.1 %collective-permute-start.11 = (f32[3,4096]{1,0:T(4,128)S(1)}, f32[3,4096]{1,0:T(4,128)S(1)}, u32[]{:S(2)}, u32[]{:S(2)}) collective-permute-start(f32[3,4096]{1,0:T(4,128)S(1)} %get-tuple-element.36), channel_id=1, source_target_pairs={{0,1},{1,0},{2,3},{3,2},{4,5},{5,4},{6,7},{7,6},{8,9},{9,8},{10,11... | collective-permute-start | bytes 147464 | tf_op jit(solution)/shard_map/ppermute | solution.py:127
  95.1 8.9 %collective-permute-start.12 = (f32[3,4096]{1,0:T(4,128)S(1)}, f32[3,4096]{1,0:T(4,128)S(1)}, u32[]{:S(2)}, u32[]{:S(2)}) collective-permute-start(f32[3,4096]{1,0:T(4,128)S(1)} %add_dynamic-update-slice_fusion), channel_id=1, source_target_pairs={{0,2},{1,3},{2,0},{3,1},{4,6},{5,7},{6,4},{7,5},{8,10},{9,11},{10,... | collective-permute-start | bytes 147464 | tf_op jit(solution)/shard_map/ppermute | solution.py:127
  104.0 1.9 %copy-start = (bf16[1,1,3,160,4096]{4,3,2,1,0:T(8,128)(2,1)}, bf16[1,1,3,160,4096]{4,3,2,1,0:T(8,128)(2,1)S(1)}, u32[]{:S(2)}) copy-start(bf16[1,1,3,160,4096]{4,3,2,1,0:T(8,128)(2,1)S(1)} %bitcast_dynamic-update-slice_fusion) | copy-start | bytes 11796484

commit v8 on v7

--- a/solution.py
+++ b/solution.py
@@ -24,21 +24,21 @@
         k = k_ref[lo : lo + window, :]
         v = v_ref[lo : lo + window, :]
         g = g_ref[lo : lo + window, :]
-        scores = lax.dot_general(q, k, NT, preferred_element_type=jnp.float32) * scaling
-        qi = lo + lax.broadcasted_iota(jnp.int32, (window, window), 0)
-        kj = lo + lax.broadcasted_iota(jnp.int32, (window, window), 1)
-        start = qi - pos_ref[lo : lo + window, :]
+        scores = lax.dot_general(k, q, NT, preferred_element_type=jnp.float32) * scaling
+        kj = lo + lax.broadcasted_iota(jnp.int32, (window, window), 0)
+        qi = lo + lax.broadcasted_iota(jnp.int32, (window, window), 1)
+        start = lo + lax.broadcasted_iota(jnp.int32, (1, window), 1) - pos_ref[:, lo : lo + window]
         allowed = (kj <= qi) & (kj >= start)
         scores = jnp.where(allowed, scores, jnp.float32(-1e30))
-        highest = jnp.max(scores, axis=1, keepdims=True)
+        highest = jnp.max(scores, axis=0, keepdims=True)
         expont = jnp.exp(scores - highest)
-        attn = expont / jnp.sum(expont, axis=1, keepdims=True)
-        grad_v = jnp.dot(attn.T.astype(jnp.bfloat16), g, preferred_element_type=jnp.float32)
-        grad_attn = lax.dot_general(g, v, NT, preferred_element_type=jnp.float32)
-        delta = jnp.sum(attn * grad_attn, axis=1, keepdims=True)
+        attn = expont / jnp.sum(expont, axis=0, keepdims=True)
+        grad_v = jnp.dot(attn.astype(jnp.bfloat16), g, preferred_element_type=jnp.float32)
+        grad_attn = lax.dot_general(v, g, NT, preferred_element_type=jnp.float32)
+        delta = jnp.sum(attn * grad_attn, axis=0, keepdims=True)
         grad_scores = attn * (grad_attn - delta) * scaling
-        grad_q = jnp.dot(grad_scores.astype(jnp.bfloat16), k, preferred_element_type=jnp.float32)
-        grad_k = jnp.dot(grad_scores.T.astype(jnp.bfloat16), q, preferred_element_type=jnp.float32)
+        grad_k = jnp.dot(grad_scores.astype(jnp.bfloat16), q, preferred_element_type=jnp.float32)
+        grad_q = jnp.dot(grad_scores.T.astype(jnp.bfloat16), k, preferred_element_type=jnp.float32)
         keep = b * half - lo
         for i, grad in enumerate((grad_q, grad_k, grad_v)):
             full_ref[i, b * half : (b + 1) * half, :] = grad[keep : keep + half].astype(jnp.bfloat16)
@@ -61,7 +61,7 @@
     grid_spec = pltpu.PrefetchScalarGridSpec(
         num_scalar_prefetch=1,
         grid=(heads,),
-        in_specs=[pl.BlockSpec((length, 1), lambda h, part_ref: (0, 0))] + [in_block] * 4,
+        in_specs=[pl.BlockSpec((1, length), lambda h, part_ref: (0, 0))] + [in_block] * 4,
         out_specs=[pl.BlockSpec((3, rows, HEAD_DIM), lambda h, part_ref: (0, 0, h))] * parts
         + [pl.BlockSpec((3, HEAD_DIM), lambda h, part_ref: (0, h))],
         scratch_shapes=[pltpu.VMEM((3, length, HEAD_DIM), jnp.bfloat16)],
@@ -79,7 +79,7 @@
     key_rows = keys[0, 0]
     value_rows = values[0, 0]
     grad_rows = grad_out[0, 0]
-    token_positions = positions[0, 0].reshape(-1, 1)
+    token_positions = positions[0, 0].reshape(1, -1)
     length, columns = query_rows.shape
     sections = lax.axis_size("section")
     parts = lax.axis_size("mp")

time: 108 us -> 104 us (0.963); the launches traced: 106 us -> 104 us
  Pallas kernels: 22.3 us -> 19.1 us
  waiting for transfers between devices: 52.6 us -> 54.7 us
  local copies, waits for them, and re-layouts: 4.41 us -> 2.83 us
    pallas_call x2, Pallas kernels: 22.3 us -> 19.1 us  [chunk_grads(): pl.pallas_call(functools.partial(grads_kernel, parts=parts), grid_spec=gr...]
    ppermute x8, waiting for transfers between devices: 44.7 us -> 46.7 us  [per_device(): lax.ppermute(grads[shift], ('section', 'mp'), pairs(shift))]
    another operation x1 -> x0, local copies, waits for them, and re-layouts: 1.58 us -> none  [per_device(): token_positions = positions[0, 0].reshape(-1, 1)]
  transfers between devices with their start and end apart: 13 -> 13, of which waited for: 6 -> 6; matrix products, arithmetic and copies ran while one was open for 2% -> 2% of each run, Pallas kernels for 15% -> 13%
where the time goes in v8:
time: 104 us
  waiting for transfers between devices  54.7 us (53%)
  starting transfers between devices  25.6 us (25%)
  Pallas kernels  19.1 us (18%)
  local copies, waits for them, and re-layouts  2.83 us (3%)
    ppermute x8, waiting for transfers between devices, per_device(): lax.ppermute(grads[shift], ('section', 'mp'), pairs(shift))  46.7 us
    pallas_call x2, Pallas kernels, chunk_grads(): pl.pallas_call(functools.partial(grads_kernel, parts=parts), grid_spec=gr...  19.1 us
    ppermute x4, starting transfers between devices, receivers_sum(): value = value + lax.ppermute(value, ('section', axis), ring)  13.9 us
    ppermute x8, starting transfers between devices, per_device(): lax.ppermute(grads[shift], ('section', 'mp'), pairs(shift))  10.3 us
    ppermute x1, waiting for transfers between devices, per_device(): lax.ppermute(own, 'section', [(s + 1, s) for s in range(sections - 1)])  6.76 us
  transfers between devices with their start and end apart: 13, of which 6 were waited for; matrix products, arithmetic and copies ran while one was open for 2% of the time, Pallas kernels for 13%

profile of v8, /device:TPU:0, one launch (start us, length us, event | category | flops | bytes accessed | tf_op | source)
XLA Modules:
  0.0 104.0 jit_solution(17862679461151394026)
XLA Ops:
  0.6 5.7 %shard_map.68 = (bf16[3,160,256]{2,1,0:T(8,128)(2,1)}, bf16[3,160,256]{2,1,0:T(8,128)(2,1)}, bf16[3,160,256]{2,1,0:T(8,128)(2,1)}, bf16[3,160,256]{2,1,0:T(8,128)(2,1)}, f32[3,256]{1,0:T(4,128)}) custom-call(s32[1]{0:T(128)} %bitcast.part_ref, s32[1,640]{1,0:T(1,128)} %bitcast.32, bf16[640,1024]{1,0:T(8,128)(2,1)} %bitcast.24, bf16[640,1024]{1,0:T(8,128)(2,1)} %bitcast.26, ...), custom_call_target="tpu_custom_call" | custom-call | tf_op jit(solution)/shard_map/pallas_call | solution.py:69
  6.4 1.3 %collective-permute-start = (bf16[3,160,256]{2,1,0:T(8,128)(2,1)}, bf16[3,160,256]{2,1,0:T(8,128)(2,1)S(1)}, u32[]{:S(2)}, u32[]{:S(2)}) collective-permute-start(bf16[3,160,256]{2,1,0:T(8,128)(2,1)} %get-tuple-element.17), channel_id=1, source_target_pairs={{16,0},{17,1},{18,2},{19,3},{20,4},{21,5},{22,6},{23,7},{24,8},{25... | collective-permute-start | bytes 737288 | tf_op jit(solution)/shard_map/ppermute | solution.py:120
  7.7 1.3 %collective-permute-start.2 = (bf16[3,160,256]{2,1,0:T(8,128)(2,1)}, bf16[3,160,256]{2,1,0:T(8,128)(2,1)S(1)}, u32[]{:S(2)}, u32[]{:S(2)}) collective-permute-start(bf16[3,160,256]{2,1,0:T(8,128)(2,1)} %get-tuple-element.24), channel_id=1, source_target_pairs={{16,1},{17,2},{18,3},{19,0},{20,5},{21,6},{22,7},{23,4},{24,9},{25... | collective-permute-start | bytes 737288 | tf_op jit(solution)/shard_map/ppermute | solution.py:120
  9.0 1.3 %collective-permute-start.3 = (bf16[3,160,256]{2,1,0:T(8,128)(2,1)}, bf16[3,160,256]{2,1,0:T(8,128)(2,1)S(1)}, u32[]{:S(2)}, u32[]{:S(2)}) collective-permute-start(bf16[3,160,256]{2,1,0:T(8,128)(2,1)} %get-tuple-element.25), channel_id=1, source_target_pairs={{16,2},{17,3},{18,0},{19,1},{20,6},{21,7},{22,4},{23,5},{24,10},{2... | collective-permute-start | bytes 737288 | tf_op jit(solution)/shard_map/ppermute | solution.py:120
  10.3 1.3 %collective-permute-start.4 = (bf16[3,160,256]{2,1,0:T(8,128)(2,1)}, bf16[3,160,256]{2,1,0:T(8,128)(2,1)S(1)}, u32[]{:S(2)}, u32[]{:S(2)}) collective-permute-start(bf16[3,160,256]{2,1,0:T(8,128)(2,1)} %get-tuple-element.26), channel_id=1, source_target_pairs={{16,3},{17,0},{18,1},{19,2},{20,7},{21,4},{22,5},{23,6},{24,11},{2... | collective-permute-start | bytes 737288 | tf_op jit(solution)/shard_map/ppermute | solution.py:120
  11.6 13.4 %shard_map.69 = (bf16[3,160,768]{2,1,0:T(8,128)(2,1)}, bf16[3,160,768]{2,1,0:T(8,128)(2,1)}, bf16[3,160,768]{2,1,0:T(8,128)(2,1)}, bf16[3,160,768]{2,1,0:T(8,128)(2,1)}, f32[3,768]{1,0:T(4,128)}) custom-call(s32[1]{0:T(128)} %bitcast.part_ref, s32[1,640]{1,0:T(1,128)} %bitcast.33, bf16[640,1024]{1,0:T(8,128)(2,1)} %bitcast.25, bf16[640,1024]{1,0:T(8,128)(2,1)} %bitcast.27, ...), custom_call_target="tpu_custom_call" | custom-call | tf_op jit(solution)/shard_map/pallas_call | solution.py:69
  25.0 0.7 pad_maximum_fusion
  25.7 1.3 %collective-permute-start.1 = (f32[3,1024]{1,0:T(4,128)S(1)}, f32[3,1024]{1,0:T(4,128)S(1)}, u32[]{:S(2)}, u32[]{:S(2)}) collective-permute-start(f32[3,1024]{1,0:T(4,128)S(1)} %pad_maximum_fusion), channel_id=1, source_target_pairs={{16,0},{17,1},{18,2},{19,3},{20,4},{21,5},{22,6},{23,7},{24,8},{25... | collective-permute-start | bytes 36872 | tf_op jit(solution)/shard_map/ppermute | solution.py:113
  27.0 6.8 %collective-permute-done.1 = f32[3,1024]{1,0:T(4,128)S(1)} collective-permute-done((f32[3,1024]{1,0:T(4,128)S(1)}, f32[3,1024]{1,0:T(4,128)S(1)}, u32[]{:S(2)}, u32[]{:S(2)}) %collective-permute-start.1) | collective-permute-done | bytes 12320 | tf_op jit(solution)/shard_map/ppermute | solution.py:113
  33.7 0.0 collective-permute-done
  33.7 0.0 collective-permute-done.2
  33.8 1.3 %collective-permute-start.5 = (bf16[3,160,768]{2,1,0:T(8,128)(2,1)}, bf16[3,160,768]{2,1,0:T(8,128)(2,1)S(1)}, u32[]{:S(2)}, u32[]{:S(2)}) collective-permute-start(bf16[3,160,768]{2,1,0:T(8,128)(2,1)} %get-tuple-element.27), channel_id=1, source_target_pairs={{16,0},{17,1},{18,2},{19,3},{20,4},{21,5},{22,6},{23,7},{24,8},{25... | collective-permute-start | bytes 2211848 | tf_op jit(solution)/shard_map/ppermute | solution.py:120
  35.1 1.3 %collective-permute-start.6 = (bf16[3,160,768]{2,1,0:T(8,128)(2,1)}, bf16[3,160,768]{2,1,0:T(8,128)(2,1)S(1)}, u32[]{:S(2)}, u32[]{:S(2)}) collective-permute-start(bf16[3,160,768]{2,1,0:T(8,128)(2,1)} %get-tuple-element.28), channel_id=1, source_target_pairs={{16,1},{17,2},{18,3},{19,0},{20,5},{21,6},{22,7},{23,4},{24,9},{25... | collective-permute-start | bytes 2211848 | tf_op jit(solution)/shard_map/ppermute | solution.py:120
  36.4 1.3 %collective-permute-start.7 = (bf16[3,160,768]{2,1,0:T(8,128)(2,1)}, bf16[3,160,768]{2,1,0:T(8,128)(2,1)S(1)}, u32[]{:S(2)}, u32[]{:S(2)}) collective-permute-start(bf16[3,160,768]{2,1,0:T(8,128)(2,1)} %get-tuple-element.29), channel_id=1, source_target_pairs={{16,2},{17,3},{18,0},{19,1},{20,6},{21,7},{22,4},{23,5},{24,10},{2... | collective-permute-start | bytes 2211848 | tf_op jit(solution)/shard_map/ppermute | solution.py:120
  37.7 1.3 %collective-permute-start.8 = (bf16[3,160,768]{2,1,0:T(8,128)(2,1)}, bf16[3,160,768]{2,1,0:T(8,128)(2,1)S(1)}, u32[]{:S(2)}, u32[]{:S(2)}) collective-permute-start(bf16[3,160,768]{2,1,0:T(8,128)(2,1)} %get-tuple-element.30), channel_id=1, source_target_pairs={{16,3},{17,0},{18,1},{19,2},{20,7},{21,4},{22,5},{23,6},{24,11},{2... | collective-permute-start | bytes 2211848 | tf_op jit(solution)/shard_map/ppermute | solution.py:120
  39.0 0.5 broadcast_in_dim.26
  39.6 15.7 %collective-permute-done.5 = bf16[3,160,768]{2,1,0:T(8,128)(2,1)S(1)} collective-permute-done((bf16[3,160,768]{2,1,0:T(8,128)(2,1)}, bf16[3,160,768]{2,1,0:T(8,128)(2,1)S(1)}, u32[]{:S(2)}, u32[]{:S(2)}) %collective-permute-start.5) | collective-permute-done | bytes 737312 | tf_op jit(solution)/shard_map/ppermute | solution.py:120
  55.2 3.4 %collective-permute-start.9 = (f32[3,1024]{1,0:T(4,128)S(1)}, f32[3,1024]{1,0:T(4,128)S(1)}, u32[]{:S(2)}, u32[]{:S(2)}) collective-permute-start(f32[3,1024]{1,0:T(4,128)S(1)} %collective-permute-done.1), channel_id=1, source_target_pairs={{0,4},{4,0},{8,12},{12,8},{1,5},{5,1},{9,13},{13,9},{2,6},{6,2},{1... | collective-permute-start | bytes 36872 | tf_op jit(solution)/shard_map/ppermute | solution.py:127
  58.7 0.1 bitcast_dynamic-update-slice_fusion.3
  58.8 8.5 %collective-permute-done.6 = bf16[3,160,768]{2,1,0:T(8,128)(2,1)S(1)} collective-permute-done((bf16[3,160,768]{2,1,0:T(8,128)(2,1)}, bf16[3,160,768]{2,1,0:T(8,128)(2,1)S(1)}, u32[]{:S(2)}, u32[]{:S(2)}) %collective-permute-start.6) | collective-permute-done | bytes 737312 | tf_op jit(solution)/shard_map/ppermute | solution.py:120
  67.4 0.1 bitcast_dynamic-update-slice_fusion.2
  67.5 6.3 %collective-permute-start.10 = (f32[3,1024]{1,0:T(4,128)S(1)}, f32[3,1024]{1,0:T(4,128)S(1)}, u32[]{:S(2)}, u32[]{:S(2)}) collective-permute-start(f32[3,1024]{1,0:T(4,128)S(1)} %add.92), channel_id=1, source_target_pairs={{0,8},{4,12},{8,0},{12,4},{1,9},{5,13},{9,1},{13,5},{2,10},{6,14},... | collective-permute-start | bytes 36872 | tf_op jit(solution)/shard_map/ppermute | solution.py:127
  73.8 14.1 %collective-permute-done.7 = bf16[3,160,768]{2,1,0:T(8,128)(2,1)S(1)} collective-permute-done((bf16[3,160,768]{2,1,0:T(8,128)(2,1)}, bf16[3,160,768]{2,1,0:T(8,128)(2,1)S(1)}, u32[]{:S(2)}, u32[]{:S(2)}) %collective-permute-start.7) | collective-permute-done | bytes 737312 | tf_op jit(solution)/shard_map/ppermute | solution.py:120
  87.9 0.1 bitcast_dynamic-update-slice_fusion.1
  88.0 1.9 %collective-permute-start.11 = (f32[3,4096]{1,0:T(4,128)S(1)}, f32[3,4096]{1,0:T(4,128)S(1)}, u32[]{:S(2)}, u32[]{:S(2)}) collective-permute-start(f32[3,4096]{1,0:T(4,128)S(1)} %get-tuple-element.34), channel_id=1, source_target_pairs={{0,1},{1,0},{2,3},{3,2},{4,5},{5,4},{6,7},{7,6},{8,9},{9,8},{10,11... | collective-permute-start | bytes 147464 | tf_op jit(solution)/shard_map/ppermute | solution.py:127
  90.0 1.2 %collective-permute-done.11 = f32[3,4096]{1,0:T(4,128)S(1)} collective-permute-done((f32[3,4096]{1,0:T(4,128)S(1)}, f32[3,4096]{1,0:T(4,128)S(1)}, u32[]{:S(2)}, u32[]{:S(2)}) %collective-permute-start.11) | collective-permute-done | bytes 49184 | tf_op jit(solution)/shard_map/ppermute | solution.py:127
  91.2 2.3 %collective-permute-start.12 = (f32[3,4096]{1,0:T(4,128)S(1)}, f32[3,4096]{1,0:T(4,128)S(1)}, u32[]{:S(2)}, u32[]{:S(2)}) collective-permute-start(f32[3,4096]{1,0:T(4,128)S(1)} %add_dynamic-update-slice_fusion), channel_id=1, source_target_pairs={{0,2},{1,3},{2,0},{3,1},{4,6},{5,7},{6,4},{7,5},{8,10},{9,11},{10,... | collective-permute-start | bytes 147464 | tf_op jit(solution)/shard_map/ppermute | solution.py:127
  93.5 8.4 %collective-permute-done.8 = bf16[3,160,768]{2,1,0:T(8,128)(2,1)S(1)} collective-permute-done((bf16[3,160,768]{2,1,0:T(8,128)(2,1)}, bf16[3,160,768]{2,1,0:T(8,128)(2,1)S(1)}, u32[]{:S(2)}, u32[]{:S(2)}) %collective-permute-start.8) | collective-permute-done | bytes 737312 | tf_op jit(solution)/shard_map/ppermute | solution.py:120
  101.9 0.1 bitcast_dynamic-update-slice_fusion
  102.0 0.0 copy-start
  102.1 0.8 copy.7
  102.9 1.1 %copy-done = bf16[1,1,3,160,4096]{4,3,2,1,0:T(8,128)(2,1)} copy-done((bf16[1,1,3,160,4096]{4,3,2,1,0:T(8,128)(2,1)}, bf16[1,1,3,160,4096]{4,3,2,1,0:T(8,128)(2,1)S(1)}, u32[]{:S(2)}) %copy-start) | copy-done | bytes 3932184
  (16 shorter events, 0.2 us)
Async XLA Ops:
  6.4 18.6 %copy-start.1 = (f32[3,256]{1,0:T(4,128)S(1)}, f32[3,256]{1,0:T(4,128)}, u32[]{:S(2)}) copy-start(f32[3,256]{1,0:T(4,128)} %get-tuple-element.22) | copy-start | bytes 9220
  6.4 27.3 %collective-permute-start = (bf16[3,160,256]{2,1,0:T(8,128)(2,1)}, bf16[3,160,256]{2,1,0:T(8,128)(2,1)S(1)}, u32[]{:S(2)}, u32[]{:S(2)}) collective-permute-start(bf16[3,160,256]{2,1,0:T(8,128)(2,1)} %get-tuple-element.17), channel_id=1, source_target_pairs={{16,0},{17,1},{18,2},{19,3},{20,4},{21,5},{22,6},{23,7},{24,8},{25... | collective-permute-start | bytes 737288 | tf_op jit(solution)/shard_map/ppermute | solution.py:120
  7.7 26.0 %collective-permute-start.2 = (bf16[3,160,256]{2,1,0:T(8,128)(2,1)}, bf16[3,160,256]{2,1,0:T(8,128)(2,1)S(1)}, u32[]{:S(2)}, u32[]{:S(2)}) collective-permute-start(bf16[3,160,256]{2,1,0:T(8,128)(2,1)} %get-tuple-element.24), channel_id=1, source_target_pairs={{16,1},{17,2},{18,3},{19,0},{20,5},{21,6},{22,7},{23,4},{24,9},{25... | collective-permute-start | bytes 737288 | tf_op jit(solution)/shard_map/ppermute | solution.py:120
  9.0 24.7 %collective-permute-start.3 = (bf16[3,160,256]{2,1,0:T(8,128)(2,1)}, bf16[3,160,256]{2,1,0:T(8,128)(2,1)S(1)}, u32[]{:S(2)}, u32[]{:S(2)}) collective-permute-start(bf16[3,160,256]{2,1,0:T(8,128)(2,1)} %get-tuple-element.25), channel_id=1, source_target_pairs={{16,2},{17,3},{18,0},{19,1},{20,6},{21,7},{22,4},{23,5},{24,10},{2... | collective-permute-start | bytes 737288 | tf_op jit(solution)/shard_map/ppermute | solution.py:120
  10.3 23.4 %collective-permute-start.4 = (bf16[3,160,256]{2,1,0:T(8,128)(2,1)}, bf16[3,160,256]{2,1,0:T(8,128)(2,1)S(1)}, u32[]{:S(2)}, u32[]{:S(2)}) collective-permute-start(bf16[3,160,256]{2,1,0:T(8,128)(2,1)} %get-tuple-element.26), channel_id=1, source_target_pairs={{16,3},{17,0},{18,1},{19,2},{20,7},{21,4},{22,5},{23,6},{24,11},{2... | collective-permute-start | bytes 737288 | tf_op jit(solution)/shard_map/ppermute | solution.py:120
  25.7 8.0 %collective-permute-start.1 = (f32[3,1024]{1,0:T(4,128)S(1)}, f32[3,1024]{1,0:T(4,128)S(1)}, u32[]{:S(2)}, u32[]{:S(2)}) collective-permute-start(f32[3,1024]{1,0:T(4,128)S(1)} %pad_maximum_fusion), channel_id=1, source_target_pairs={{16,0},{17,1},{18,2},{19,3},{20,4},{21,5},{22,6},{23,7},{24,8},{25... | collective-permute-start | bytes 36872 | tf_op jit(solution)/shard_map/ppermute | solution.py:113
  33.8 21.5 %collective-permute-start.5 = (bf16[3,160,768]{2,1,0:T(8,128)(2,1)}, bf16[3,160,768]{2,1,0:T(8,128)(2,1)S(1)}, u32[]{:S(2)}, u32[]{:S(2)}) collective-permute-start(bf16[3,160,768]{2,1,0:T(8,128)(2,1)} %get-tuple-element.27), channel_id=1, source_target_pairs={{16,0},{17,1},{18,2},{19,3},{20,4},{21,5},{22,6},{23,7},{24,8},{25... | collective-permute-start | bytes 2211848 | tf_op jit(solution)/shard_map/ppermute | solution.py:120
  35.1 32.3 %collective-permute-start.6 = (bf16[3,160,768]{2,1,0:T(8,128)(2,1)}, bf16[3,160,768]{2,1,0:T(8,128)(2,1)S(1)}, u32[]{:S(2)}, u32[]{:S(2)}) collective-permute-start(bf16[3,160,768]{2,1,0:T(8,128)(2,1)} %get-tuple-element.28), channel_id=1, source_target_pairs={{16,1},{17,2},{18,3},{19,0},{20,5},{21,6},{22,7},{23,4},{24,9},{25... | collective-permute-start | bytes 2211848 | tf_op jit(solution)/shard_map/ppermute | solution.py:120
  36.4 51.4 %collective-permute-start.7 = (bf16[3,160,768]{2,1,0:T(8,128)(2,1)}, bf16[3,160,768]{2,1,0:T(8,128)(2,1)S(1)}, u32[]{:S(2)}, u32[]{:S(2)}) collective-permute-start(bf16[3,160,768]{2,1,0:T(8,128)(2,1)} %get-tuple-element.29), channel_id=1, source_target_pairs={{16,2},{17,3},{18,0},{19,1},{20,6},{21,7},{22,4},{23,5},{24,10},{2... | collective-permute-start | bytes 2211848 | tf_op jit(solution)/shard_map/ppermute | solution.py:120
  37.7 64.2 %collective-permute-start.8 = (bf16[3,160,768]{2,1,0:T(8,128)(2,1)}, bf16[3,160,768]{2,1,0:T(8,128)(2,1)S(1)}, u32[]{:S(2)}, u32[]{:S(2)}) collective-permute-start(bf16[3,160,768]{2,1,0:T(8,128)(2,1)} %get-tuple-element.30), channel_id=1, source_target_pairs={{16,3},{17,0},{18,1},{19,2},{20,7},{21,4},{22,5},{23,6},{24,11},{2... | collective-permute-start | bytes 2211848 | tf_op jit(solution)/shard_map/ppermute | solution.py:120
  55.2 12.3 %collective-permute-start.9 = (f32[3,1024]{1,0:T(4,128)S(1)}, f32[3,1024]{1,0:T(4,128)S(1)}, u32[]{:S(2)}, u32[]{:S(2)}) collective-permute-start(f32[3,1024]{1,0:T(4,128)S(1)} %collective-permute-done.1), channel_id=1, source_target_pairs={{0,4},{4,0},{8,12},{12,8},{1,5},{5,1},{9,13},{13,9},{2,6},{6,2},{1... | collective-permute-start | bytes 36872 | tf_op jit(solution)/shard_map/ppermute | solution.py:127
  67.5 20.5 %collective-permute-start.10 = (f32[3,1024]{1,0:T(4,128)S(1)}, f32[3,1024]{1,0:T(4,128)S(1)}, u32[]{:S(2)}, u32[]{:S(2)}) collective-permute-start(f32[3,1024]{1,0:T(4,128)S(1)} %add.92), channel_id=1, source_target_pairs={{0,8},{4,12},{8,0},{12,4},{1,9},{5,13},{9,1},{13,5},{2,10},{6,14},... | collective-permute-start | bytes 36872 | tf_op jit(solution)/shard_map/ppermute | solution.py:127
  88.0 3.1 %collective-permute-start.11 = (f32[3,4096]{1,0:T(4,128)S(1)}, f32[3,4096]{1,0:T(4,128)S(1)}, u32[]{:S(2)}, u32[]{:S(2)}) collective-permute-start(f32[3,4096]{1,0:T(4,128)S(1)} %get-tuple-element.34), channel_id=1, source_target_pairs={{0,1},{1,0},{2,3},{3,2},{4,5},{5,4},{6,7},{7,6},{8,9},{9,8},{10,11... | collective-permute-start | bytes 147464 | tf_op jit(solution)/shard_map/ppermute | solution.py:127
  91.2 10.8 %collective-permute-start.12 = (f32[3,4096]{1,0:T(4,128)S(1)}, f32[3,4096]{1,0:T(4,128)S(1)}, u32[]{:S(2)}, u32[]{:S(2)}) collective-permute-start(f32[3,4096]{1,0:T(4,128)S(1)} %add_dynamic-update-slice_fusion), channel_id=1, source_target_pairs={{0,2},{1,3},{2,0},{3,1},{4,6},{5,7},{6,4},{7,5},{8,10},{9,11},{10,... | collective-permute-start | bytes 147464 | tf_op jit(solution)/shard_map/ppermute | solution.py:127
  102.0 1.9 %copy-start = (bf16[1,1,3,160,4096]{4,3,2,1,0:T(8,128)(2,1)}, bf16[1,1,3,160,4096]{4,3,2,1,0:T(8,128)(2,1)S(1)}, u32[]{:S(2)}) copy-start(bf16[1,1,3,160,4096]{4,3,2,1,0:T(8,128)(2,1)S(1)} %bitcast_dynamic-update-slice_fusion) | copy-start | bytes 11796484

commit v9 on v8

--- a/solution.py
+++ b/solution.py
@@ -20,19 +20,22 @@
     rows = length // parts
     scaling = 1.0 / math.sqrt(HEAD_DIM)
     for b, lo in enumerate((0, length - window)):
+        klo = b * half
         q = q_ref[lo : lo + window, :]
-        k = k_ref[lo : lo + window, :]
-        v = v_ref[lo : lo + window, :]
         g = g_ref[lo : lo + window, :]
+        k = k_ref[klo : klo + half, :]
+        v = v_ref[klo : klo + half, :]
         scores = lax.dot_general(k, q, NT, preferred_element_type=jnp.float32) * scaling
-        kj = lo + lax.broadcasted_iota(jnp.int32, (window, window), 0)
-        qi = lo + lax.broadcasted_iota(jnp.int32, (window, window), 1)
+        kj = klo + lax.broadcasted_iota(jnp.int32, (half, window), 0)
+        qi = lo + lax.broadcasted_iota(jnp.int32, (half, window), 1)
         start = lo + lax.broadcasted_iota(jnp.int32, (1, window), 1) - pos_ref[:, lo : lo + window]
         allowed = (kj <= qi) & (kj >= start)
         scores = jnp.where(allowed, scores, jnp.float32(-1e30))
         highest = jnp.max(scores, axis=0, keepdims=True)
         expont = jnp.exp(scores - highest)
         attn = expont / jnp.sum(expont, axis=0, keepdims=True)
+        query = lo + lax.broadcasted_iota(jnp.int32, (1, window), 1)
+        attn = jnp.where((query >= klo) & (query < klo + half), attn, jnp.float32(0.0))
         grad_v = jnp.dot(attn.astype(jnp.bfloat16), g, preferred_element_type=jnp.float32)
         grad_attn = lax.dot_general(v, g, NT, preferred_element_type=jnp.float32)
         delta = jnp.sum(attn * grad_attn, axis=0, keepdims=True)
@@ -40,8 +43,9 @@
         grad_k = jnp.dot(grad_scores.astype(jnp.bfloat16), q, preferred_element_type=jnp.float32)
         grad_q = jnp.dot(grad_scores.T.astype(jnp.bfloat16), k, preferred_element_type=jnp.float32)
         keep = b * half - lo
-        for i, grad in enumerate((grad_q, grad_k, grad_v)):
-            full_ref[i, b * half : (b + 1) * half, :] = grad[keep : keep + half].astype(jnp.bfloat16)
+        full_ref[0, b * half : (b + 1) * half, :] = grad_q[keep : keep + half].astype(jnp.bfloat16)
+        full_ref[1, b * half : (b + 1) * half, :] = grad_k.astype(jnp.bfloat16)
+        full_ref[2, b * half : (b + 1) * half, :] = grad_v.astype(jnp.bfloat16)
     sum_ref[...] = jnp.sum(full_ref[...].astype(jnp.float32), axis=1)
     part = part_ref[0]
     for shift, out_ref in enumerate(out_refs):

time: 104 us -> 104 us (level)
  Pallas kernels: 19.1 us -> 17.8 us
    pallas_call x2, Pallas kernels: 19.1 us -> 17.8 us  [chunk_grads(): pl.pallas_call(functools.partial(grads_kernel, parts=parts), grid_spec=gr...]
  transfers between devices with their start and end apart: 13 -> 13, of which waited for: 6 -> 6; matrix products, arithmetic and copies ran while one was open for 2% -> 2% of each run, Pallas kernels for 13% -> 12%
where the time goes in v9:
time: 104 us
  waiting for transfers between devices  55 us (53%)
  starting transfers between devices  26.2 us (25%)
  Pallas kernels  17.8 us (17%)
  local copies, waits for them, and re-layouts  2.83 us (3%)
    ppermute x8, waiting for transfers between devices, per_device(): lax.ppermute(grads[shift], ('section', 'mp'), pairs(shift))  46.8 us
    pallas_call x2, Pallas kernels, chunk_grads(): pl.pallas_call(functools.partial(grads_kernel, parts=parts), grid_spec=gr...  17.8 us
    ppermute x4, starting transfers between devices, receivers_sum(): value = value + lax.ppermute(value, ('section', axis), ring)  14.6 us
    ppermute x8, starting transfers between devices, per_device(): lax.ppermute(grads[shift], ('section', 'mp'), pairs(shift))  10.3 us
    ppermute x1, waiting for transfers between devices, per_device(): lax.ppermute(own, 'section', [(s + 1, s) for s in range(sections - 1)])  7 us
  transfers between devices with their start and end apart: 13, of which 6 were waited for; matrix products, arithmetic and copies ran while one was open for 2% of the time, Pallas kernels for 12%

profile of v9, /device:TPU:0, one launch (start us, length us, event | category | flops | bytes accessed | tf_op | source)
XLA Modules:
  0.0 103.6 jit_solution(11719769934308176462)
XLA Ops:
  0.6 5.4 %shard_map.68 = (bf16[3,160,256]{2,1,0:T(8,128)(2,1)}, bf16[3,160,256]{2,1,0:T(8,128)(2,1)}, bf16[3,160,256]{2,1,0:T(8,128)(2,1)}, bf16[3,160,256]{2,1,0:T(8,128)(2,1)}, f32[3,256]{1,0:T(4,128)}) custom-call(s32[1]{0:T(128)} %bitcast.part_ref, s32[1,640]{1,0:T(1,128)} %bitcast.32, bf16[640,1024]{1,0:T(8,128)(2,1)} %bitcast.24, bf16[640,1024]{1,0:T(8,128)(2,1)} %bitcast.26, ...), custom_call_target="tpu_custom_call" | custom-call | tf_op jit(solution)/shard_map/pallas_call | solution.py:73
  6.1 1.3 %collective-permute-start = (bf16[3,160,256]{2,1,0:T(8,128)(2,1)}, bf16[3,160,256]{2,1,0:T(8,128)(2,1)S(1)}, u32[]{:S(2)}, u32[]{:S(2)}) collective-permute-start(bf16[3,160,256]{2,1,0:T(8,128)(2,1)} %get-tuple-element.17), channel_id=1, source_target_pairs={{16,0},{17,1},{18,2},{19,3},{20,4},{21,5},{22,6},{23,7},{24,8},{25... | collective-permute-start | bytes 737288 | tf_op jit(solution)/shard_map/ppermute | solution.py:124
  7.4 1.3 %collective-permute-start.2 = (bf16[3,160,256]{2,1,0:T(8,128)(2,1)}, bf16[3,160,256]{2,1,0:T(8,128)(2,1)S(1)}, u32[]{:S(2)}, u32[]{:S(2)}) collective-permute-start(bf16[3,160,256]{2,1,0:T(8,128)(2,1)} %get-tuple-element.24), channel_id=1, source_target_pairs={{16,1},{17,2},{18,3},{19,0},{20,5},{21,6},{22,7},{23,4},{24,9},{25... | collective-permute-start | bytes 737288 | tf_op jit(solution)/shard_map/ppermute | solution.py:124
  8.7 1.3 %collective-permute-start.3 = (bf16[3,160,256]{2,1,0:T(8,128)(2,1)}, bf16[3,160,256]{2,1,0:T(8,128)(2,1)S(1)}, u32[]{:S(2)}, u32[]{:S(2)}) collective-permute-start(bf16[3,160,256]{2,1,0:T(8,128)(2,1)} %get-tuple-element.25), channel_id=1, source_target_pairs={{16,2},{17,3},{18,0},{19,1},{20,6},{21,7},{22,4},{23,5},{24,10},{2... | collective-permute-start | bytes 737288 | tf_op jit(solution)/shard_map/ppermute | solution.py:124
  10.0 1.3 %collective-permute-start.4 = (bf16[3,160,256]{2,1,0:T(8,128)(2,1)}, bf16[3,160,256]{2,1,0:T(8,128)(2,1)S(1)}, u32[]{:S(2)}, u32[]{:S(2)}) collective-permute-start(bf16[3,160,256]{2,1,0:T(8,128)(2,1)} %get-tuple-element.26), channel_id=1, source_target_pairs={{16,3},{17,0},{18,1},{19,2},{20,7},{21,4},{22,5},{23,6},{24,11},{2... | collective-permute-start | bytes 737288 | tf_op jit(solution)/shard_map/ppermute | solution.py:124
  11.3 12.3 %shard_map.69 = (bf16[3,160,768]{2,1,0:T(8,128)(2,1)}, bf16[3,160,768]{2,1,0:T(8,128)(2,1)}, bf16[3,160,768]{2,1,0:T(8,128)(2,1)}, bf16[3,160,768]{2,1,0:T(8,128)(2,1)}, f32[3,768]{1,0:T(4,128)}) custom-call(s32[1]{0:T(128)} %bitcast.part_ref, s32[1,640]{1,0:T(1,128)} %bitcast.33, bf16[640,1024]{1,0:T(8,128)(2,1)} %bitcast.25, bf16[640,1024]{1,0:T(8,128)(2,1)} %bitcast.27, ...), custom_call_target="tpu_custom_call" | custom-call | tf_op jit(solution)/shard_map/pallas_call | solution.py:73
  23.6 0.7 pad_maximum_fusion
  24.3 1.3 %collective-permute-start.1 = (f32[3,1024]{1,0:T(4,128)S(1)}, f32[3,1024]{1,0:T(4,128)S(1)}, u32[]{:S(2)}, u32[]{:S(2)}) collective-permute-start(f32[3,1024]{1,0:T(4,128)S(1)} %pad_maximum_fusion), channel_id=1, source_target_pairs={{16,0},{17,1},{18,2},{19,3},{20,4},{21,5},{22,6},{23,7},{24,8},{25... | collective-permute-start | bytes 36872 | tf_op jit(solution)/shard_map/ppermute | solution.py:117
  25.6 7.0 %collective-permute-done.1 = f32[3,1024]{1,0:T(4,128)S(1)} collective-permute-done((f32[3,1024]{1,0:T(4,128)S(1)}, f32[3,1024]{1,0:T(4,128)S(1)}, u32[]{:S(2)}, u32[]{:S(2)}) %collective-permute-start.1) | collective-permute-done | bytes 12320 | tf_op jit(solution)/shard_map/ppermute | solution.py:117
  32.6 0.0 collective-permute-done
  32.6 0.0 collective-permute-done.2
  32.6 1.3 %collective-permute-start.5 = (bf16[3,160,768]{2,1,0:T(8,128)(2,1)}, bf16[3,160,768]{2,1,0:T(8,128)(2,1)S(1)}, u32[]{:S(2)}, u32[]{:S(2)}) collective-permute-start(bf16[3,160,768]{2,1,0:T(8,128)(2,1)} %get-tuple-element.27), channel_id=1, source_target_pairs={{16,0},{17,1},{18,2},{19,3},{20,4},{21,5},{22,6},{23,7},{24,8},{25... | collective-permute-start | bytes 2211848 | tf_op jit(solution)/shard_map/ppermute | solution.py:124
  34.0 1.3 %collective-permute-start.6 = (bf16[3,160,768]{2,1,0:T(8,128)(2,1)}, bf16[3,160,768]{2,1,0:T(8,128)(2,1)S(1)}, u32[]{:S(2)}, u32[]{:S(2)}) collective-permute-start(bf16[3,160,768]{2,1,0:T(8,128)(2,1)} %get-tuple-element.28), channel_id=1, source_target_pairs={{16,1},{17,2},{18,3},{19,0},{20,5},{21,6},{22,7},{23,4},{24,9},{25... | collective-permute-start | bytes 2211848 | tf_op jit(solution)/shard_map/ppermute | solution.py:124
  35.3 1.3 %collective-permute-start.7 = (bf16[3,160,768]{2,1,0:T(8,128)(2,1)}, bf16[3,160,768]{2,1,0:T(8,128)(2,1)S(1)}, u32[]{:S(2)}, u32[]{:S(2)}) collective-permute-start(bf16[3,160,768]{2,1,0:T(8,128)(2,1)} %get-tuple-element.29), channel_id=1, source_target_pairs={{16,2},{17,3},{18,0},{19,1},{20,6},{21,7},{22,4},{23,5},{24,10},{2... | collective-permute-start | bytes 2211848 | tf_op jit(solution)/shard_map/ppermute | solution.py:124
  36.6 1.3 %collective-permute-start.8 = (bf16[3,160,768]{2,1,0:T(8,128)(2,1)}, bf16[3,160,768]{2,1,0:T(8,128)(2,1)S(1)}, u32[]{:S(2)}, u32[]{:S(2)}) collective-permute-start(bf16[3,160,768]{2,1,0:T(8,128)(2,1)} %get-tuple-element.30), channel_id=1, source_target_pairs={{16,3},{17,0},{18,1},{19,2},{20,7},{21,4},{22,5},{23,6},{24,11},{2... | collective-permute-start | bytes 2211848 | tf_op jit(solution)/shard_map/ppermute | solution.py:124
  37.9 0.5 broadcast_in_dim.26
  38.5 15.3 %collective-permute-done.5 = bf16[3,160,768]{2,1,0:T(8,128)(2,1)S(1)} collective-permute-done((bf16[3,160,768]{2,1,0:T(8,128)(2,1)}, bf16[3,160,768]{2,1,0:T(8,128)(2,1)S(1)}, u32[]{:S(2)}, u32[]{:S(2)}) %collective-permute-start.5) | collective-permute-done | bytes 737312 | tf_op jit(solution)/shard_map/ppermute | solution.py:124
  53.8 4.6 %collective-permute-start.9 = (f32[3,1024]{1,0:T(4,128)S(1)}, f32[3,1024]{1,0:T(4,128)S(1)}, u32[]{:S(2)}, u32[]{:S(2)}) collective-permute-start(f32[3,1024]{1,0:T(4,128)S(1)} %collective-permute-done.1), channel_id=1, source_target_pairs={{0,4},{4,0},{8,12},{12,8},{1,5},{5,1},{9,13},{13,9},{2,6},{6,2},{1... | collective-permute-start | bytes 36872 | tf_op jit(solution)/shard_map/ppermute | solution.py:131
  58.3 0.1 bitcast_dynamic-update-slice_fusion.3
  58.5 8.7 %collective-permute-done.6 = bf16[3,160,768]{2,1,0:T(8,128)(2,1)S(1)} collective-permute-done((bf16[3,160,768]{2,1,0:T(8,128)(2,1)}, bf16[3,160,768]{2,1,0:T(8,128)(2,1)S(1)}, u32[]{:S(2)}, u32[]{:S(2)}) %collective-permute-start.6) | collective-permute-done | bytes 737312 | tf_op jit(solution)/shard_map/ppermute | solution.py:124
  67.1 0.1 bitcast_dynamic-update-slice_fusion.2
  67.3 6.2 %collective-permute-start.10 = (f32[3,1024]{1,0:T(4,128)S(1)}, f32[3,1024]{1,0:T(4,128)S(1)}, u32[]{:S(2)}, u32[]{:S(2)}) collective-permute-start(f32[3,1024]{1,0:T(4,128)S(1)} %add.92), channel_id=1, source_target_pairs={{0,8},{4,12},{8,0},{12,4},{1,9},{5,13},{9,1},{13,5},{2,10},{6,14},... | collective-permute-start | bytes 36872 | tf_op jit(solution)/shard_map/ppermute | solution.py:131
  73.5 14.1 %collective-permute-done.7 = bf16[3,160,768]{2,1,0:T(8,128)(2,1)S(1)} collective-permute-done((bf16[3,160,768]{2,1,0:T(8,128)(2,1)}, bf16[3,160,768]{2,1,0:T(8,128)(2,1)S(1)}, u32[]{:S(2)}, u32[]{:S(2)}) %collective-permute-start.7) | collective-permute-done | bytes 737312 | tf_op jit(solution)/shard_map/ppermute | solution.py:124
  87.6 0.1 bitcast_dynamic-update-slice_fusion.1
  87.7 1.9 %collective-permute-start.11 = (f32[3,4096]{1,0:T(4,128)S(1)}, f32[3,4096]{1,0:T(4,128)S(1)}, u32[]{:S(2)}, u32[]{:S(2)}) collective-permute-start(f32[3,4096]{1,0:T(4,128)S(1)} %get-tuple-element.34), channel_id=1, source_target_pairs={{0,1},{1,0},{2,3},{3,2},{4,5},{5,4},{6,7},{7,6},{8,9},{9,8},{10,11... | collective-permute-start | bytes 147464 | tf_op jit(solution)/shard_map/ppermute | solution.py:131
  89.7 1.2 %collective-permute-done.11 = f32[3,4096]{1,0:T(4,128)S(1)} collective-permute-done((f32[3,4096]{1,0:T(4,128)S(1)}, f32[3,4096]{1,0:T(4,128)S(1)}, u32[]{:S(2)}, u32[]{:S(2)}) %collective-permute-start.11) | collective-permute-done | bytes 49184 | tf_op jit(solution)/shard_map/ppermute | solution.py:131
  90.9 1.9 %collective-permute-start.12 = (f32[3,4096]{1,0:T(4,128)S(1)}, f32[3,4096]{1,0:T(4,128)S(1)}, u32[]{:S(2)}, u32[]{:S(2)}) collective-permute-start(f32[3,4096]{1,0:T(4,128)S(1)} %add_dynamic-update-slice_fusion), channel_id=1, source_target_pairs={{0,2},{1,3},{2,0},{3,1},{4,6},{5,7},{6,4},{7,5},{8,10},{9,11},{10,... | collective-permute-start | bytes 147464 | tf_op jit(solution)/shard_map/ppermute | solution.py:131
  92.8 8.7 %collective-permute-done.8 = bf16[3,160,768]{2,1,0:T(8,128)(2,1)S(1)} collective-permute-done((bf16[3,160,768]{2,1,0:T(8,128)(2,1)}, bf16[3,160,768]{2,1,0:T(8,128)(2,1)S(1)}, u32[]{:S(2)}, u32[]{:S(2)}) %collective-permute-start.8) | collective-permute-done | bytes 737312 | tf_op jit(solution)/shard_map/ppermute | solution.py:124
  101.5 0.1 bitcast_dynamic-update-slice_fusion
  101.6 0.0 copy-start
  101.7 0.8 copy.7
  102.5 1.1 %copy-done = bf16[1,1,3,160,4096]{4,3,2,1,0:T(8,128)(2,1)} copy-done((bf16[1,1,3,160,4096]{4,3,2,1,0:T(8,128)(2,1)}, bf16[1,1,3,160,4096]{4,3,2,1,0:T(8,128)(2,1)S(1)}, u32[]{:S(2)}) %copy-start) | copy-done | bytes 3932184
  (16 shorter events, 0.2 us)
Async XLA Ops:
  6.0 17.6 %copy-start.1 = (f32[3,256]{1,0:T(4,128)S(1)}, f32[3,256]{1,0:T(4,128)}, u32[]{:S(2)}) copy-start(f32[3,256]{1,0:T(4,128)} %get-tuple-element.22) | copy-start | bytes 9220
  6.1 26.6 %collective-permute-start = (bf16[3,160,256]{2,1,0:T(8,128)(2,1)}, bf16[3,160,256]{2,1,0:T(8,128)(2,1)S(1)}, u32[]{:S(2)}, u32[]{:S(2)}) collective-permute-start(bf16[3,160,256]{2,1,0:T(8,128)(2,1)} %get-tuple-element.17), channel_id=1, source_target_pairs={{16,0},{17,1},{18,2},{19,3},{20,4},{21,5},{22,6},{23,7},{24,8},{25... | collective-permute-start | bytes 737288 | tf_op jit(solution)/shard_map/ppermute | solution.py:124
  7.4 25.3 %collective-permute-start.2 = (bf16[3,160,256]{2,1,0:T(8,128)(2,1)}, bf16[3,160,256]{2,1,0:T(8,128)(2,1)S(1)}, u32[]{:S(2)}, u32[]{:S(2)}) collective-permute-start(bf16[3,160,256]{2,1,0:T(8,128)(2,1)} %get-tuple-element.24), channel_id=1, source_target_pairs={{16,1},{17,2},{18,3},{19,0},{20,5},{21,6},{22,7},{23,4},{24,9},{25... | collective-permute-start | bytes 737288 | tf_op jit(solution)/shard_map/ppermute | solution.py:124
  8.7 24.0 %collective-permute-start.3 = (bf16[3,160,256]{2,1,0:T(8,128)(2,1)}, bf16[3,160,256]{2,1,0:T(8,128)(2,1)S(1)}, u32[]{:S(2)}, u32[]{:S(2)}) collective-permute-start(bf16[3,160,256]{2,1,0:T(8,128)(2,1)} %get-tuple-element.25), channel_id=1, source_target_pairs={{16,2},{17,3},{18,0},{19,1},{20,6},{21,7},{22,4},{23,5},{24,10},{2... | collective-permute-start | bytes 737288 | tf_op jit(solution)/shard_map/ppermute | solution.py:124
  10.0 22.7 %collective-permute-start.4 = (bf16[3,160,256]{2,1,0:T(8,128)(2,1)}, bf16[3,160,256]{2,1,0:T(8,128)(2,1)S(1)}, u32[]{:S(2)}, u32[]{:S(2)}) collective-permute-start(bf16[3,160,256]{2,1,0:T(8,128)(2,1)} %get-tuple-element.26), channel_id=1, source_target_pairs={{16,3},{17,0},{18,1},{19,2},{20,7},{21,4},{22,5},{23,6},{24,11},{2... | collective-permute-start | bytes 737288 | tf_op jit(solution)/shard_map/ppermute | solution.py:124
  24.3 8.3 %collective-permute-start.1 = (f32[3,1024]{1,0:T(4,128)S(1)}, f32[3,1024]{1,0:T(4,128)S(1)}, u32[]{:S(2)}, u32[]{:S(2)}) collective-permute-start(f32[3,1024]{1,0:T(4,128)S(1)} %pad_maximum_fusion), channel_id=1, source_target_pairs={{16,0},{17,1},{18,2},{19,3},{20,4},{21,5},{22,6},{23,7},{24,8},{25... | collective-permute-start | bytes 36872 | tf_op jit(solution)/shard_map/ppermute | solution.py:117
  32.6 21.1 %collective-permute-start.5 = (bf16[3,160,768]{2,1,0:T(8,128)(2,1)}, bf16[3,160,768]{2,1,0:T(8,128)(2,1)S(1)}, u32[]{:S(2)}, u32[]{:S(2)}) collective-permute-start(bf16[3,160,768]{2,1,0:T(8,128)(2,1)} %get-tuple-element.27), channel_id=1, source_target_pairs={{16,0},{17,1},{18,2},{19,3},{20,4},{21,5},{22,6},{23,7},{24,8},{25... | collective-permute-start | bytes 2211848 | tf_op jit(solution)/shard_map/ppermute | solution.py:124
  34.0 33.2 %collective-permute-start.6 = (bf16[3,160,768]{2,1,0:T(8,128)(2,1)}, bf16[3,160,768]{2,1,0:T(8,128)(2,1)S(1)}, u32[]{:S(2)}, u32[]{:S(2)}) collective-permute-start(bf16[3,160,768]{2,1,0:T(8,128)(2,1)} %get-tuple-element.28), channel_id=1, source_target_pairs={{16,1},{17,2},{18,3},{19,0},{20,5},{21,6},{22,7},{23,4},{24,9},{25... | collective-permute-start | bytes 2211848 | tf_op jit(solution)/shard_map/ppermute | solution.py:124
  35.3 52.2 %collective-permute-start.7 = (bf16[3,160,768]{2,1,0:T(8,128)(2,1)}, bf16[3,160,768]{2,1,0:T(8,128)(2,1)S(1)}, u32[]{:S(2)}, u32[]{:S(2)}) collective-permute-start(bf16[3,160,768]{2,1,0:T(8,128)(2,1)} %get-tuple-element.29), channel_id=1, source_target_pairs={{16,2},{17,3},{18,0},{19,1},{20,6},{21,7},{22,4},{23,5},{24,10},{2... | collective-permute-start | bytes 2211848 | tf_op jit(solution)/shard_map/ppermute | solution.py:124
  36.6 64.9 %collective-permute-start.8 = (bf16[3,160,768]{2,1,0:T(8,128)(2,1)}, bf16[3,160,768]{2,1,0:T(8,128)(2,1)S(1)}, u32[]{:S(2)}, u32[]{:S(2)}) collective-permute-start(bf16[3,160,768]{2,1,0:T(8,128)(2,1)} %get-tuple-element.30), channel_id=1, source_target_pairs={{16,3},{17,0},{18,1},{19,2},{20,7},{21,4},{22,5},{23,6},{24,11},{2... | collective-permute-start | bytes 2211848 | tf_op jit(solution)/shard_map/ppermute | solution.py:124
  53.8 13.5 %collective-permute-start.9 = (f32[3,1024]{1,0:T(4,128)S(1)}, f32[3,1024]{1,0:T(4,128)S(1)}, u32[]{:S(2)}, u32[]{:S(2)}) collective-permute-start(f32[3,1024]{1,0:T(4,128)S(1)} %collective-permute-done.1), channel_id=1, source_target_pairs={{0,4},{4,0},{8,12},{12,8},{1,5},{5,1},{9,13},{13,9},{2,6},{6,2},{1... | collective-permute-start | bytes 36872 | tf_op jit(solution)/shard_map/ppermute | solution.py:131
  67.3 20.4 %collective-permute-start.10 = (f32[3,1024]{1,0:T(4,128)S(1)}, f32[3,1024]{1,0:T(4,128)S(1)}, u32[]{:S(2)}, u32[]{:S(2)}) collective-permute-start(f32[3,1024]{1,0:T(4,128)S(1)} %add.92), channel_id=1, source_target_pairs={{0,8},{4,12},{8,0},{12,4},{1,9},{5,13},{9,1},{13,5},{2,10},{6,14},... | collective-permute-start | bytes 36872 | tf_op jit(solution)/shard_map/ppermute | solution.py:131
  87.7 3.1 %collective-permute-start.11 = (f32[3,4096]{1,0:T(4,128)S(1)}, f32[3,4096]{1,0:T(4,128)S(1)}, u32[]{:S(2)}, u32[]{:S(2)}) collective-permute-start(f32[3,4096]{1,0:T(4,128)S(1)} %get-tuple-element.34), channel_id=1, source_target_pairs={{0,1},{1,0},{2,3},{3,2},{4,5},{5,4},{6,7},{7,6},{8,9},{9,8},{10,11... | collective-permute-start | bytes 147464 | tf_op jit(solution)/shard_map/ppermute | solution.py:131
  90.9 10.7 %collective-permute-start.12 = (f32[3,4096]{1,0:T(4,128)S(1)}, f32[3,4096]{1,0:T(4,128)S(1)}, u32[]{:S(2)}, u32[]{:S(2)}) collective-permute-start(f32[3,4096]{1,0:T(4,128)S(1)} %add_dynamic-update-slice_fusion), channel_id=1, source_target_pairs={{0,2},{1,3},{2,0},{3,1},{4,6},{5,7},{6,4},{7,5},{8,10},{9,11},{10,... | collective-permute-start | bytes 147464 | tf_op jit(solution)/shard_map/ppermute | solution.py:131
  101.6 1.9 %copy-start = (bf16[1,1,3,160,4096]{4,3,2,1,0:T(8,128)(2,1)}, bf16[1,1,3,160,4096]{4,3,2,1,0:T(8,128)(2,1)S(1)}, u32[]{:S(2)}) copy-start(bf16[1,1,3,160,4096]{4,3,2,1,0:T(8,128)(2,1)S(1)} %bitcast_dynamic-update-slice_fusion) | copy-start | bytes 11796484

commit v10 on v9

--- a/solution.py
+++ b/solution.py
@@ -107,8 +107,15 @@
     arrived = [[None] * chunk_count for _ in range(parts)]
     sums = []
     for c in range(chunk_count):
-        *grads, chunk_sums = chunk_grads(
-            part_arg, token_positions, query_rows, key_rows, value_rows, grad_rows, firsts[c], sizes[c], parts
+        def run(*args, first=firsts[c], heads=sizes[c]):
+            return tuple(chunk_grads(part_arg, *args, first, heads, parts))
+
+        def skip(*args, heads=sizes[c]):
+            width = heads * HEAD_DIM
+            return tuple([jnp.zeros((3, rows, width), jnp.bfloat16)] * parts + [jnp.zeros((3, width), jnp.float32)])
+
+        *grads, chunk_sums = lax.cond(
+            lax.axis_index("section") > 0, run, skip, token_positions, query_rows, key_rows, value_rows, grad_rows
         )
         sums.append(chunk_sums)
         tie = []

time: 104 us -> 103 us (level)
  Pallas kernels: 17.8 us -> 0 us
  waiting for transfers between devices: 55 us -> 67.6 us
  local copies, waits for them, and re-layouts: 2.83 us -> 9.98 us
  starting transfers between devices: 26.2 us -> 23.8 us
    pallas_call x2 -> x0, Pallas kernels: 17.8 us -> none  [chunk_grads(): pl.pallas_call(functools.partial(grads_kernel, parts=parts), grid_spec=gr...]
    ppermute x1, waiting for transfers between devices: 7 us -> 22.3 us  [per_device(): lax.ppermute(own, 'section', [(s + 1, s) for s in range(sections - 1)])]
    dynamic_update_slice x8, local copies, waits for them, and re-layouts: 0.46 us -> 4.57 us  [per_device(): lax.dynamic_update_slice_in_dim(received, arrived[shift][c], source * col...]
    another operation x0 -> x10, local copies, waits for them, and re-layouts: none -> 3.05 us
    ppermute x8, waiting for transfers between devices: 46.8 us -> 44.2 us  [per_device(): lax.ppermute(grads[shift], ('section', 'mp'), pairs(shift))]
    ppermute x4, starting transfers between devices: 14.6 us -> 12.2 us  [receivers_sum(): value = value + lax.ppermute(value, ('section', axis), ring)]
  transfers between devices with their start and end apart: 13 -> 13, of which waited for: 6 -> 6; matrix products, arithmetic and copies ran while one was open for 2% -> 5% of each run, Pallas kernels for 12% -> 0%
where the time goes in v10:
time: 103 us
  waiting for transfers between devices  67.6 us (66%)
  starting transfers between devices  23.8 us (23%)
  local copies, waits for them, and re-layouts  9.98 us (10%)
    ppermute x8, waiting for transfers between devices, per_device(): lax.ppermute(grads[shift], ('section', 'mp'), pairs(shift))  44.2 us
    ppermute x1, waiting for transfers between devices, per_device(): lax.ppermute(own, 'section', [(s + 1, s) for s in range(sections - 1)])  22.3 us
    ppermute x4, starting transfers between devices, receivers_sum(): value = value + lax.ppermute(value, ('section', axis), ring)  12.2 us
    ppermute x8, starting transfers between devices, per_device(): lax.ppermute(grads[shift], ('section', 'mp'), pairs(shift))  10.3 us
    dynamic_update_slice x8, local copies, waits for them, and re-layouts, per_device(): lax.dynamic_update_slice_in_dim(received, arrived[shift][c], source * col...  4.57 us
    another operation x10, local copies, waits for them, and re-layouts  3.05 us
  transfers between devices with their start and end apart: 13, of which 6 were waited for; matrix products, arithmetic and copies ran while one was open for 5% of the time, Pallas kernels for 0%

profile of v10, /device:TPU:0, one launch (start us, length us, event | category | flops | bytes accessed | tf_op | source)
XLA Modules:
  0.0 102.5 jit_solution(16518115702078085989)
XLA Ops:
  0.6 2.9 %conditional.2 = ((bf16[3,160,256]{2,1,0:T(8,128)(2,1)}, bf16[3,160,256]{2,1,0:T(8,128)(2,1)}, bf16[3,160,256]{2,1,0:T(8,128)(2,1)}, bf16[3,160,256]{2,1,0:T(8,128)(2,1)}, f32[3,256]{1,0:T(4,128)S(1)})) conditional(s32[]{:T(128)} %convert_element_type.4, () %tuple.24, (s32[1]{0:T(128)}, s32[1,640]{1,0:T(1,128)}, bf16[640,1024]{1,0:T(8,128)(2,1)}, ...), branch_computations={%region_0.0_spmd, %region_1.0_spmd} | conditional | bytes 986172 | solution.py:117
  0.6 0.7 broadcast.15
  1.4 0.7 broadcast.15.clone
  2.1 0.7 broadcast.15.clone.1
  2.8 0.7 broadcast.15.clone.2
  3.5 1.3 %collective-permute-start = (bf16[3,160,256]{2,1,0:T(8,128)(2,1)}, bf16[3,160,256]{2,1,0:T(8,128)(2,1)}, u32[]{:S(2)}, u32[]{:S(2)}) collective-permute-start(bf16[3,160,256]{2,1,0:T(8,128)(2,1)} %get-tuple-element.53), channel_id=1, source_target_pairs={{16,0},{17,1},{18,2},{19,3},{20,4},{21,5},{22,6},{23,7},{24,8},{25... | collective-permute-start | bytes 737288 | tf_op jit(solution)/shard_map/ppermute | solution.py:131
  4.8 1.3 %collective-permute-start.2 = (bf16[3,160,256]{2,1,0:T(8,128)(2,1)}, bf16[3,160,256]{2,1,0:T(8,128)(2,1)}, u32[]{:S(2)}, u32[]{:S(2)}) collective-permute-start(bf16[3,160,256]{2,1,0:T(8,128)(2,1)} %get-tuple-element.60), channel_id=1, source_target_pairs={{16,1},{17,2},{18,3},{19,0},{20,5},{21,6},{22,7},{23,4},{24,9},{25... | collective-permute-start | bytes 737288 | tf_op jit(solution)/shard_map/ppermute | solution.py:131
  6.1 1.3 %collective-permute-start.3 = (bf16[3,160,256]{2,1,0:T(8,128)(2,1)}, bf16[3,160,256]{2,1,0:T(8,128)(2,1)S(1)}, u32[]{:S(2)}, u32[]{:S(2)}) collective-permute-start(bf16[3,160,256]{2,1,0:T(8,128)(2,1)} %get-tuple-element.61), channel_id=1, source_target_pairs={{16,2},{17,3},{18,0},{19,1},{20,6},{21,7},{22,4},{23,5},{24,10},{2... | collective-permute-start | bytes 737288 | tf_op jit(solution)/shard_map/ppermute | solution.py:131
  7.4 1.3 %collective-permute-start.4 = (bf16[3,160,256]{2,1,0:T(8,128)(2,1)}, bf16[3,160,256]{2,1,0:T(8,128)(2,1)S(1)}, u32[]{:S(2)}, u32[]{:S(2)}) collective-permute-start(bf16[3,160,256]{2,1,0:T(8,128)(2,1)} %get-tuple-element.62), channel_id=1, source_target_pairs={{16,3},{17,0},{18,1},{19,2},{20,7},{21,4},{22,5},{23,6},{24,11},{2... | collective-permute-start | bytes 737288 | tf_op jit(solution)/shard_map/ppermute | solution.py:131
  8.7 0.3 conditional.3
  9.0 1.3 %collective-permute-start.1 = (f32[3,1024]{1,0:T(4,128)S(1)}, f32[3,1024]{1,0:T(4,128)S(1)}, u32[]{:S(2)}, u32[]{:S(2)}) collective-permute-start(f32[3,1024]{1,0:T(4,128)S(1)} %pad_maximum_fusion), channel_id=1, source_target_pairs={{16,0},{17,1},{18,2},{19,3},{20,4},{21,5},{22,6},{23,7},{24,8},{25... | collective-permute-start | bytes 36872 | tf_op jit(solution)/shard_map/ppermute | solution.py:124
  10.3 22.3 %collective-permute-done.1 = f32[3,1024]{1,0:T(4,128)S(1)} collective-permute-done((f32[3,1024]{1,0:T(4,128)S(1)}, f32[3,1024]{1,0:T(4,128)S(1)}, u32[]{:S(2)}, u32[]{:S(2)}) %collective-permute-start.1) | collective-permute-done | bytes 12320 | tf_op jit(solution)/shard_map/ppermute | solution.py:124
  32.5 1.3 %collective-permute-start.5 = (bf16[3,160,768]{2,1,0:T(8,128)(2,1)S(1)}, bf16[3,160,768]{2,1,0:T(8,128)(2,1)}, u32[]{:S(2)}, u32[]{:S(2)}) collective-permute-start(bf16[3,160,768]{2,1,0:T(8,128)(2,1)S(1)} %get-tuple-element.63), channel_id=1, source_target_pairs={{16,0},{17,1},{18,2},{19,3},{20,4},{21,5},{22,6},{23,7},{24,8},{25... | collective-permute-start | bytes 2211848 | tf_op jit(solution)/shard_map/ppermute | solution.py:131
  33.9 1.3 %collective-permute-start.6 = (bf16[3,160,768]{2,1,0:T(8,128)(2,1)S(1)}, bf16[3,160,768]{2,1,0:T(8,128)(2,1)}, u32[]{:S(2)}, u32[]{:S(2)}) collective-permute-start(bf16[3,160,768]{2,1,0:T(8,128)(2,1)S(1)} %get-tuple-element.64), channel_id=1, source_target_pairs={{16,1},{17,2},{18,3},{19,0},{20,5},{21,6},{22,7},{23,4},{24,9},{25... | collective-permute-start | bytes 2211848 | tf_op jit(solution)/shard_map/ppermute | solution.py:131
  35.2 1.3 %collective-permute-start.7 = (bf16[3,160,768]{2,1,0:T(8,128)(2,1)S(1)}, bf16[3,160,768]{2,1,0:T(8,128)(2,1)S(1)}, u32[]{:S(2)}, u32[]{:S(2)}) collective-permute-start(bf16[3,160,768]{2,1,0:T(8,128)(2,1)S(1)} %get-tuple-element.65), channel_id=1, source_target_pairs={{16,2},{17,3},{18,0},{19,1},{20,6},{21,7},{22,4},{23,5},{24,10},{2... | collective-permute-start | bytes 2211848 | tf_op jit(solution)/shard_map/ppermute | solution.py:131
  36.5 1.3 %collective-permute-start.8 = (bf16[3,160,768]{2,1,0:T(8,128)(2,1)S(1)}, bf16[3,160,768]{2,1,0:T(8,128)(2,1)S(1)}, u32[]{:S(2)}, u32[]{:S(2)}) collective-permute-start(bf16[3,160,768]{2,1,0:T(8,128)(2,1)S(1)} %get-tuple-element.66), channel_id=1, source_target_pairs={{16,3},{17,0},{18,1},{19,2},{20,7},{21,4},{22,5},{23,6},{24,11},{2... | collective-permute-start | bytes 2211848 | tf_op jit(solution)/shard_map/ppermute | solution.py:131
  37.8 0.5 broadcast_in_dim.26
  38.3 1.0 bitcast_dynamic-update-slice_fusion.7
  39.3 14.5 %collective-permute-done.5 = bf16[3,160,768]{2,1,0:T(8,128)(2,1)} collective-permute-done((bf16[3,160,768]{2,1,0:T(8,128)(2,1)S(1)}, bf16[3,160,768]{2,1,0:T(8,128)(2,1)}, u32[]{:S(2)}, u32[]{:S(2)}) %collective-permute-start.5) | collective-permute-done | bytes 737312 | tf_op jit(solution)/shard_map/ppermute | solution.py:131
  53.8 3.5 %collective-permute-start.9 = (f32[3,1024]{1,0:T(4,128)S(1)}, f32[3,1024]{1,0:T(4,128)S(1)}, u32[]{:S(2)}, u32[]{:S(2)}) collective-permute-start(f32[3,1024]{1,0:T(4,128)S(1)} %collective-permute-done.1), channel_id=1, source_target_pairs={{0,4},{4,0},{8,12},{12,8},{1,5},{5,1},{9,13},{13,9},{2,6},{6,2},{1... | collective-permute-start | bytes 36872 | tf_op jit(solution)/shard_map/ppermute | solution.py:138
  57.3 1.2 %bitcast_dynamic-update-slice_fusion.3 = bf16[1,1,3,160,4096]{4,3,2,1,0:T(8,128)(2,1)S(1)} fusion(bf16[1,1,3,160,4096]{4,3,2,1,0:T(8,128)(2,1)S(1)} %bitcast_dynamic-update-slice_fusion.7, s32[]{:T(128)S(6)} %select_n.48, bf16[3,160,768]{2,1,0:T(8,128)(2,1)} %collective-permute-done.5), kind=kLoop, calls=%fused_computation.3 | loop fusion | bytes 1474564 | tf_op jit(solution)/shard_map/dynamic_update_slice | solution.py:155
  58.5 1.0 bitcast_dynamic-update-slice_fusion.6
  59.5 8.3 %collective-permute-done.6 = bf16[3,160,768]{2,1,0:T(8,128)(2,1)} collective-permute-done((bf16[3,160,768]{2,1,0:T(8,128)(2,1)S(1)}, bf16[3,160,768]{2,1,0:T(8,128)(2,1)}, u32[]{:S(2)}, u32[]{:S(2)}) %collective-permute-start.6) | collective-permute-done | bytes 737312 | tf_op jit(solution)/shard_map/ppermute | solution.py:131
  67.8 1.2 %bitcast_dynamic-update-slice_fusion.2 = bf16[1,1,3,160,4096]{4,3,2,1,0:T(8,128)(2,1)S(1)} fusion(bf16[1,1,3,160,4096]{4,3,2,1,0:T(8,128)(2,1)S(1)} %bitcast_dynamic-update-slice_fusion.6, s32[]{:T(128)S(6)} %select_n.51, bf16[3,160,768]{2,1,0:T(8,128)(2,1)} %collective-permute-done.6), kind=kLoop, calls=%fused_computation.2 | loop fusion | bytes 1474564 | tf_op jit(solution)/shard_map/dynamic_update_slice | solution.py:155
  69.0 4.5 %collective-permute-start.10 = (f32[3,1024]{1,0:T(4,128)S(1)}, f32[3,1024]{1,0:T(4,128)S(1)}, u32[]{:S(2)}, u32[]{:S(2)}) collective-permute-start(f32[3,1024]{1,0:T(4,128)S(1)} %add.92), channel_id=1, source_target_pairs={{0,8},{4,12},{8,0},{12,4},{1,9},{5,13},{9,1},{13,5},{2,10},{6,14},... | collective-permute-start | bytes 36872 | tf_op jit(solution)/shard_map/ppermute | solution.py:138
  73.5 12.9 %collective-permute-done.7 = bf16[3,160,768]{2,1,0:T(8,128)(2,1)S(1)} collective-permute-done((bf16[3,160,768]{2,1,0:T(8,128)(2,1)S(1)}, bf16[3,160,768]{2,1,0:T(8,128)(2,1)S(1)}, u32[]{:S(2)}, u32[]{:S(2)}) %collective-permute-start.7) | collective-permute-done | bytes 737312 | tf_op jit(solution)/shard_map/ppermute | solution.py:131
  86.6 1.9 %collective-permute-start.11 = (f32[3,4096]{1,0:T(4,128)S(1)}, f32[3,4096]{1,0:T(4,128)S(1)}, u32[]{:S(2)}, u32[]{:S(2)}) collective-permute-start(f32[3,4096]{1,0:T(4,128)S(1)} %get-tuple-element.68), channel_id=1, source_target_pairs={{0,1},{1,0},{2,3},{3,2},{4,5},{5,4},{6,7},{7,6},{8,9},{9,8},{10,11... | collective-permute-start | bytes 147464 | tf_op jit(solution)/shard_map/ppermute | solution.py:138
  88.5 1.2 %collective-permute-done.11 = f32[3,4096]{1,0:T(4,128)S(1)} collective-permute-done((f32[3,4096]{1,0:T(4,128)S(1)}, f32[3,4096]{1,0:T(4,128)S(1)}, u32[]{:S(2)}, u32[]{:S(2)}) %collective-permute-start.11) | collective-permute-done | bytes 49184 | tf_op jit(solution)/shard_map/ppermute | solution.py:138
  89.7 2.3 %collective-permute-start.12 = (f32[3,4096]{1,0:T(4,128)S(1)}, f32[3,4096]{1,0:T(4,128)S(1)}, u32[]{:S(2)}, u32[]{:S(2)}) collective-permute-start(f32[3,4096]{1,0:T(4,128)S(1)} %add_dynamic-update-slice_fusion), channel_id=1, source_target_pairs={{0,2},{1,3},{2,0},{3,1},{4,6},{5,7},{6,4},{7,5},{8,10},{9,11},{10,... | collective-permute-start | bytes 147464 | tf_op jit(solution)/shard_map/ppermute | solution.py:138
  92.0 8.5 %collective-permute-done.8 = bf16[3,160,768]{2,1,0:T(8,128)(2,1)S(1)} collective-permute-done((bf16[3,160,768]{2,1,0:T(8,128)(2,1)S(1)}, bf16[3,160,768]{2,1,0:T(8,128)(2,1)S(1)}, u32[]{:S(2)}, u32[]{:S(2)}) %collective-permute-start.8) | collective-permute-done | bytes 737312 | tf_op jit(solution)/shard_map/ppermute | solution.py:131
  100.6 0.8 broadcast_in_dim.36
  101.4 1.1 %copy-done = bf16[1,1,3,160,4096]{4,3,2,1,0:T(8,128)(2,1)} copy-done((bf16[1,1,3,160,4096]{4,3,2,1,0:T(8,128)(2,1)}, bf16[1,1,3,160,4096]{4,3,2,1,0:T(8,128)(2,1)S(1)}, u32[]{:S(2)}) %copy-start) | copy-done | bytes 3932184
  (24 shorter events, 0.5 us)
Async XLA Ops:
  3.5 29.0 %collective-permute-start = (bf16[3,160,256]{2,1,0:T(8,128)(2,1)}, bf16[3,160,256]{2,1,0:T(8,128)(2,1)}, u32[]{:S(2)}, u32[]{:S(2)}) collective-permute-start(bf16[3,160,256]{2,1,0:T(8,128)(2,1)} %get-tuple-element.53), channel_id=1, source_target_pairs={{16,0},{17,1},{18,2},{19,3},{20,4},{21,5},{22,6},{23,7},{24,8},{25... | collective-permute-start | bytes 737288 | tf_op jit(solution)/shard_map/ppermute | solution.py:131
  4.8 27.7 %collective-permute-start.2 = (bf16[3,160,256]{2,1,0:T(8,128)(2,1)}, bf16[3,160,256]{2,1,0:T(8,128)(2,1)}, u32[]{:S(2)}, u32[]{:S(2)}) collective-permute-start(bf16[3,160,256]{2,1,0:T(8,128)(2,1)} %get-tuple-element.60), channel_id=1, source_target_pairs={{16,1},{17,2},{18,3},{19,0},{20,5},{21,6},{22,7},{23,4},{24,9},{25... | collective-permute-start | bytes 737288 | tf_op jit(solution)/shard_map/ppermute | solution.py:131
  6.1 26.5 %collective-permute-start.3 = (bf16[3,160,256]{2,1,0:T(8,128)(2,1)}, bf16[3,160,256]{2,1,0:T(8,128)(2,1)S(1)}, u32[]{:S(2)}, u32[]{:S(2)}) collective-permute-start(bf16[3,160,256]{2,1,0:T(8,128)(2,1)} %get-tuple-element.61), channel_id=1, source_target_pairs={{16,2},{17,3},{18,0},{19,1},{20,6},{21,7},{22,4},{23,5},{24,10},{2... | collective-permute-start | bytes 737288 | tf_op jit(solution)/shard_map/ppermute | solution.py:131
  7.4 25.2 %collective-permute-start.4 = (bf16[3,160,256]{2,1,0:T(8,128)(2,1)}, bf16[3,160,256]{2,1,0:T(8,128)(2,1)S(1)}, u32[]{:S(2)}, u32[]{:S(2)}) collective-permute-start(bf16[3,160,256]{2,1,0:T(8,128)(2,1)} %get-tuple-element.62), channel_id=1, source_target_pairs={{16,3},{17,0},{18,1},{19,2},{20,7},{21,4},{22,5},{23,6},{24,11},{2... | collective-permute-start | bytes 737288 | tf_op jit(solution)/shard_map/ppermute | solution.py:131
  9.0 23.6 %collective-permute-start.1 = (f32[3,1024]{1,0:T(4,128)S(1)}, f32[3,1024]{1,0:T(4,128)S(1)}, u32[]{:S(2)}, u32[]{:S(2)}) collective-permute-start(f32[3,1024]{1,0:T(4,128)S(1)} %pad_maximum_fusion), channel_id=1, source_target_pairs={{16,0},{17,1},{18,2},{19,3},{20,4},{21,5},{22,6},{23,7},{24,8},{25... | collective-permute-start | bytes 36872 | tf_op jit(solution)/shard_map/ppermute | solution.py:124
  32.5 21.3 %collective-permute-start.5 = (bf16[3,160,768]{2,1,0:T(8,128)(2,1)S(1)}, bf16[3,160,768]{2,1,0:T(8,128)(2,1)}, u32[]{:S(2)}, u32[]{:S(2)}) collective-permute-start(bf16[3,160,768]{2,1,0:T(8,128)(2,1)S(1)} %get-tuple-element.63), channel_id=1, source_target_pairs={{16,0},{17,1},{18,2},{19,3},{20,4},{21,5},{22,6},{23,7},{24,8},{25... | collective-permute-start | bytes 2211848 | tf_op jit(solution)/shard_map/ppermute | solution.py:131
  33.9 33.9 %collective-permute-start.6 = (bf16[3,160,768]{2,1,0:T(8,128)(2,1)S(1)}, bf16[3,160,768]{2,1,0:T(8,128)(2,1)}, u32[]{:S(2)}, u32[]{:S(2)}) collective-permute-start(bf16[3,160,768]{2,1,0:T(8,128)(2,1)S(1)} %get-tuple-element.64), channel_id=1, source_target_pairs={{16,1},{17,2},{18,3},{19,0},{20,5},{21,6},{22,7},{23,4},{24,9},{25... | collective-permute-start | bytes 2211848 | tf_op jit(solution)/shard_map/ppermute | solution.py:131
  35.2 51.2 %collective-permute-start.7 = (bf16[3,160,768]{2,1,0:T(8,128)(2,1)S(1)}, bf16[3,160,768]{2,1,0:T(8,128)(2,1)S(1)}, u32[]{:S(2)}, u32[]{:S(2)}) collective-permute-start(bf16[3,160,768]{2,1,0:T(8,128)(2,1)S(1)} %get-tuple-element.65), channel_id=1, source_target_pairs={{16,2},{17,3},{18,0},{19,1},{20,6},{21,7},{22,4},{23,5},{24,10},{2... | collective-permute-start | bytes 2211848 | tf_op jit(solution)/shard_map/ppermute | solution.py:131
  36.5 63.9 %collective-permute-start.8 = (bf16[3,160,768]{2,1,0:T(8,128)(2,1)S(1)}, bf16[3,160,768]{2,1,0:T(8,128)(2,1)S(1)}, u32[]{:S(2)}, u32[]{:S(2)}) collective-permute-start(bf16[3,160,768]{2,1,0:T(8,128)(2,1)S(1)} %get-tuple-element.66), channel_id=1, source_target_pairs={{16,3},{17,0},{18,1},{19,2},{20,7},{21,4},{22,5},{23,6},{24,11},{2... | collective-permute-start | bytes 2211848 | tf_op jit(solution)/shard_map/ppermute | solution.py:131
  53.8 15.2 %collective-permute-start.9 = (f32[3,1024]{1,0:T(4,128)S(1)}, f32[3,1024]{1,0:T(4,128)S(1)}, u32[]{:S(2)}, u32[]{:S(2)}) collective-permute-start(f32[3,1024]{1,0:T(4,128)S(1)} %collective-permute-done.1), channel_id=1, source_target_pairs={{0,4},{4,0},{8,12},{12,8},{1,5},{5,1},{9,13},{13,9},{2,6},{6,2},{1... | collective-permute-start | bytes 36872 | tf_op jit(solution)/shard_map/ppermute | solution.py:138
  69.0 17.5 %collective-permute-start.10 = (f32[3,1024]{1,0:T(4,128)S(1)}, f32[3,1024]{1,0:T(4,128)S(1)}, u32[]{:S(2)}, u32[]{:S(2)}) collective-permute-start(f32[3,1024]{1,0:T(4,128)S(1)} %add.92), channel_id=1, source_target_pairs={{0,8},{4,12},{8,0},{12,4},{1,9},{5,13},{9,1},{13,5},{2,10},{6,14},... | collective-permute-start | bytes 36872 | tf_op jit(solution)/shard_map/ppermute | solution.py:138
  86.6 3.1 %collective-permute-start.11 = (f32[3,4096]{1,0:T(4,128)S(1)}, f32[3,4096]{1,0:T(4,128)S(1)}, u32[]{:S(2)}, u32[]{:S(2)}) collective-permute-start(f32[3,4096]{1,0:T(4,128)S(1)} %get-tuple-element.68), channel_id=1, source_target_pairs={{0,1},{1,0},{2,3},{3,2},{4,5},{5,4},{6,7},{7,6},{8,9},{9,8},{10,11... | collective-permute-start | bytes 147464 | tf_op jit(solution)/shard_map/ppermute | solution.py:138
  89.7 10.9 %collective-permute-start.12 = (f32[3,4096]{1,0:T(4,128)S(1)}, f32[3,4096]{1,0:T(4,128)S(1)}, u32[]{:S(2)}, u32[]{:S(2)}) collective-permute-start(f32[3,4096]{1,0:T(4,128)S(1)} %add_dynamic-update-slice_fusion), channel_id=1, source_target_pairs={{0,2},{1,3},{2,0},{3,1},{4,6},{5,7},{6,4},{7,5},{8,10},{9,11},{10,... | collective-permute-start | bytes 147464 | tf_op jit(solution)/shard_map/ppermute | solution.py:138
  100.6 1.9 %copy-start = (bf16[1,1,3,160,4096]{4,3,2,1,0:T(8,128)(2,1)}, bf16[1,1,3,160,4096]{4,3,2,1,0:T(8,128)(2,1)S(1)}, u32[]{:S(2)}) copy-start(bf16[1,1,3,160,4096]{4,3,2,1,0:T(8,128)(2,1)S(1)} %bitcast_dynamic-update-slice_fusion) | copy-start | bytes 11796484
